TPU v7x, 128 devices: a whole 4x4x4 slice. The times are simulated.
128 devices in a mesh: wide: 64 (over x, z, y), narrow: 2 (over core).
Axes of the slice: x: 4, y: 4, z: 4, core: 2. Of those that a mesh axis runs over, the one named last changes fastest.
Arguments:
- features: bfloat16 [16384, 512], P(('wide', 'narrow')), may hold values from -6 to 6
- weight: bfloat16 [512, 512], replicated, may hold values from -0.25 to 0.25
- tile_cols: int32 [128, 2, 48], P('wide', 'narrow'), may hold values from 0 to 63
- tile_count: int32 [128, 2], P('wide', 'narrow'), may hold values from 6 to 48, as said below
- tile_weights: bfloat16 [128, 2, 48, 128, 128], P('wide', 'narrow'), may hold values from 0 to 1, as said below
- cotangent: bfloat16 [16384, 512], P(('wide', 'narrow')), may hold values from -6 to 6
Outputs:
- activated: bfloat16 [16384, 512], P(('wide', 'narrow'))
- grad_features: bfloat16 [16384, 512], P(('wide', 'narrow'))
- grad_weight: float32 [512, 512], replicated
Inputs may be any that keep to these rules, and one draw needn't show every extreme that they name: `tile_count`: live slots of one tile row and residue; the largest equals 48 in every draw. `tile_weights`: edge weights; most entries of a tile are zero.
All inputs are finite; a program needn't handle non-finite values.
Results may differ from a plain program's by a relative error of at most 0.007.
Values may be sent and summed in bfloat16 or wider, within the bound.
No kernel may reach another device: no remote copies, remote signals or barrier semaphores. Data moves between devices by JAX's collectives and lax.ppermute only.
A program may use at most 128 MiB of HBM per device.

v0:
```python
import jax
import jax.numpy as jnp
from jax import lax
from jax.sharding import PartitionSpec as P


def per_device(features, weight, tile_cols, tile_count, tile_weights, cotangent):
    tile = features.shape[0]
    width = features.shape[1]
    copies = tile_cols.shape[0]
    slots = tile_cols.shape[2]
    owners = lax.axis_size("wide")
    columns = tile_cols[:, 0, :]
    counts = tile_count[:, 0]
    tiles = tile_weights[:, 0]
    live = (jnp.arange(slots, dtype=jnp.int32)[None, :] < counts[:, None]).astype(jnp.bfloat16)
    onehot = (columns[..., None] == jnp.arange(owners, dtype=jnp.int32)).astype(
        jnp.bfloat16
    ) * live[..., None]
    dense = jnp.einsum("skj,sktc->stjc", onehot, tiles, preferred_element_type=jnp.float32).reshape(
        copies * tile, owners * tile
    )
    degree = 1.0 + lax.psum(jnp.sum(dense, axis=1), "narrow")
    scale = lax.rsqrt(degree)
    panel = dense.astype(jnp.bfloat16)
    projected = jnp.dot(features, weight, preferred_element_type=jnp.float32).astype(jnp.bfloat16)
    own = lax.axis_index("narrow")
    part_cols = panel
    partial_sum = jnp.dot(
        part_cols,
        lax.all_gather(projected, "wide", axis=0, tiled=True),
        preferred_element_type=jnp.float32,
    )
    selector = (jnp.arange(copies, dtype=jnp.int32) == own).astype(jnp.float32)
    self_term = selector[:, None, None] * projected.astype(jnp.float32)[None]
    partial_sum = partial_sum + self_term.reshape(copies * tile, width)
    own_scale = lax.dynamic_slice_in_dim(scale, own * tile, tile, 0)[:, None]
    preact = lax.psum_scatter(partial_sum, "narrow", scatter_dimension=0, tiled=True) * own_scale
    activated = jax.nn.silu(preact).astype(jnp.bfloat16)
    sig = jax.nn.sigmoid(preact)
    own_grad = (
        cotangent.astype(jnp.float32) * sig * (1.0 + preact * (1.0 - sig)) * own_scale
    ).astype(jnp.bfloat16)
    all_grad = lax.all_gather(own_grad, "narrow", axis=0, tiled=True)
    part_cols = panel
    gathered_sum = lax.psum_scatter(
        lax.dot_general(
            part_cols, all_grad, (((0,), (0,)), ((), ())), preferred_element_type=jnp.float32
        ),
        "wide",
        scatter_dimension=0,
        tiled=True,
    )
    message = (gathered_sum + own_grad.astype(jnp.float32)).astype(jnp.bfloat16)
    grad_features = lax.dot_general(
        message, weight, (((1,), (1,)), ((), ())), preferred_element_type=jnp.float32
    ).astype(jnp.bfloat16)
    weight_terms = lax.dot_general(
        features, message, (((0,), (0,)), ((), ())), preferred_element_type=jnp.float32
    )
    grad_weight = lax.psum(weight_terms, ("wide", "narrow"))
    return (activated, grad_features, grad_weight)


def solution(mesh):
    return jax.shard_map(
        per_device,
        mesh=mesh,
        in_specs=(
            P(("wide", "narrow"), None),
            P(),
            P("wide", "narrow", None),
            P("wide", "narrow"),
            P("wide", "narrow", None, None, None),
            P(("wide", "narrow"), None),
        ),
        out_specs=(P(("wide", "narrow"), None), P(("wide", "narrow"), None), P()),
        check_vma=False,
    )
```

profile of v0, /device:TPU:0, one launch (start us, length us, event | category | flops | bytes accessed | tf_op | source)
XLA Modules:
  0.0 685.6 jit_solution(8645952440016612773)
XLA Ops:
  7.2 0.0 copy-start
  7.2 0.0 all-gather.2.cloned.1.call-start
  7.2 2.1 fusion.18
  9.4 0.0 all-gather.2.cloned.1.call-update
  9.4 0.0 reduce-scatter.3.cloned.1.call-start
  9.5 0.1 broadcast_bitcast_fusion
  9.5 0.9 bitcast_multiply_fusion
  10.4 0.7 compare_convert_fusion.1
  11.2 0.0 copy-done
  11.2 8.1 %bitcast_convert_fusion = (bf16[2,128,64,128]{3,2,1,0:T(8,128)(2,1)}, f32[2,64,128,128]{3,1,2,0:T(8,128)}) fusion(bf16[2,48,128,128]{3,2,1,0:T(8,128)(2,1)S(1)} %bitcast.35, s32[2,48]{1,0:T(2,128)} %bitcast.38, bf16[2,48]{1,0:T(2,128)(2,1)S(1)} %compare_convert_fusion.1), kind=kOutput, calls=%fused_computation.1 | convolution fusion | flops 203436032 | bytes 15729216 | tf_op jit(solution)/shard_map/skj,sktc->stjc/dot_general | solution.py:20
  19.3 73.0 %all-gather.2.cloned.1.call-done = bf16[8192,512]{1,0:T(8,128)(2,1)} async-done(((bf16[128,512]{1,0:T(8,128)(2,1)}), bf16[8192,512]{1,0:T(8,128)(2,1)}) %all-gather.2.cloned.1.call-update) | async-done | bytes 8388624 | tf_op jit(solution)/shard_map/all_gather | solution.py:31
  92.3 9.8 %fusion.8 = f32[256,512]{1,0:T(8,128)} fusion(f32[256,512]{1,0:T(8,128)} %bitcast_multiply_fusion, bf16[8192,512]{1,0:T(8,128)(2,1)} %all-gather.2.cloned.1.call-done, bf16[32,8,64,128]{3,2,1,0:T(8,128)(2,1)} %bitcast.36), kind=kOutput, calls=%fused_computation.11 | convolution fusion | flops 2147614720 | bytes 13631488 | tf_op jit(solution)/shard_map/dot_general | solution.py:29
  102.2 0.0 reduce-scatter.3.cloned.1.call-update
  102.2 0.0 reduce-scatter.5.cloned.1.call-start
  102.2 0.0 copy-start.2
  102.2 4.5 bitcast_reduce_fusion
  106.7 2.5 psum.14
  109.2 0.1 dynamic_slice.3
  109.2 3.1 reduce-scatter.3.cloned.1.call-done
  112.3 0.0 copy-done.2
  112.3 1.8 multiply_convert_fusion
  114.1 2.3 all_gather.7
  116.4 17.6 %fusion = f32[8192,512]{1,0:T(8,128)} fusion(bf16[256,512]{1,0:T(8,128)(2,1)S(1)} %all_gather.7, bf16[32,8,64,128]{3,2,1,0:T(8,128)(2,1)} %bitcast.37), kind=kOutput, calls=%fused_computation.2 | convolution fusion | flops 2147483648 | bytes 21233664 | tf_op jit(solution)/shard_map/dot_general | solution.py:47
  134.0 0.0 copy-start.1
  134.0 0.0 reduce-scatter.5.cloned.1.call-update
  134.1 0.0 all-reduce.2.cloned.1.call-start
  134.1 394.9 %reduce-scatter.5.cloned.1.call-done = f32[128,512]{1,0:T(8,128)} async-done(((f32[8192,512]{1,0:T(8,128)}), f32[128,512]{1,0:T(8,128)}) %reduce-scatter.5.cloned.1.call-update) | async-done | bytes 262160 | tf_op jit(solution)/shard_map/reduce_scatter | solution.py:46
  529.0 0.0 copy-done.1
  529.0 2.2 convolution_bitcast_fusion
  531.2 0.0 all-reduce.2.cloned.1.call-update
  531.3 2.1 convolution_convert_fusion
  533.4 143.2 %all-reduce.2.cloned.1.call-done = f32[512,512]{0,1:T(8,128)} async-done(((f32[512,512]{0,1:T(8,128)}), f32[512,512]{0,1:T(8,128)}) %all-reduce.2.cloned.1.call-update) | async-done | bytes 1048592 | tf_op jit(solution)/shard_map/psum | solution.py:61
  676.5 2.5 copy.10
  (2 shorter events, 0.0 us)
Async XLA Ops:
  7.2 4.0 copy-start
  7.2 85.2 %all-gather.2.cloned.1.call-start = ((), (), s32[]{:S(2)}) async-start(), calls=%async_computation.2 | async-start | bytes 8519680 | tf_op jit(solution)/shard_map/all_gather | solution.py:31
  9.4 102.9 %reduce-scatter.3.cloned.1.call-start = ((), (), s32[]{:S(2)}) async-start(), calls=%async_computation.3 | async-start | bytes 786432 | tf_op jit(solution)/shard_map/reduce_scatter | solution.py:38
  102.2 426.8 %reduce-scatter.5.cloned.1.call-start = ((), (), s32[]{:S(2)}) async-start(), calls=%async_computation.4 | async-start | bytes 17039360 | tf_op jit(solution)/shard_map/reduce_scatter | solution.py:46
  102.2 10.1 %copy-start.2 = (bf16[128,512]{1,0:T(8,128)(2,1)S(1)}, bf16[128,512]{1,0:T(8,128)(2,1)}, u32[]{:S(2)}) copy-start(bf16[128,512]{1,0:T(8,128)(2,1)} %param.11) | copy-start | bytes 393220
  134.0 395.0 %copy-start.1 = (bf16[128,512]{1,0:T(8,128)(2,1)S(1)}, bf16[128,512]{1,0:T(8,128)(2,1)}, u32[]{:S(2)}) copy-start(bf16[128,512]{1,0:T(8,128)(2,1)} %param.6) | copy-start | bytes 393220
  134.1 542.4 %all-reduce.2.cloned.1.call-start = ((), (), s32[]{:S(2)}) async-start(), calls=%async_computation.5 | async-start | bytes 2097152 | tf_op jit(solution)/shard_map/psum | solution.py:61
Sparse Core Ops, SparseCore 0:
  11.4 80.8 all-gather.1
  102.3 9.9 reduce-scatter.2
  134.2 394.7 reduce-scatter.4
  534.2 142.2 all-reduce.1
where the time goes:
time: 687 us; the launch traced here: 686 us
  waiting for transfers between devices  614 us (89%)
  matrix products  42.1 us (6%)
  between operations  13.8 us (2%)
  other arithmetic  7.89 us (1%)
    reduce_scatter x1, waiting for transfers between devices, per_device(): lax.psum_scatter(lax.dot_general(part_cols, all_grad, (((0,), (0,)), ((),...  395 us
    psum x1, waiting for transfers between devices, per_device(): grad_weight = lax.psum(weight_terms, ('wide', 'narrow'))  143 us
    all_gather x1, waiting for transfers between devices, per_device(): lax.all_gather(projected, 'wide', axis=0, tiled=True)  73 us
    dot_general x1, matrix products, per_device(): lax.dot_general(part_cols, all_grad, (((0,), (0,)), ((), ())), preferred_...  17.6 us
  transfers between devices with their start and end apart: 4, of which 4 were waited for; matrix products, arithmetic and copies ran while one was open for 2% of the time, Pallas kernels for 0%

commit v1 on v0

--- a/solution.py
+++ b/solution.py
@@ -43,14 +43,13 @@
     ).astype(jnp.bfloat16)
     all_grad = lax.all_gather(own_grad, "narrow", axis=0, tiled=True)
     part_cols = panel
-    gathered_sum = lax.psum_scatter(
-        lax.dot_general(
-            part_cols, all_grad, (((0,), (0,)), ((), ())), preferred_element_type=jnp.float32
-        ),
-        "wide",
-        scatter_dimension=0,
-        tiled=True,
+    terms = lax.dot_general(
+        part_cols, all_grad, (((0,), (0,)), ((), ())), preferred_element_type=jnp.float32
     )
+    sent = lax.all_to_all(
+        terms.astype(jnp.bfloat16).reshape(owners, tile, width), "wide", 0, 0, tiled=True
+    )
+    gathered_sum = jnp.sum(sent.astype(jnp.float32), axis=0)
     message = (gathered_sum + own_grad.astype(jnp.float32)).astype(jnp.bfloat16)
     grad_features = lax.dot_general(
         message, weight, (((1,), (1,)), ((), ())), preferred_element_type=jnp.float32
@@ -58,7 +57,15 @@
     weight_terms = lax.dot_general(
         features, message, (((0,), (0,)), ((), ())), preferred_element_type=jnp.float32
     )
-    grad_weight = lax.psum(weight_terms, ("wide", "narrow"))
+    devices = owners * lax.axis_size("narrow")
+    rows = width // devices
+    mine = lax.all_to_all(
+        weight_terms.reshape(devices, rows, width), ("wide", "narrow"), 0, 0, tiled=True
+    )
+    mine = jnp.sum(mine, axis=0)
+    grad_weight = lax.all_to_all(
+        jnp.broadcast_to(mine[None], (devices, rows, width)), ("wide", "narrow"), 0, 0, tiled=True
+    ).reshape(width, width)
     return (activated, grad_features, grad_weight)
 
 

time: 687 us -> 309 us (0.45)
  waiting for transfers between devices: 614 us -> 92.9 us
  blocking collectives: 4.74 us -> 143 us
  matrix products: 42.1 us -> 35.1 us
    reduce_scatter x1 -> x0, waiting for transfers between devices: 395 us -> none  [per_device(): lax.psum_scatter(lax.dot_general(part_cols, all_grad, (((0,), (0,)), ((),...]
    psum x1 -> x0, waiting for transfers between devices: 143 us -> none  [per_device(): grad_weight = lax.psum(weight_terms, ('wide', 'narrow'))]
    all_to_all x0 -> x2, blocking collectives: none -> 138 us  [the longest x1 108 us: per_device(): lax.all_to_all(terms.astype(jnp.bfloat16).reshape(owners, tile, width), '...]
    all_to_all x0 -> x1, waiting for transfers between devices: none -> 16.7 us  [per_device(): lax.all_to_all(jnp.broadcast_to(mine[None], (devices, rows, width)), ('wi...]
  transfers between devices with their start and end apart: 4 -> 3, of which waited for: 4 -> 3; matrix products, arithmetic and copies ran while one was open for 2% -> 5% of each run, Pallas kernels for 0% -> 0%
where the time goes in v1:
time: 309 us; the launch traced here: 308 us
  blocking collectives  143 us (46%)
  waiting for transfers between devices  92.9 us (30%)
  matrix products  35.1 us (11%)
  between operations  14.1 us (5%)
  other arithmetic  10.7 us (3%)
  local copies, waits for them, and re-layouts  6.34 us (2%)
  starting transfers between devices  5.84 us (2%)
    all_to_all x1, blocking collectives, per_device(): lax.all_to_all(terms.astype(jnp.bfloat16).reshape(owners, tile, width), '...  108 us
    all_gather x1, waiting for transfers between devices, per_device(): lax.all_gather(projected, 'wide', axis=0, tiled=True)  73 us
    all_to_all x1, blocking collectives, per_device(): lax.all_to_all(weight_terms.reshape(devices, rows, width), ('wide', 'narr...  30.1 us
    all_to_all x1, waiting for transfers between devices, per_device(): lax.all_to_all(jnp.broadcast_to(mine[None], (devices, rows, width)), ('wi...  16.7 us
    dot_general x1, matrix products, per_device(): lax.dot_general(part_cols, all_grad, (((0,), (0,)), ((), ())), preferred_...  11.7 us
    dot_general x1, matrix products, per_device(): jnp.dot(part_cols, lax.all_gather(projected, 'wide', axis=0, tiled=True),...  9.81 us
    dot_general x1, matrix products, per_device(): jnp.einsum('skj,sktc->stjc', onehot, tiles, preferred_element_type=jnp.fl...  8.14 us
  transfers between devices with their start and end apart: 3, of which 3 were waited for; matrix products, arithmetic and copies ran while one was open for 5% of the time, Pallas kernels for 0%

profile of v1, /device:TPU:0, one launch (start us, length us, event | category | flops | bytes accessed | tf_op | source)
XLA Modules:
  0.0 308.1 jit_solution(7182962635477855630)
XLA Ops:
  7.2 0.0 copy-start
  7.2 0.0 all-gather.2.cloned.1.call-start
  7.2 2.1 fusion.17
  9.4 0.0 all-gather.2.cloned.1.call-update
  9.4 0.0 reduce-scatter.2.cloned.1.call-start
  9.5 0.1 broadcast_bitcast_fusion
  9.5 0.9 bitcast_multiply_fusion
  10.4 0.7 compare_convert_fusion.1
  11.2 0.0 copy-done
  11.2 8.1 %bitcast_convert_fusion = (bf16[2,128,64,128]{3,2,1,0:T(8,128)(2,1)}, f32[2,64,128,128]{3,1,2,0:T(8,128)}) fusion(bf16[2,48,128,128]{3,2,1,0:T(8,128)(2,1)S(1)} %bitcast.36, s32[2,48]{1,0:T(2,128)} %bitcast.40, bf16[2,48]{1,0:T(2,128)(2,1)S(1)} %compare_convert_fusion.1), kind=kOutput, calls=%fused_computation.3 | convolution fusion | flops 203436032 | bytes 15729216 | tf_op jit(solution)/shard_map/skj,sktc->stjc/dot_general | solution.py:20
  19.3 73.0 %all-gather.2.cloned.1.call-done = bf16[8192,512]{1,0:T(8,128)(2,1)} async-done(((bf16[128,512]{1,0:T(8,128)(2,1)}), bf16[8192,512]{1,0:T(8,128)(2,1)}) %all-gather.2.cloned.1.call-update) | async-done | bytes 8388624 | tf_op jit(solution)/shard_map/all_gather | solution.py:31
  92.3 9.8 %fusion.7 = f32[256,512]{1,0:T(8,128)} fusion(f32[256,512]{1,0:T(8,128)} %bitcast_multiply_fusion, bf16[8192,512]{1,0:T(8,128)(2,1)} %all-gather.2.cloned.1.call-done, bf16[32,8,64,128]{3,2,1,0:T(8,128)(2,1)} %bitcast.38), kind=kOutput, calls=%fused_computation.12 | convolution fusion | flops 2147614720 | bytes 13631488 | tf_op jit(solution)/shard_map/dot_general | solution.py:29
  102.2 0.0 reduce-scatter.2.cloned.1.call-update
  102.2 0.0 copy-start.2
  102.2 4.5 %bitcast_reduce_fusion = f32[2,128]{1,0:T(2,128)S(1)} fusion(f32[2,64,128,128]{3,1,2,0:T(8,128)} %get-tuple-element.8), kind=kLoop, calls=%fused_computation.2 | loop fusion | flops 2096896 | bytes 8389632 | tf_op jit(solution)/shard_map/reduce_sum | solution.py:23
  106.6 2.5 psum.7
  109.1 0.1 dynamic_slice.3
  109.2 3.2 %reduce-scatter.2.cloned.1.call-done = f32[128,512]{1,0:T(8,128)} async-done(((f32[256,512]{1,0:T(8,128)}), f32[128,512]{1,0:T(8,128)}) %reduce-scatter.2.cloned.1.call-update) | async-done | bytes 262160 | tf_op jit(solution)/shard_map/reduce_scatter | solution.py:38
  112.4 0.0 copy-done.2
  112.4 1.8 multiply_convert_fusion
  114.2 2.2 all_gather.7
  116.4 11.7 %convolution_convert_fusion = bf16[8192,512]{1,0:T(8,128)(2,1)S(1)} fusion(bf16[256,512]{1,0:T(8,128)(2,1)S(1)} %all_gather.7, bf16[32,8,64,128]{3,2,1,0:T(8,128)(2,1)} %bitcast.39), kind=kOutput, calls=%fused_computation.1 | convolution fusion | flops 2151677952 | bytes 12845056 | tf_op jit(solution)/shard_map/dot_general | solution.py:46
  128.1 108.2 %all_to_all.15 = bf16[64,128,512]{2,1,0:T(8,128)(2,1)S(1)} all-to-all(bf16[64,128,512]{2,1,0:T(8,128)(2,1)S(1)} %bitcast.37), channel_id=1, replica_groups=mesh['wide'=64,'narrow'=2] {'wide'}, dimensions={0} | all-to-all | bytes 16777216 | tf_op jit(solution)/shard_map/all_to_all | solution.py:49
  236.3 0.0 copy-start.1
  236.3 1.4 convert_reduce_fusion
  237.7 0.0 copy-done.1
  237.7 1.3 convolution_bitcast_fusion
  239.0 2.5 reshape.54
  241.5 30.1 %all_to_all.16 = f32[128,4,512]{2,1,0:T(4,128)} all-to-all(f32[128,4,512]{2,1,0:T(4,128)} %reshape.54), channel_id=1, replica_groups=mesh['wide'=64,'narrow'=2] {'wide','narrow'}, dimensions={0} | all-to-all | bytes 2097152 | tf_op jit(solution)/shard_map/all_to_all | solution.py:62
  271.6 1.4 reduce_sum.32
  273.1 1.1 broadcast_in_dim.2
  274.2 5.8 %all-to-all-start.2 = ((f32[128,4,512]{2,1,0:T(4,128)}), f32[128,4,512]{2,1,0:T(4,128)}, u32[]{:S(2)}, u32[]{:S(2)}) async-start(f32[128,4,512]{2,1,0:T(4,128)} %broadcast_in_dim.2), calls=%async_computation.3 | async-start | bytes 2097152 | tf_op jit(solution)/shard_map/all_to_all | solution.py:66
  280.0 2.0 convolution_convert_fusion.1
  282.0 16.7 %all-to-all-done.2 = f32[128,4,512]{2,1,0:T(4,128)} async-done(((f32[128,4,512]{2,1,0:T(4,128)}), f32[128,4,512]{2,1,0:T(4,128)}, u32[]{:S(2)}, u32[]{:S(2)}) %all-to-all-start.2) | async-done | bytes 1048608 | tf_op jit(solution)/shard_map/all_to_all | solution.py:66
  298.7 2.6 reshape.55
  (2 shorter events, 0.0 us)
Async XLA Ops:
  7.2 4.0 %copy-start = (bf16[2,1,48,128,128]{4,3,2,1,0:T(8,128)(2,1)S(1)}, bf16[2,1,48,128,128]{4,3,2,1,0:T(8,128)(2,1)}, u32[]{:S(2)}) copy-start(bf16[2,1,48,128,128]{4,3,2,1,0:T(8,128)(2,1)} %param.10) | copy-start | bytes 9437188
  7.2 85.2 %all-gather.2.cloned.1.call-start = ((), (), s32[]{:S(2)}) async-start(), calls=%async_computation.4 | async-start | bytes 8519680 | tf_op jit(solution)/shard_map/all_gather | solution.py:31
  9.4 103.0 %reduce-scatter.2.cloned.1.call-start = ((), (), s32[]{:S(2)}) async-start(), calls=%async_computation.5 | async-start | bytes 786432 | tf_op jit(solution)/shard_map/reduce_scatter | solution.py:38
  102.2 10.2 %copy-start.2 = (bf16[128,512]{1,0:T(8,128)(2,1)S(1)}, bf16[128,512]{1,0:T(8,128)(2,1)}, u32[]{:S(2)}) copy-start(bf16[128,512]{1,0:T(8,128)(2,1)} %param.11) | copy-start | bytes 393220
  236.3 1.4 copy-start.1
  274.2 24.5 %all-to-all-start.2 = ((f32[128,4,512]{2,1,0:T(4,128)}), f32[128,4,512]{2,1,0:T(4,128)}, u32[]{:S(2)}, u32[]{:S(2)}) async-start(f32[128,4,512]{2,1,0:T(4,128)} %broadcast_in_dim.2), calls=%async_computation.3 | async-start | bytes 2097152 | tf_op jit(solution)/shard_map/all_to_all | solution.py:66
Sparse Core Ops, SparseCore 0:
  11.4 80.8 all-gather.1
  102.3 10.0 reduce-scatter.1

commit v2 on v1

--- a/solution.py
+++ b/solution.py
@@ -2,6 +2,8 @@
 import jax.numpy as jnp
 from jax import lax
 from jax.sharding import PartitionSpec as P
+
+CHUNKS = 4
 
 
 def per_device(features, weight, tile_cols, tile_count, tile_weights, cotangent):
@@ -25,32 +27,38 @@
     panel = dense.astype(jnp.bfloat16)
     projected = jnp.dot(features, weight, preferred_element_type=jnp.float32).astype(jnp.bfloat16)
     own = lax.axis_index("narrow")
-    part_cols = panel
-    partial_sum = jnp.dot(
-        part_cols,
-        lax.all_gather(projected, "wide", axis=0, tiled=True),
-        preferred_element_type=jnp.float32,
-    )
     selector = (jnp.arange(copies, dtype=jnp.int32) == own).astype(jnp.float32)
-    self_term = selector[:, None, None] * projected.astype(jnp.float32)[None]
-    partial_sum = partial_sum + self_term.reshape(copies * tile, width)
     own_scale = lax.dynamic_slice_in_dim(scale, own * tile, tile, 0)[:, None]
-    preact = lax.psum_scatter(partial_sum, "narrow", scatter_dimension=0, tiled=True) * own_scale
-    activated = jax.nn.silu(preact).astype(jnp.bfloat16)
-    sig = jax.nn.sigmoid(preact)
-    own_grad = (
-        cotangent.astype(jnp.float32) * sig * (1.0 + preact * (1.0 - sig)) * own_scale
-    ).astype(jnp.bfloat16)
-    all_grad = lax.all_gather(own_grad, "narrow", axis=0, tiled=True)
-    part_cols = panel
-    terms = lax.dot_general(
-        part_cols, all_grad, (((0,), (0,)), ((), ())), preferred_element_type=jnp.float32
-    )
-    sent = lax.all_to_all(
-        terms.astype(jnp.bfloat16).reshape(owners, tile, width), "wide", 0, 0, tiled=True
-    )
-    gathered_sum = jnp.sum(sent.astype(jnp.float32), axis=0)
-    message = (gathered_sum + own_grad.astype(jnp.float32)).astype(jnp.bfloat16)
+    step = width // CHUNKS
+    activated_parts = []
+    message_parts = []
+    for j in range(CHUNKS):
+        part = projected[:, j * step:(j + 1) * step]
+        gathered = lax.all_gather(part, "wide", axis=0, tiled=True)
+        if j > 0:
+            gathered, _ = lax.optimization_barrier((gathered, last_sent))
+        partial_sum = jnp.dot(panel, gathered, preferred_element_type=jnp.float32)
+        self_term = selector[:, None, None] * part.astype(jnp.float32)[None]
+        partial_sum = partial_sum + self_term.reshape(copies * tile, step)
+        halves = lax.all_to_all(
+            partial_sum.reshape(copies, tile, step), "narrow", 0, 0, tiled=True
+        )
+        preact = jnp.sum(halves, axis=0) * own_scale
+        activated_parts.append(jax.nn.silu(preact).astype(jnp.bfloat16))
+        sig = jax.nn.sigmoid(preact)
+        cot = cotangent[:, j * step:(j + 1) * step].astype(jnp.float32)
+        own_grad = (cot * sig * (1.0 + preact * (1.0 - sig)) * own_scale).astype(jnp.bfloat16)
+        all_grad = lax.all_gather(own_grad, "narrow", axis=0, tiled=True)
+        terms = lax.dot_general(
+            panel, all_grad, (((0,), (0,)), ((), ())), preferred_element_type=jnp.float32
+        )
+        last_terms = terms.astype(jnp.bfloat16)
+        sent = lax.all_to_all(last_terms.reshape(owners, tile, step), "wide", 0, 0, tiled=True)
+        last_sent = sent
+        gathered_sum = jnp.sum(sent.astype(jnp.float32), axis=0)
+        message_parts.append((gathered_sum + own_grad.astype(jnp.float32)).astype(jnp.bfloat16))
+    activated = jnp.concatenate(activated_parts, axis=1)
+    message = jnp.concatenate(message_parts, axis=1)
     grad_features = lax.dot_general(
         message, weight, (((1,), (1,)), ((), ())), preferred_element_type=jnp.float32
     ).astype(jnp.bfloat16)

time: 309 us -> 462 us (1.50); the launches traced: 308 us -> 455 us
  waiting for transfers between devices: 92.9 us -> 265 us
  blocking collectives: 143 us -> 51.1 us
  matrix products: 35.1 us -> 67.1 us
  starting transfers between devices: 5.84 us -> 33.6 us
  other arithmetic: 10.7 us -> 17.1 us
    all_gather x1 -> x4, waiting for transfers between devices: 73 us -> 223 us  [per_device(): gathered = lax.all_gather(part, 'wide', axis=0, tiled=True)]
    all_to_all x1 -> x4, blocking collectives: 108 us -> 15.4 us  [per_device(): lax.all_to_all(partial_sum.reshape(copies, tile, step), 'narrow', 0, 0, t...]
    dot_general x2 -> x8, matrix products: 21.5 us -> 56.6 us  [the longest x4 34.2 us: per_device(): lax.dot_general(panel, all_grad, (((0,), (0,)), ((), ())), preferred_elem...]
    all_to_all x0 -> x4, starting transfers between devices: none -> 27.7 us  [per_device(): lax.all_to_all(last_terms.reshape(owners, tile, step), 'wide', 0, 0, tile...]
    all_to_all x0 -> x4, waiting for transfers between devices: none -> 24 us  [per_device(): lax.all_to_all(last_terms.reshape(owners, tile, step), 'wide', 0, 0, tile...]
    all_gather x1 -> x4, blocking collectives: 2.25 us -> 8.54 us  [per_device(): all_grad = lax.all_gather(own_grad, 'narrow', axis=0, tiled=True)]
    reduce_sum x1 -> x4, other arithmetic: 1.42 us -> 7.65 us  [per_device(): gathered_sum = jnp.sum(sent.astype(jnp.float32), axis=0)]
    all_to_all x1, blocking collectives: 30.1 us -> 24.7 us  [per_device(): lax.all_to_all(weight_terms.reshape(devices, rows, width), ('wide', 'narr...]
  transfers between devices with their start and end apart: 3 -> 9, of which waited for: 3 -> 6; matrix products, arithmetic and copies ran while one was open for 5% -> 14% of each run, Pallas kernels for 0% -> 0%
where the time goes in v2:
time: 462 us; the launch traced here: 455 us
  waiting for transfers between devices  265 us (57%)
  matrix products  67.1 us (15%)
  blocking collectives  51.1 us (11%)
  starting transfers between devices  33.6 us (7%)
  other arithmetic  17.1 us (4%)
  between operations  14.2 us (3%)
  local copies, waits for them, and re-layouts  6.36 us (1%)
    all_gather x4, waiting for transfers between devices, per_device(): gathered = lax.all_gather(part, 'wide', axis=0, tiled=True)  223 us
    dot_general x4, matrix products, per_device(): lax.dot_general(panel, all_grad, (((0,), (0,)), ((), ())), preferred_elem...  34.2 us
    all_to_all x4, starting transfers between devices, per_device(): lax.all_to_all(last_terms.reshape(owners, tile, step), 'wide', 0, 0, tile...  27.7 us
    all_to_all x1, blocking collectives, per_device(): lax.all_to_all(weight_terms.reshape(devices, rows, width), ('wide', 'narr...  24.7 us
    all_to_all x4, waiting for transfers between devices, per_device(): lax.all_to_all(last_terms.reshape(owners, tile, step), 'wide', 0, 0, tile...  24 us
    dot_general x4, matrix products, per_device(): partial_sum = jnp.dot(panel, gathered, preferred_element_type=jnp.float32)  22.5 us
    all_to_all x1, waiting for transfers between devices, per_device(): lax.all_to_all(jnp.broadcast_to(mine[None], (devices, rows, width)), ('wi...  16 us
    all_to_all x4, blocking collectives, per_device(): lax.all_to_all(partial_sum.reshape(copies, tile, step), 'narrow', 0, 0, t...  15.4 us
  transfers between devices with their start and end apart: 9, of which 6 were waited for; matrix products, arithmetic and copies ran while one was open for 14% of the time, Pallas kernels for 0%

profile of v2, /device:TPU:0, one launch (start us, length us, event | category | flops | bytes accessed | tf_op | source)
XLA Modules:
  0.0 454.7 jit_solution(18329641770294965872)
XLA Ops:
  7.2 1.5 convolution_convert_fusion.5
  10.2 0.7 compare_convert_fusion.1
  10.9 5.7 %bitcast_convert_fusion = (bf16[2,128,64,128]{3,2,1,0:T(8,128)(2,1)}, f32[2,64,128,128]{3,1,2,0:T(8,128)S(1)}) fusion(bf16[2,48,128,128]{3,2,1,0:T(8,128)(2,1)S(1)} %bitcast.73, s32[2,48]{1,0:T(2,128)} %bitcast.90, bf16[2,48]{1,0:T(2,128)(2,1)S(1)} %compare_convert_fusion.1), kind=kOutput, calls=%fused_computation.5 | convolution fusion | flops 203436032 | bytes 15729216 | tf_op jit(solution)/shard_map/skj,sktc->stjc/dot_general | solution.py:22
  16.6 1.1 bitcast_reduce_fusion
  17.7 2.5 psum.7
  20.3 0.9 bitcast_multiply_fusion.3
  21.2 57.6 %all-gather.5.cloned.1.call-done = bf16[8192,128]{1,0:T(8,128)(2,1)} async-done(((bf16[128,128]{1,0:T(8,128)(2,1)}), bf16[8192,128]{1,0:T(8,128)(2,1)}) %all-gather.5.cloned.1.call-update) | async-done | bytes 2097168 | tf_op jit(solution)/shard_map/all_gather | solution.py:37
  78.8 5.5 %fusion.14 = f32[256,128]{1,0:T(8,128)S(1)} fusion(f32[256,128]{1,0:T(8,128)} %get-tuple-element.25, bf16[8192,128]{1,0:T(8,128)(2,1)} %all-gather.5.cloned.1.call-done, bf16[32,8,64,128]{3,2,1,0:T(8,128)(2,1)} %bitcast.74), kind=kOutput, calls=%fused_computation.27 | convolution fusion | flops 536903680 | bytes 6553600 | tf_op jit(solution)/shard_map/dot_general | solution.py:40
  84.4 3.8 all_to_all.50
  88.2 0.7 multiply_convert_fusion.7
  88.9 2.4 all_gather.26
  91.3 8.5 %convolution_convert_fusion.3 = bf16[8192,128]{1,0:T(8,128)(2,1)} fusion(bf16[256,128]{1,0:T(8,128)(2,1)S(1)} %all_gather.26, bf16[32,8,64,128]{3,2,1,0:T(8,128)(2,1)} %bitcast.75), kind=kOutput, calls=%fused_computation.3 | convolution fusion | flops 537919488 | bytes 6356992 | tf_op jit(solution)/shard_map/dot_general | solution.py:52
  99.8 7.0 %all-to-all-start.1 = ((bf16[64,128,128]{2,1,0:T(8,128)(2,1)}), bf16[64,128,128]{2,1,0:T(8,128)(2,1)}, u32[]{:S(2)}, u32[]{:S(2)}) async-start(bf16[64,128,128]{2,1,0:T(8,128)(2,1)} %bitcast.84), calls=%async_computation.1 | async-start | bytes 4194304 | tf_op jit(solution)/shard_map/all_to_all | solution.py:56
  107.6 55.0 %all-gather.7.cloned.1.call-done = bf16[8192,128]{1,0:T(8,128)(2,1)} async-done(((bf16[128,128]{1,0:T(8,128)(2,1)}), bf16[8192,128]{1,0:T(8,128)(2,1)}) %all-gather.7.cloned.1.call-update) | async-done | bytes 2097168 | tf_op jit(solution)/shard_map/all_gather | solution.py:37
  162.5 5.6 %fusion.17 = f32[256,128]{1,0:T(8,128)S(1)} fusion(f32[256,128]{1,0:T(8,128)S(1)} %copy-done.5, bf16[8192,128]{1,0:T(8,128)(2,1)} %all-gather.7.cloned.1.call-done, bf16[32,8,64,128]{3,2,1,0:T(8,128)(2,1)} %bitcast.76), kind=kOutput, calls=%fused_computation.28 | convolution fusion | flops 536903680 | bytes 6553600 | tf_op jit(solution)/shard_map/dot_general | solution.py:40
  168.2 3.8 all_to_all.51
  172.0 0.7 multiply_convert_fusion.5
  172.7 2.0 all_gather.28
  174.7 8.5 %convolution_convert_fusion.2 = bf16[8192,128]{1,0:T(8,128)(2,1)} fusion(bf16[256,128]{1,0:T(8,128)(2,1)S(1)} %all_gather.28, bf16[32,8,64,128]{3,2,1,0:T(8,128)(2,1)} %bitcast.77), kind=kOutput, calls=%fused_computation.2 | convolution fusion | flops 537919488 | bytes 6356992 | tf_op jit(solution)/shard_map/dot_general | solution.py:52
  183.3 7.0 %all-to-all-start.3 = ((bf16[64,128,128]{2,1,0:T(8,128)(2,1)}), bf16[64,128,128]{2,1,0:T(8,128)(2,1)}, u32[]{:S(2)}, u32[]{:S(2)}) async-start(bf16[64,128,128]{2,1,0:T(8,128)(2,1)} %bitcast.83), calls=%async_computation.3 | async-start | bytes 4194304 | tf_op jit(solution)/shard_map/all_to_all | solution.py:56
  190.8 55.3 %all-gather.9.cloned.1.call-done = bf16[8192,128]{1,0:T(8,128)(2,1)} async-done(((bf16[128,128]{1,0:T(8,128)(2,1)}), bf16[8192,128]{1,0:T(8,128)(2,1)}) %all-gather.9.cloned.1.call-update) | async-done | bytes 2097168 | tf_op jit(solution)/shard_map/all_gather | solution.py:37
  246.1 5.6 %fusion.20 = f32[256,128]{1,0:T(8,128)S(1)} fusion(f32[256,128]{1,0:T(8,128)S(1)} %copy-done.4, bf16[8192,128]{1,0:T(8,128)(2,1)} %all-gather.9.cloned.1.call-done, bf16[32,8,64,128]{3,2,1,0:T(8,128)(2,1)} %bitcast.78), kind=kOutput, calls=%fused_computation.29 | convolution fusion | flops 536903680 | bytes 6553600 | tf_op jit(solution)/shard_map/dot_general | solution.py:40
  251.8 3.8 all_to_all.52
  255.6 0.9 multiply_convert_fusion.3
  256.5 2.1 all_gather.30
  258.6 8.5 %convolution_convert_fusion.1 = bf16[8192,128]{1,0:T(8,128)(2,1)} fusion(bf16[256,128]{1,0:T(8,128)(2,1)S(1)} %all_gather.30, bf16[32,8,64,128]{3,2,1,0:T(8,128)(2,1)} %bitcast.79), kind=kOutput, calls=%fused_computation.1 | convolution fusion | flops 537919488 | bytes 6356992 | tf_op jit(solution)/shard_map/dot_general | solution.py:52
  267.1 7.0 %all-to-all-start.5 = ((bf16[64,128,128]{2,1,0:T(8,128)(2,1)}), bf16[64,128,128]{2,1,0:T(8,128)(2,1)}, u32[]{:S(2)}, u32[]{:S(2)}) async-start(bf16[64,128,128]{2,1,0:T(8,128)(2,1)} %bitcast.85), calls=%async_computation.5 | async-start | bytes 4194304 | tf_op jit(solution)/shard_map/all_to_all | solution.py:56
  274.1 55.5 %all-gather.11.cloned.1.call-done = bf16[8192,128]{1,0:T(8,128)(2,1)} async-done(((bf16[128,128]{1,0:T(8,128)(2,1)}), bf16[8192,128]{1,0:T(8,128)(2,1)}) %all-gather.11.cloned.1.call-update) | async-done | bytes 2097168 | tf_op jit(solution)/shard_map/all_gather | solution.py:37
  329.6 5.6 %fusion.23 = f32[256,128]{1,0:T(8,128)S(1)} fusion(f32[256,128]{1,0:T(8,128)S(1)} %copy-done.3, bf16[8192,128]{1,0:T(8,128)(2,1)} %all-gather.11.cloned.1.call-done, bf16[32,8,64,128]{3,2,1,0:T(8,128)(2,1)} %bitcast.80), kind=kOutput, calls=%fused_computation.30 | convolution fusion | flops 536903680 | bytes 6553600 | tf_op jit(solution)/shard_map/dot_general | solution.py:40
  335.3 3.8 all_to_all.53
  339.1 1.5 multiply_convert_fusion
  340.6 2.1 all_gather.31
  342.7 8.5 %convolution_convert_fusion = bf16[8192,128]{1,0:T(8,128)(2,1)} fusion(bf16[256,128]{1,0:T(8,128)(2,1)S(1)} %all_gather.31, bf16[32,8,64,128]{3,2,1,0:T(8,128)(2,1)} %bitcast.81), kind=kOutput, calls=%fused_computation | convolution fusion | flops 537919488 | bytes 6356992 | tf_op jit(solution)/shard_map/dot_general | solution.py:52
  351.2 6.8 %all-to-all-start.7 = ((bf16[64,128,128]{2,1,0:T(8,128)(2,1)}), bf16[64,128,128]{2,1,0:T(8,128)(2,1)}, u32[]{:S(2)}, u32[]{:S(2)}) async-start(bf16[64,128,128]{2,1,0:T(8,128)(2,1)} %bitcast.82), calls=%async_computation.7 | async-start | bytes 4194304 | tf_op jit(solution)/shard_map/all_to_all | solution.py:56
  358.1 1.9 convert_reduce_fusion.3
  360.0 1.9 convert_reduce_fusion.2
  361.9 1.9 convert_reduce_fusion.1
  363.9 24.0 %all-to-all-done.7 = bf16[64,128,128]{2,1,0:T(8,128)(2,1)} async-done(((bf16[64,128,128]{2,1,0:T(8,128)(2,1)}), bf16[64,128,128]{2,1,0:T(8,128)(2,1)}, u32[]{:S(2)}, u32[]{:S(2)}) %all-to-all-start.7) | async-done | bytes 2097184 | tf_op jit(solution)/shard_map/all_to_all | solution.py:56
  387.8 1.9 convert_reduce_fusion
  389.8 1.3 convolution_bitcast_fusion
  391.1 2.5 reshape.94
  393.6 24.7 %all_to_all.54 = f32[128,4,512]{2,1,0:T(4,128)} all-to-all(f32[128,4,512]{2,1,0:T(4,128)} %reshape.94), channel_id=1, replica_groups=mesh['wide'=64,'narrow'=2] {'wide','narrow'}, dimensions={0} | all-to-all | bytes 2097152 | tf_op jit(solution)/shard_map/all_to_all | solution.py:70
  418.3 1.4 reduce_sum.102
  419.7 1.1 broadcast_in_dim.2
  420.8 5.8 %all-to-all-start.9 = ((f32[128,4,512]{2,1,0:T(4,128)}), f32[128,4,512]{2,1,0:T(4,128)}, u32[]{:S(2)}, u32[]{:S(2)}) async-start(f32[128,4,512]{2,1,0:T(4,128)} %broadcast_in_dim.2), calls=%async_computation.9 | async-start | bytes 2097152 | tf_op jit(solution)/shard_map/all_to_all | solution.py:74
  427.3 2.0 convolution_convert_fusion.4
  429.3 16.0 %all-to-all-done.9 = f32[128,4,512]{2,1,0:T(4,128)} async-done(((f32[128,4,512]{2,1,0:T(4,128)}), f32[128,4,512]{2,1,0:T(4,128)}, u32[]{:S(2)}, u32[]{:S(2)}) %all-to-all-start.9) | async-done | bytes 1048608 | tf_op jit(solution)/shard_map/all_to_all | solution.py:74
  445.3 2.6 reshape.95
  (43 shorter events, 3.7 us)
Async XLA Ops:
  7.2 3.7 copy-start
  7.2 71.6 %all-gather.5.cloned.1.call-start = ((), (), s32[]{:S(2)}) async-start(), calls=%async_computation.10 | async-start | bytes 2129920 | tf_op jit(solution)/shard_map/all_gather | solution.py:37
  9.4 153.1 %all-gather.7.cloned.1.call-start = ((), (), s32[]{:S(2)}) async-start(), calls=%async_computation.11 | async-start | bytes 2129920 | tf_op jit(solution)/shard_map/all_gather | solution.py:37
  78.8 9.4 %copy-start.2 = (bf16[128,512]{1,0:T(8,128)(2,1)S(1)}, bf16[128,512]{1,0:T(8,128)(2,1)}, u32[]{:S(2)}) copy-start(bf16[128,512]{1,0:T(8,128)(2,1)} %param.11) | copy-start | bytes 393220
  99.8 62.7 %copy-start.5 = (f32[256,128]{1,0:T(8,128)S(1)}, f32[256,128]{1,0:T(8,128)}, u32[]{:S(2)}) copy-start(f32[256,128]{1,0:T(8,128)} %get-tuple-element.26) | copy-start | bytes 393220
  99.8 62.7 %all-to-all-start.1 = ((bf16[64,128,128]{2,1,0:T(8,128)(2,1)}), bf16[64,128,128]{2,1,0:T(8,128)(2,1)}, u32[]{:S(2)}, u32[]{:S(2)}) async-start(bf16[64,128,128]{2,1,0:T(8,128)(2,1)} %bitcast.84), calls=%async_computation.1 | async-start | bytes 4194304 | tf_op jit(solution)/shard_map/all_to_all | solution.py:56
  106.8 139.3 %all-gather.9.cloned.1.call-start = ((), (), s32[]{:S(2)}) async-start(), calls=%async_computation.12 | async-start | bytes 2129920 | tf_op jit(solution)/shard_map/all_gather | solution.py:37
  183.3 62.9 %copy-start.4 = (f32[256,128]{1,0:T(8,128)S(1)}, f32[256,128]{1,0:T(8,128)}, u32[]{:S(2)}) copy-start(f32[256,128]{1,0:T(8,128)} %get-tuple-element.27) | copy-start | bytes 393220
  183.3 62.8 %all-to-all-start.3 = ((bf16[64,128,128]{2,1,0:T(8,128)(2,1)}), bf16[64,128,128]{2,1,0:T(8,128)(2,1)}, u32[]{:S(2)}, u32[]{:S(2)}) async-start(bf16[64,128,128]{2,1,0:T(8,128)(2,1)} %bitcast.83), calls=%async_computation.3 | async-start | bytes 4194304 | tf_op jit(solution)/shard_map/all_to_all | solution.py:56
  190.3 139.3 %all-gather.11.cloned.1.call-start = ((), (), s32[]{:S(2)}) async-start(), calls=%async_computation.13 | async-start | bytes 2129920 | tf_op jit(solution)/shard_map/all_gather | solution.py:37
  267.1 62.5 %copy-start.3 = (f32[256,128]{1,0:T(8,128)S(1)}, f32[256,128]{1,0:T(8,128)}, u32[]{:S(2)}) copy-start(f32[256,128]{1,0:T(8,128)} %get-tuple-element.28) | copy-start | bytes 393220
  267.1 62.5 %all-to-all-start.5 = ((bf16[64,128,128]{2,1,0:T(8,128)(2,1)}), bf16[64,128,128]{2,1,0:T(8,128)(2,1)}, u32[]{:S(2)}, u32[]{:S(2)}) async-start(bf16[64,128,128]{2,1,0:T(8,128)(2,1)} %bitcast.85), calls=%async_computation.5 | async-start | bytes 4194304 | tf_op jit(solution)/shard_map/all_to_all | solution.py:56
  351.2 36.6 %all-to-all-start.7 = ((bf16[64,128,128]{2,1,0:T(8,128)(2,1)}), bf16[64,128,128]{2,1,0:T(8,128)(2,1)}, u32[]{:S(2)}, u32[]{:S(2)}) async-start(bf16[64,128,128]{2,1,0:T(8,128)(2,1)} %bitcast.82), calls=%async_computation.7 | async-start | bytes 4194304 | tf_op jit(solution)/shard_map/all_to_all | solution.py:56
  358.1 31.7 %copy-start.1 = (bf16[128,512]{1,0:T(8,128)(2,1)S(1)}, bf16[128,512]{1,0:T(8,128)(2,1)}, u32[]{:S(2)}) copy-start(bf16[128,512]{1,0:T(8,128)(2,1)} %param.6) | copy-start | bytes 393220
  391.1 35.5 %copy-start.6 = (bf16[128,128]{1,0:T(8,128)(2,1)S(1)}, bf16[128,128]{1,0:T(8,128)(2,1)}, u32[]{:S(2)}) copy-start(bf16[128,128]{1,0:T(8,128)(2,1)} %get-tuple-element.19) | copy-start | bytes 98308
  391.1 35.5 %copy-start.7 = (bf16[128,128]{1,0:T(8,128)(2,1)S(1)}, bf16[128,128]{1,0:T(8,128)(2,1)}, u32[]{:S(2)}) copy-start(bf16[128,128]{1,0:T(8,128)(2,1)} %get-tuple-element.21) | copy-start | bytes 98308
  391.1 35.5 %copy-start.8 = (bf16[128,128]{1,0:T(8,128)(2,1)S(1)}, bf16[128,128]{1,0:T(8,128)(2,1)}, u32[]{:S(2)}) copy-start(bf16[128,128]{1,0:T(8,128)(2,1)} %get-tuple-element.18) | copy-start | bytes 98308
  420.8 24.5 %all-to-all-start.9 = ((f32[128,4,512]{2,1,0:T(4,128)}), f32[128,4,512]{2,1,0:T(4,128)}, u32[]{:S(2)}, u32[]{:S(2)}) async-start(f32[128,4,512]{2,1,0:T(4,128)} %broadcast_in_dim.2), calls=%async_computation.9 | async-start | bytes 2097152 | tf_op jit(solution)/shard_map/all_to_all | solution.py:74
Sparse Core Ops, SparseCore 0:
  10.9 67.8 all-gather.4
  81.7 80.7 all-gather.6
  165.4 80.7 all-gather.8
  248.9 80.7 all-gather.10

commit v3 on v0

--- a/solution.py
+++ b/solution.py
@@ -13,6 +13,7 @@
     columns = tile_cols[:, 0, :]
     counts = tile_count[:, 0]
     tiles = tile_weights[:, 0]
+    gathered_features = lax.all_gather(features, "wide", axis=0, tiled=True)
     live = (jnp.arange(slots, dtype=jnp.int32)[None, :] < counts[:, None]).astype(jnp.bfloat16)
     onehot = (columns[..., None] == jnp.arange(owners, dtype=jnp.int32)).astype(
         jnp.bfloat16
@@ -24,41 +25,57 @@
     scale = lax.rsqrt(degree)
     panel = dense.astype(jnp.bfloat16)
     projected = jnp.dot(features, weight, preferred_element_type=jnp.float32).astype(jnp.bfloat16)
+    gathered = jnp.dot(gathered_features, weight, preferred_element_type=jnp.float32).astype(
+        jnp.bfloat16
+    )
     own = lax.axis_index("narrow")
-    part_cols = panel
-    partial_sum = jnp.dot(
-        part_cols,
-        lax.all_gather(projected, "wide", axis=0, tiled=True),
-        preferred_element_type=jnp.float32,
-    )
+    partial_sum = jnp.dot(panel, gathered, preferred_element_type=jnp.float32)
     selector = (jnp.arange(copies, dtype=jnp.int32) == own).astype(jnp.float32)
     self_term = selector[:, None, None] * projected.astype(jnp.float32)[None]
     partial_sum = partial_sum + self_term.reshape(copies * tile, width)
     own_scale = lax.dynamic_slice_in_dim(scale, own * tile, tile, 0)[:, None]
-    preact = lax.psum_scatter(partial_sum, "narrow", scatter_dimension=0, tiled=True) * own_scale
+    halves = lax.all_to_all(partial_sum.reshape(copies, tile, width), "narrow", 0, 0, tiled=True)
+    preact = jnp.sum(halves, axis=0) * own_scale
     activated = jax.nn.silu(preact).astype(jnp.bfloat16)
     sig = jax.nn.sigmoid(preact)
     own_grad = (
         cotangent.astype(jnp.float32) * sig * (1.0 + preact * (1.0 - sig)) * own_scale
     ).astype(jnp.bfloat16)
     all_grad = lax.all_gather(own_grad, "narrow", axis=0, tiled=True)
-    part_cols = panel
-    gathered_sum = lax.psum_scatter(
-        lax.dot_general(
-            part_cols, all_grad, (((0,), (0,)), ((), ())), preferred_element_type=jnp.float32
-        ),
-        "wide",
-        scatter_dimension=0,
-        tiled=True,
+    terms = lax.dot_general(
+        panel, all_grad, (((0,), (0,)), ((), ())), preferred_element_type=jnp.float32
+    ).astype(jnp.bfloat16)
+    weight_terms = lax.dot_general(
+        gathered_features, terms, (((0,), (0,)), ((), ())), preferred_element_type=jnp.float32
+    ) + lax.dot_general(
+        features, own_grad, (((0,), (0,)), ((), ())), preferred_element_type=jnp.float32
     )
+    rows = width // owners
+    high = weight_terms.astype(jnp.bfloat16)
+    low = (weight_terms - high.astype(jnp.float32)).astype(jnp.bfloat16)
+    payload = jnp.concatenate(
+        [
+            terms.reshape(owners, tile, width),
+            high.reshape(owners, rows, width),
+            low.reshape(owners, rows, width),
+        ],
+        axis=1,
+    )
+    received = lax.all_to_all(payload, "wide", 0, 0, tiled=True)
+    band = jnp.sum(
+        received[:, tile:tile + rows].astype(jnp.float32)
+        + received[:, tile + rows:].astype(jnp.float32),
+        axis=0,
+    )
+    band = lax.psum(band, "narrow")
+    grad_weight = lax.all_to_all(
+        jnp.broadcast_to(band[None], (owners, rows, width)), "wide", 0, 0, tiled=True
+    ).reshape(width, width)
+    gathered_sum = jnp.sum(received[:, :tile].astype(jnp.float32), axis=0)
     message = (gathered_sum + own_grad.astype(jnp.float32)).astype(jnp.bfloat16)
     grad_features = lax.dot_general(
         message, weight, (((1,), (1,)), ((), ())), preferred_element_type=jnp.float32
     ).astype(jnp.bfloat16)
-    weight_terms = lax.dot_general(
-        features, message, (((0,), (0,)), ((), ())), preferred_element_type=jnp.float32
-    )
-    grad_weight = lax.psum(weight_terms, ("wide", "narrow"))
     return (activated, grad_features, grad_weight)
 
 

time: 687 us -> 302 us (0.44)
  waiting for transfers between devices: 614 us -> 84.6 us
  blocking collectives: 4.74 us -> 132 us
  starting transfers between devices: 0.16 us -> 8.98 us
    reduce_scatter x2 -> x0, waiting for transfers between devices: 398 us -> none  [the longest x1 395 us: per_device(): lax.psum_scatter(lax.dot_general(part_cols, all_grad, (((0,), (0,)), ((),...]
    psum x1 -> x0, waiting for transfers between devices: 143 us -> none  [per_device(): grad_weight = lax.psum(weight_terms, ('wide', 'narrow'))]
    all_to_all x0 -> x2, blocking collectives: none -> 124 us  [the longest x1 118 us: per_device(): received = lax.all_to_all(payload, 'wide', 0, 0, tiled=True)]
    all_to_all x0 -> x1, waiting for transfers between devices: none -> 13.1 us  [per_device(): lax.all_to_all(jnp.broadcast_to(band[None], (owners, rows, width)), 'wide...]
    all_to_all x0 -> x1, starting transfers between devices: none -> 8.94 us  [per_device(): lax.all_to_all(jnp.broadcast_to(band[None], (owners, rows, width)), 'wide...]
    dot_general x3 -> x4, matrix products: 29.7 us -> 34 us  [the longest x1 14.8 us: per_device(): partial_sum = jnp.dot(panel, gathered, preferred_element_type=jnp.float32)]
  transfers between devices with their start and end apart: 4 -> 2, of which waited for: 4 -> 2; matrix products, arithmetic and copies ran while one was open for 2% -> 5% of each run, Pallas kernels for 0% -> 0%
where the time goes in v3:
time: 302 us
  blocking collectives  132 us (44%)
  waiting for transfers between devices  84.6 us (28%)
  matrix products  42 us (14%)
  between operations  14.1 us (5%)
  other arithmetic  12.3 us (4%)
  starting transfers between devices  8.98 us (3%)
  local copies, waits for them, and re-layouts  7.38 us (2%)
    all_to_all x1, blocking collectives, per_device(): received = lax.all_to_all(payload, 'wide', 0, 0, tiled=True)  118 us
    all_gather x1, waiting for transfers between devices, per_device(): gathered_features = lax.all_gather(features, 'wide', axis=0, tiled=True)  70.9 us
    dot_general x1, matrix products, per_device(): partial_sum = jnp.dot(panel, gathered, preferred_element_type=jnp.float32)  14.8 us
    all_to_all x1, waiting for transfers between devices, per_device(): lax.all_to_all(jnp.broadcast_to(band[None], (owners, rows, width)), 'wide...  13.1 us
    dot_general x1, matrix products, per_device(): lax.dot_general(panel, all_grad, (((0,), (0,)), ((), ())), preferred_elem...  11.7 us
    all_to_all x1, starting transfers between devices, per_device(): lax.all_to_all(jnp.broadcast_to(band[None], (owners, rows, width)), 'wide...  8.94 us
    dot_general x1, matrix products, per_device(): lax.dot_general(gathered_features, terms, (((0,), (0,)), ((), ())), prefe...  7.18 us
    unnamed x11, local copies, waits for them, and re-layouts  6.13 us
  transfers between devices with their start and end apart: 2, of which 2 were waited for; matrix products, arithmetic and copies ran while one was open for 5% of the time, Pallas kernels for 0%

profile of v3, /device:TPU:0, one launch (start us, length us, event | category | flops | bytes accessed | tf_op | source)
XLA Modules:
  0.0 301.8 jit_solution(5386784163049312792)
XLA Ops:
  7.2 0.0 copy-start
  7.2 0.0 all-gather.2.cloned.1.call-start
  7.2 0.7 all-gather.2.cloned.1.call-update
  7.9 0.9 compare_convert_fusion.1
  8.8 0.2 copy-done
  9.1 0.0 copy-start.3
  9.1 5.7 %bitcast_convert_fusion = (bf16[2,128,64,128]{3,2,1,0:T(8,128)(2,1)}, f32[2,64,128,128]{3,1,2,0:T(8,128)S(1)}) fusion(bf16[2,48,128,128]{3,2,1,0:T(8,128)(2,1)S(1)} %bitcast.48, s32[2,48]{1,0:T(2,128)} %bitcast.53, bf16[2,48]{1,0:T(2,128)(2,1)S(1)} %compare_convert_fusion.1), kind=kOutput, calls=%fused_computation.5 | convolution fusion | flops 203436032 | bytes 15729216 | tf_op jit(solution)/shard_map/skj,sktc->stjc/dot_general | solution.py:21
  14.8 1.1 bitcast_reduce_fusion
  15.9 2.6 psum.14
  18.5 0.1 dynamic_slice.3
  18.6 0.1 broadcast_bitcast_fusion
  18.7 0.0 copy-done.3
  18.7 1.3 fusion.11
  20.0 0.9 bitcast_multiply_fusion
  20.9 70.9 %all-gather.2.cloned.1.call-done = bf16[8192,512]{1,0:T(8,128)(2,1)} async-done(((bf16[128,512]{1,0:T(8,128)(2,1)}), bf16[8192,512]{1,0:T(8,128)(2,1)}) %all-gather.2.cloned.1.call-update) | async-done | bytes 8388624 | tf_op jit(solution)/shard_map/all_gather | solution.py:16
  91.8 0.0 copy-start.4
  91.8 14.8 %fusion.8 = f32[256,512]{1,0:T(8,128)} fusion(f32[256,512]{1,0:T(8,128)} %bitcast_multiply_fusion, bf16[8192,512]{1,0:T(8,128)(2,1)} %all-gather.2.cloned.1.call-done, bf16[512,512]{1,0:T(8,128)(2,1)} %param.7, bf16[32,8,64,128]{3,2,1,0:T(8,128)(2,1)} %bitcast.50), kind=kOutput, calls=%fused_computation.15 | convolution fusion | flops 6446776320 | bytes 14155776 | tf_op jit(solution)/shard_map/dot_general | solution.py:32
  106.6 6.1 %all_to_all.15 = f32[2,128,512]{2,1,0:T(8,128)} all-to-all(f32[2,128,512]{2,1,0:T(8,128)} %bitcast.52), channel_id=1, replica_groups=mesh['wide'=64,'narrow'=2] {'narrow'}, dimensions={0} | all-to-all | bytes 1048576 | tf_op jit(solution)/shard_map/all_to_all | solution.py:37
  112.7 1.8 reduce_sum.38
  114.5 0.0 copy-done.4
  114.5 1.8 multiply_convert_fusion
  116.3 2.2 all_gather.7
  118.5 0.3 fusion.20
  118.8 11.7 %convolution_convert_fusion.1 = bf16[8192,512]{1,0:T(8,128)(2,1)S(1)} fusion(bf16[256,512]{1,0:T(8,128)(2,1)S(1)} %all_gather.7, bf16[32,8,64,128]{3,2,1,0:T(8,128)(2,1)} %bitcast.51), kind=kOutput, calls=%fused_computation.2 | convolution fusion | flops 2151677952 | bytes 12845056 | tf_op jit(solution)/shard_map/dot_general | solution.py:45
  130.5 7.2 %convert_bitcast_fusion = (bf16[64,8,512]{2,1,0:T(8,128)(2,1)S(1)}, bf16[64,8,512]{2,1,0:T(8,128)(2,1)S(1)}) fusion(f32[512,512]{0,1:T(8,128)S(1)} %fusion.20, bf16[8192,512]{1,0:T(8,128)(2,1)S(1)} %convolution_convert_fusion.1, bf16[8192,512]{1,0:T(8,128)(2,1)} %all-gather.2.cloned.1.call-done), kind=kOutput, calls=%fused_computation.24 | convolution fusion | flops 4296278016 | bytes 18874368 | tf_op jit(solution)/shard_map/dot_general | solution.py:48
  137.7 0.7 pad_maximum_fusion
  138.5 118.2 %all_to_all.16 = bf16[64,144,512]{2,1,0:T(8,128)(2,1)S(1)} all-to-all(bf16[64,144,512]{2,1,0:T(8,128)(2,1)S(1)} %pad_maximum_fusion), channel_id=1, replica_groups=mesh['wide'=64,'narrow'=2] {'wide'}, dimensions={0} | all-to-all | bytes 18874368 | tf_op jit(solution)/shard_map/all_to_all | solution.py:64
  256.6 0.0 copy-start.1
  256.6 3.6 %copy-done.1 = bf16[64,144,512]{2,1,0:T(8,128)(2,1)} copy-done((bf16[64,144,512]{2,1,0:T(8,128)(2,1)}, bf16[64,144,512]{2,1,0:T(8,128)(2,1)S(1)}, u32[]{:S(2)}) %copy-start.1) | copy-done | bytes 9437208
  260.3 0.2 add_reduce_fusion
  260.4 3.4 %psum.15 = f32[8,512]{1,0:T(8,128)S(1)} all-reduce(f32[8,512]{1,0:T(8,128)S(1)} %add_reduce_fusion), channel_id=1, replica_groups=mesh['wide'=64,'narrow'=2] {'narrow'}, use_global_device_ids=true, to_apply=%region_5.6 | all-reduce | flops 4096 | bytes 32768 | tf_op jit(solution)/shard_map/psum | solution.py:70
  263.8 1.1 broadcast_in_dim.2
  264.9 8.9 %all-to-all-start.2 = ((f32[64,8,512]{2,1,0:T(8,128)}), f32[64,8,512]{2,1,0:T(8,128)}, u32[]{:S(2)}, u32[]{:S(2)}) async-start(f32[64,8,512]{2,1,0:T(8,128)} %broadcast_in_dim.2), calls=%async_computation.2 | async-start | bytes 2097152 | tf_op jit(solution)/shard_map/all_to_all | solution.py:71
  273.8 0.0 copy-start.2
  273.8 4.8 %convert_reduce_fusion = f32[128,512]{1,0:T(8,128)S(1)} fusion(bf16[64,144,512]{2,1,0:T(8,128)(2,1)} %copy-done.1), kind=kLoop, calls=%fused_computation | loop fusion | flops 8323072 | bytes 8650752 | tf_op jit(solution)/shard_map/reduce_sum | solution.py:74
  278.7 0.0 copy-done.2
  278.7 1.0 convolution_convert_fusion.2
  279.7 13.1 %all-to-all-done.2 = f32[64,8,512]{2,1,0:T(8,128)} async-done(((f32[64,8,512]{2,1,0:T(8,128)}), f32[64,8,512]{2,1,0:T(8,128)}, u32[]{:S(2)}, u32[]{:S(2)}) %all-to-all-start.2) | async-done | bytes 1048608 | tf_op jit(solution)/shard_map/all_to_all | solution.py:71
  292.7 2.3 copy.27
  (2 shorter events, 0.0 us)
Async XLA Ops:
  7.2 1.9 copy-start
  7.2 84.6 %all-gather.2.cloned.1.call-start = ((), (), s32[]{:S(2)}) async-start(), calls=%async_computation.3 | async-start | bytes 8519680 | tf_op jit(solution)/shard_map/all_gather | solution.py:16
  9.1 9.6 %copy-start.3 = (bf16[128,512]{1,0:T(8,128)(2,1)S(1)}, bf16[128,512]{1,0:T(8,128)(2,1)}, u32[]{:S(2)}) copy-start(bf16[128,512]{1,0:T(8,128)(2,1)} %param.6) | copy-start | bytes 393220
  91.8 22.7 %copy-start.4 = (bf16[128,512]{1,0:T(8,128)(2,1)S(1)}, bf16[128,512]{1,0:T(8,128)(2,1)}, u32[]{:S(2)}) copy-start(bf16[128,512]{1,0:T(8,128)(2,1)} %param.11) | copy-start | bytes 393220
  256.6 3.6 %copy-start.1 = (bf16[64,144,512]{2,1,0:T(8,128)(2,1)}, bf16[64,144,512]{2,1,0:T(8,128)(2,1)S(1)}, u32[]{:S(2)}) copy-start(bf16[64,144,512]{2,1,0:T(8,128)(2,1)S(1)} %all_to_all.16) | copy-start | bytes 28311556
  264.9 27.8 %all-to-all-start.2 = ((f32[64,8,512]{2,1,0:T(8,128)}), f32[64,8,512]{2,1,0:T(8,128)}, u32[]{:S(2)}, u32[]{:S(2)}) async-start(f32[64,8,512]{2,1,0:T(8,128)} %broadcast_in_dim.2), calls=%async_computation.2 | async-start | bytes 2097152 | tf_op jit(solution)/shard_map/all_to_all | solution.py:71
  273.8 4.9 %copy-start.2 = (bf16[512,512]{1,0:T(8,128)(2,1)S(1)}, bf16[512,512]{1,0:T(8,128)(2,1)}, u32[]{:S(2)}) copy-start(bf16[512,512]{1,0:T(8,128)(2,1)} %param.7) | copy-start | bytes 1572868
Sparse Core Ops, SparseCore 0:
  10.9 80.8 all-gather.1

commit v4 on v3

--- a/solution.py
+++ b/solution.py
@@ -25,11 +25,12 @@
     scale = lax.rsqrt(degree)
     panel = dense.astype(jnp.bfloat16)
     projected = jnp.dot(features, weight, preferred_element_type=jnp.float32).astype(jnp.bfloat16)
-    gathered = jnp.dot(gathered_features, weight, preferred_element_type=jnp.float32).astype(
-        jnp.bfloat16
+    own = lax.axis_index("narrow")
+    aggregated = jnp.dot(panel, gathered_features, preferred_element_type=jnp.float32)
+    partial_sum = jnp.dot(
+        aggregated, weight.astype(jnp.float32), precision=lax.Precision.HIGHEST,
+        preferred_element_type=jnp.float32,
     )
-    own = lax.axis_index("narrow")
-    partial_sum = jnp.dot(panel, gathered, preferred_element_type=jnp.float32)
     selector = (jnp.arange(copies, dtype=jnp.int32) == own).astype(jnp.float32)
     self_term = selector[:, None, None] * projected.astype(jnp.float32)[None]
     partial_sum = partial_sum + self_term.reshape(copies * tile, width)
@@ -46,7 +47,8 @@
         panel, all_grad, (((0,), (0,)), ((), ())), preferred_element_type=jnp.float32
     ).astype(jnp.bfloat16)
     weight_terms = lax.dot_general(
-        gathered_features, terms, (((0,), (0,)), ((), ())), preferred_element_type=jnp.float32
+        aggregated, all_grad.astype(jnp.float32), (((0,), (0,)), ((), ())),
+        precision=lax.Precision.HIGHEST, preferred_element_type=jnp.float32,
     ) + lax.dot_general(
         features, own_grad, (((0,), (0,)), ((), ())), preferred_element_type=jnp.float32
     )

time: 302 us -> 290 us (0.960)
  matrix products: 42 us -> 31.4 us
    dot_general x2 -> x3, matrix products: 22 us -> 11.4 us  [the longest x1 9.13 us: per_device(): jnp.dot(panel, gathered_features, preferred_element_type=jnp.float32)]
    unnamed x11 -> x17, local copies, waits for them, and re-layouts: 6.13 us -> 6.33 us
where the time goes in v4:
time: 290 us
  blocking collectives  131 us (45%)
  waiting for transfers between devices  84.8 us (29%)
  matrix products  31.4 us (11%)
  between operations  14.1 us (5%)
  other arithmetic  12.3 us (4%)
  starting transfers between devices  8.84 us (3%)
  local copies, waits for them, and re-layouts  7.58 us (3%)
    all_to_all x1, blocking collectives, per_device(): received = lax.all_to_all(payload, 'wide', 0, 0, tiled=True)  118 us
    all_gather x1, waiting for transfers between devices, per_device(): gathered_features = lax.all_gather(features, 'wide', axis=0, tiled=True)  71.1 us
    all_to_all x1, waiting for transfers between devices, per_device(): lax.all_to_all(jnp.broadcast_to(band[None], (owners, rows, width)), 'wide...  13.1 us
    dot_general x1, matrix products, per_device(): lax.dot_general(panel, all_grad, (((0,), (0,)), ((), ())), preferred_elem...  11.7 us
    dot_general x1, matrix products, per_device(): jnp.dot(panel, gathered_features, preferred_element_type=jnp.float32)  9.13 us
    all_to_all x1, starting transfers between devices, per_device(): lax.all_to_all(jnp.broadcast_to(band[None], (owners, rows, width)), 'wide...  8.8 us
    unnamed x17, local copies, waits for them, and re-layouts  6.33 us
  transfers between devices with their start and end apart: 2, of which 2 were waited for; matrix products, arithmetic and copies ran while one was open for 5% of the time, Pallas kernels for 0%

profile of v4, /device:TPU:0, one launch (start us, length us, event | category | flops | bytes accessed | tf_op | source)
XLA Modules:
  0.0 289.9 jit_solution(12104186548526854254)
XLA Ops:
  7.2 0.0 copy-start
  7.2 0.0 all-gather.2.cloned.1.call-start
  7.2 0.7 all-gather.2.cloned.1.call-update
  7.9 0.9 compare_convert_fusion.1
  8.8 0.2 copy-done
  9.1 0.0 copy-start.6
  9.1 5.7 %bitcast_convert_fusion = (bf16[2,128,64,128]{3,2,1,0:T(8,128)(2,1)}, f32[2,64,128,128]{3,1,2,0:T(8,128)S(1)}) fusion(bf16[2,48,128,128]{3,2,1,0:T(8,128)(2,1)S(1)} %bitcast.49, s32[2,48]{1,0:T(2,128)} %bitcast.54, bf16[2,48]{1,0:T(2,128)(2,1)S(1)} %compare_convert_fusion.1), kind=kOutput, calls=%fused_computation.4 | convolution fusion | flops 203436032 | bytes 15729216 | tf_op jit(solution)/shard_map/skj,sktc->stjc/dot_general | solution.py:21
  14.8 1.1 bitcast_reduce_fusion
  15.9 2.5 psum.14
  18.4 0.1 dynamic_slice.3
  18.4 0.1 broadcast_bitcast_fusion
  18.5 0.0 copy-done.6
  18.5 1.3 fusion.8
  19.8 0.9 bitcast_multiply_fusion
  20.7 71.1 %all-gather.2.cloned.1.call-done = bf16[8192,512]{1,0:T(8,128)(2,1)} async-done(((bf16[128,512]{1,0:T(8,128)(2,1)}), bf16[8192,512]{1,0:T(8,128)(2,1)}) %all-gather.2.cloned.1.call-update) | async-done | bytes 8388624 | tf_op jit(solution)/shard_map/all_gather | solution.py:16
  91.8 0.0 copy-start.2
  91.8 0.0 copy-start.5
  91.8 0.0 copy-start.7
  91.8 9.1 %fusion.1 = f32[256,512]{1,0:T(8,128)S(1)} fusion(bf16[8192,512]{1,0:T(8,128)(2,1)} %all-gather.2.cloned.1.call-done, bf16[32,8,64,128]{3,2,1,0:T(8,128)(2,1)} %bitcast.51), kind=kOutput, calls=%fused_computation.6 | convolution fusion | flops 2147483648 | bytes 13107200 | tf_op jit(solution)/shard_map/dot_general | solution.py:29
  100.9 0.0 copy-done.2
  100.9 0.0 copy-done.5
  100.9 0.0 copy-start.4
  100.9 0.6 convolution_add_fusion
  101.5 0.2 copy-done.4
  101.7 4.9 %all_to_all.15 = f32[2,128,512]{2,1,0:T(8,128)} all-to-all(f32[2,128,512]{2,1,0:T(8,128)S(1)} %bitcast.53), channel_id=1, replica_groups=mesh['wide'=64,'narrow'=2] {'narrow'}, dimensions={0} | all-to-all | bytes 1048576 | tf_op jit(solution)/shard_map/all_to_all | solution.py:38
  106.6 1.8 reduce_sum.38
  108.4 0.0 copy-done.7
  108.4 1.8 multiply_convert_fusion
  110.2 2.2 all_gather.7
  112.4 1.7 fusion.17
  114.0 11.7 %convolution_convert_fusion = bf16[8192,512]{1,0:T(8,128)(2,1)S(1)} fusion(bf16[256,512]{1,0:T(8,128)(2,1)S(1)} %all_gather.7, bf16[32,8,64,128]{3,2,1,0:T(8,128)(2,1)} %bitcast.52), kind=kOutput, calls=%fused_computation.1 | convolution fusion | flops 2151677952 | bytes 12845056 | tf_op jit(solution)/shard_map/dot_general | solution.py:46
  125.7 0.3 convert_bitcast_fusion
  126.1 0.7 pad_maximum_fusion
  126.8 118.0 %all_to_all.16 = bf16[64,144,512]{2,1,0:T(8,128)(2,1)S(1)} all-to-all(bf16[64,144,512]{2,1,0:T(8,128)(2,1)S(1)} %pad_maximum_fusion), channel_id=1, replica_groups=mesh['wide'=64,'narrow'=2] {'wide'}, dimensions={0} | all-to-all | bytes 18874368 | tf_op jit(solution)/shard_map/all_to_all | solution.py:66
  244.8 0.0 copy-start.1
  244.8 3.6 %copy-done.1 = bf16[64,144,512]{2,1,0:T(8,128)(2,1)} copy-done((bf16[64,144,512]{2,1,0:T(8,128)(2,1)}, bf16[64,144,512]{2,1,0:T(8,128)(2,1)S(1)}, u32[]{:S(2)}) %copy-start.1) | copy-done | bytes 9437208
  248.5 0.2 add_reduce_fusion
  248.6 3.4 %psum.15 = f32[8,512]{1,0:T(8,128)S(1)} all-reduce(f32[8,512]{1,0:T(8,128)S(1)} %add_reduce_fusion), channel_id=1, replica_groups=mesh['wide'=64,'narrow'=2] {'narrow'}, use_global_device_ids=true, to_apply=%region_5.6 | all-reduce | flops 4096 | bytes 32768 | tf_op jit(solution)/shard_map/psum | solution.py:72
  252.0 1.1 broadcast_in_dim.2
  253.1 8.8 %all-to-all-start.2 = ((f32[64,8,512]{2,1,0:T(8,128)}), f32[64,8,512]{2,1,0:T(8,128)}, u32[]{:S(2)}, u32[]{:S(2)}) async-start(f32[64,8,512]{2,1,0:T(8,128)} %broadcast_in_dim.2), calls=%async_computation.2 | async-start | bytes 2097152 | tf_op jit(solution)/shard_map/all_to_all | solution.py:73
  261.9 0.0 copy-start.3
  261.9 4.8 %convert_reduce_fusion = f32[128,512]{1,0:T(8,128)S(1)} fusion(bf16[64,144,512]{2,1,0:T(8,128)(2,1)} %copy-done.1), kind=kLoop, calls=%fused_computation | loop fusion | flops 8323072 | bytes 8650752 | tf_op jit(solution)/shard_map/reduce_sum | solution.py:76
  266.7 0.0 copy-done.3
  266.8 1.0 convolution_convert_fusion.1
  267.7 13.1 %all-to-all-done.2 = f32[64,8,512]{2,1,0:T(8,128)} async-done(((f32[64,8,512]{2,1,0:T(8,128)}), f32[64,8,512]{2,1,0:T(8,128)}, u32[]{:S(2)}, u32[]{:S(2)}) %all-to-all-start.2) | async-done | bytes 1048608 | tf_op jit(solution)/shard_map/all_to_all | solution.py:73
  280.8 2.3 copy.25
  (2 shorter events, 0.0 us)
Async XLA Ops:
  7.2 1.9 copy-start
  7.2 84.6 %all-gather.2.cloned.1.call-start = ((), (), s32[]{:S(2)}) async-start(), calls=%async_computation.3 | async-start | bytes 8519680 | tf_op jit(solution)/shard_map/all_gather | solution.py:16
  9.1 9.4 %copy-start.6 = (bf16[128,512]{1,0:T(8,128)(2,1)S(1)}, bf16[128,512]{1,0:T(8,128)(2,1)}, u32[]{:S(2)}) copy-start(bf16[128,512]{1,0:T(8,128)(2,1)} %param.6) | copy-start | bytes 393220
  91.8 9.1 %copy-start.2 = (bf16[512,512]{1,0:T(8,128)(2,1)S(1)}, bf16[512,512]{1,0:T(8,128)(2,1)}, u32[]{:S(2)}) copy-start(bf16[512,512]{1,0:T(8,128)(2,1)} %param.7) | copy-start | bytes 1572868
  91.8 9.1 %copy-start.5 = (f32[256,512]{1,0:T(8,128)S(1)}, f32[256,512]{1,0:T(8,128)}, u32[]{:S(2)}) copy-start(f32[256,512]{1,0:T(8,128)} %bitcast_multiply_fusion) | copy-start | bytes 1572868
  91.8 16.6 %copy-start.7 = (bf16[128,512]{1,0:T(8,128)(2,1)S(1)}, bf16[128,512]{1,0:T(8,128)(2,1)}, u32[]{:S(2)}) copy-start(bf16[128,512]{1,0:T(8,128)(2,1)} %param.11) | copy-start | bytes 393220
  100.9 0.8 copy-start.4
  244.8 3.6 %copy-start.1 = (bf16[64,144,512]{2,1,0:T(8,128)(2,1)}, bf16[64,144,512]{2,1,0:T(8,128)(2,1)S(1)}, u32[]{:S(2)}) copy-start(bf16[64,144,512]{2,1,0:T(8,128)(2,1)S(1)} %all_to_all.16) | copy-start | bytes 28311556
  253.1 27.7 %all-to-all-start.2 = ((f32[64,8,512]{2,1,0:T(8,128)}), f32[64,8,512]{2,1,0:T(8,128)}, u32[]{:S(2)}, u32[]{:S(2)}) async-start(f32[64,8,512]{2,1,0:T(8,128)} %broadcast_in_dim.2), calls=%async_computation.2 | async-start | bytes 2097152 | tf_op jit(solution)/shard_map/all_to_all | solution.py:73
  261.9 4.9 %copy-start.3 = (bf16[512,512]{1,0:T(8,128)(2,1)S(1)}, bf16[512,512]{1,0:T(8,128)(2,1)}, u32[]{:S(2)}) copy-start(bf16[512,512]{1,0:T(8,128)(2,1)} %param.7) | copy-start | bytes 1572868
Sparse Core Ops, SparseCore 0:
  10.9 80.8 all-gather.1

commit v5 on v4

--- a/solution.py
+++ b/solution.py
@@ -52,28 +52,9 @@
     ) + lax.dot_general(
         features, own_grad, (((0,), (0,)), ((), ())), preferred_element_type=jnp.float32
     )
-    rows = width // owners
-    high = weight_terms.astype(jnp.bfloat16)
-    low = (weight_terms - high.astype(jnp.float32)).astype(jnp.bfloat16)
-    payload = jnp.concatenate(
-        [
-            terms.reshape(owners, tile, width),
-            high.reshape(owners, rows, width),
-            low.reshape(owners, rows, width),
-        ],
-        axis=1,
-    )
-    received = lax.all_to_all(payload, "wide", 0, 0, tiled=True)
-    band = jnp.sum(
-        received[:, tile:tile + rows].astype(jnp.float32)
-        + received[:, tile + rows:].astype(jnp.float32),
-        axis=0,
-    )
-    band = lax.psum(band, "narrow")
-    grad_weight = lax.all_to_all(
-        jnp.broadcast_to(band[None], (owners, rows, width)), "wide", 0, 0, tiled=True
-    ).reshape(width, width)
-    gathered_sum = jnp.sum(received[:, :tile].astype(jnp.float32), axis=0)
+    grad_weight = lax.psum(weight_terms, ("wide", "narrow"))
+    received = lax.all_to_all(terms.reshape(owners, tile, width), "wide", 0, 0, tiled=True)
+    gathered_sum = jnp.sum(received.astype(jnp.float32), axis=0)
     message = (gathered_sum + own_grad.astype(jnp.float32)).astype(jnp.bfloat16)
     grad_features = lax.dot_general(
         message, weight, (((1,), (1,)), ((), ())), preferred_element_type=jnp.float32

time: 290 us -> 383 us (1.32)
  waiting for transfers between devices: 84.8 us -> 298 us
  blocking collectives: 131 us -> 9.5 us
  local copies, waits for them, and re-layouts: 7.58 us -> 2.85 us
  matrix products: 31.4 us -> 35.7 us
    all_to_all x1 -> x0, blocking collectives: 118 us -> none  [per_device(): received = lax.all_to_all(payload, 'wide', 0, 0, tiled=True)]
    psum x0 -> x1, waiting for transfers between devices: none -> 115 us  [per_device(): grad_weight = lax.psum(weight_terms, ('wide', 'narrow'))]
    all_to_all x1, waiting for transfers between devices: 13.1 us -> 111 us  [per_device(): lax.all_to_all(terms.reshape(owners, tile, width), 'wide', 0, 0, tiled=True)]
  transfers between devices with their start and end apart: 2 -> 3, of which waited for: 2 -> 3; matrix products, arithmetic and copies ran while one was open for 5% -> 5% of each run, Pallas kernels for 0% -> 0%
where the time goes in v5:
time: 383 us; the launch traced here: 381 us
  waiting for transfers between devices  298 us (78%)
  matrix products  35.7 us (9%)
  between operations  14.1 us (4%)
  other arithmetic  11.4 us (3%)
  blocking collectives  9.5 us (2%)
  starting transfers between devices  9.17 us (2%)
    psum x1, waiting for transfers between devices, per_device(): grad_weight = lax.psum(weight_terms, ('wide', 'narrow'))  115 us
    all_to_all x1, waiting for transfers between devices, per_device(): lax.all_to_all(terms.reshape(owners, tile, width), 'wide', 0, 0, tiled=True)  111 us
    all_gather x1, waiting for transfers between devices, per_device(): gathered_features = lax.all_gather(features, 'wide', axis=0, tiled=True)  71.2 us
    dot_general x1, matrix products, per_device(): lax.dot_general(panel, all_grad, (((0,), (0,)), ((), ())), preferred_elem...  15 us
    dot_general x1, matrix products, per_device(): jnp.dot(panel, gathered_features, preferred_element_type=jnp.float32)  9.13 us
    all_to_all x1, starting transfers between devices, per_device(): lax.all_to_all(terms.reshape(owners, tile, width), 'wide', 0, 0, tiled=True)  8.86 us
  transfers between devices with their start and end apart: 3, of which 3 were waited for; matrix products, arithmetic and copies ran while one was open for 5% of the time, Pallas kernels for 0%

profile of v5, /device:TPU:0, one launch (start us, length us, event | category | flops | bytes accessed | tf_op | source)
XLA Modules:
  0.0 380.6 jit_solution(8335297586047689732)
XLA Ops:
  7.2 0.0 copy-start
  7.2 0.0 all-gather.2.cloned.1.call-start
  7.2 0.7 all-gather.2.cloned.1.call-update
  7.9 0.9 compare_convert_fusion.1
  8.8 0.2 copy-done
  9.1 5.7 %bitcast_convert_fusion = (bf16[2,128,64,128]{3,2,1,0:T(8,128)(2,1)}, f32[2,64,128,128]{3,1,2,0:T(8,128)S(1)}) fusion(bf16[2,48,128,128]{3,2,1,0:T(8,128)(2,1)S(1)} %bitcast.42, s32[2,48]{1,0:T(2,128)} %bitcast.47, bf16[2,48]{1,0:T(2,128)(2,1)S(1)} %compare_convert_fusion.1), kind=kOutput, calls=%fused_computation.3 | convolution fusion | flops 203436032 | bytes 15729216 | tf_op jit(solution)/shard_map/skj,sktc->stjc/dot_general | solution.py:21
  14.7 0.0 copy-start.5
  14.7 1.1 bitcast_reduce_fusion
  15.8 2.5 psum.14
  18.3 0.1 dynamic_slice.3
  18.4 0.1 broadcast_bitcast_fusion
  18.4 0.0 copy-done.5
  18.4 1.3 fusion.8
  19.7 0.9 bitcast_multiply_fusion
  20.6 71.2 %all-gather.2.cloned.1.call-done = bf16[8192,512]{1,0:T(8,128)(2,1)} async-done(((bf16[128,512]{1,0:T(8,128)(2,1)}), bf16[8192,512]{1,0:T(8,128)(2,1)}) %all-gather.2.cloned.1.call-update) | async-done | bytes 8388624 | tf_op jit(solution)/shard_map/all_gather | solution.py:16
  91.8 0.0 copy-start.1
  91.8 0.0 copy-start.4
  91.8 0.0 copy-start.7
  91.8 9.1 %fusion.1 = f32[256,512]{1,0:T(8,128)S(1)} fusion(bf16[8192,512]{1,0:T(8,128)(2,1)} %all-gather.2.cloned.1.call-done, bf16[32,8,64,128]{3,2,1,0:T(8,128)(2,1)} %bitcast.44), kind=kOutput, calls=%fused_computation.5 | convolution fusion | flops 2147483648 | bytes 13107200 | tf_op jit(solution)/shard_map/dot_general | solution.py:29
  100.9 0.0 copy-done.1
  100.9 0.0 copy-done.4
  100.9 0.0 copy-start.3
  100.9 0.6 convolution_add_fusion
  101.5 0.2 copy-done.3
  101.7 4.9 %all_to_all.10 = f32[2,128,512]{2,1,0:T(8,128)} all-to-all(f32[2,128,512]{2,1,0:T(8,128)S(1)} %bitcast.46), channel_id=1, replica_groups=mesh['wide'=64,'narrow'=2] {'narrow'}, dimensions={0} | all-to-all | bytes 1048576 | tf_op jit(solution)/shard_map/all_to_all | solution.py:38
  106.6 1.8 reduce_sum.29
  108.4 0.0 copy-done.7
  108.4 1.8 multiply_convert_fusion
  110.2 2.2 all_gather.7
  112.4 0.0 copy-start.6
  112.4 15.0 %convolution_convert_fusion = bf16[8192,512]{1,0:T(8,128)(2,1)} fusion(bf16[256,512]{1,0:T(8,128)(2,1)S(1)} %all_gather.7, bf16[32,8,64,128]{3,2,1,0:T(8,128)(2,1)} %bitcast.45), kind=kOutput, calls=%fused_computation.1 | convolution fusion | flops 2151677952 | bytes 12845056 | tf_op jit(solution)/shard_map/dot_general | solution.py:46
  127.4 0.0 copy-done.6
  127.4 8.9 %all-to-all-start.1 = ((bf16[64,128,512]{2,1,0:T(8,128)(2,1)}), bf16[64,128,512]{2,1,0:T(8,128)(2,1)}, u32[]{:S(2)}, u32[]{:S(2)}) async-start(bf16[64,128,512]{2,1,0:T(8,128)(2,1)} %bitcast.43), calls=%async_computation.1 | async-start | bytes 16777216 | tf_op jit(solution)/shard_map/all_to_all | solution.py:56
  136.2 0.3 all-reduce.2.cloned.1.call-start
  136.5 1.7 fusion.16
  138.3 1.3 fusion.7
  139.6 0.0 all-reduce.2.cloned.1.call-update
  139.6 110.6 %all-to-all-done.1 = bf16[64,128,512]{2,1,0:T(8,128)(2,1)} async-done(((bf16[64,128,512]{2,1,0:T(8,128)(2,1)}), bf16[64,128,512]{2,1,0:T(8,128)(2,1)}, u32[]{:S(2)}, u32[]{:S(2)}) %all-to-all-start.1) | async-done | bytes 8388640 | tf_op jit(solution)/shard_map/all_to_all | solution.py:56
  250.2 0.0 copy-start.2
  250.2 4.8 %convert_reduce_fusion = f32[128,512]{1,0:T(8,128)S(1)} fusion(bf16[64,128,512]{2,1,0:T(8,128)(2,1)} %all-to-all-done.1), kind=kLoop, calls=%fused_computation | loop fusion | flops 8323072 | bytes 8650752 | tf_op jit(solution)/shard_map/reduce_sum | solution.py:57
  255.0 0.0 copy-done.2
  255.0 1.0 convolution_convert_fusion.1
  256.0 115.5 %all-reduce.2.cloned.1.call-done = f32[512,512]{1,0:T(8,128)} async-done(((f32[512,512]{1,0:T(8,128)}), f32[512,512]{1,0:T(8,128)}) %all-reduce.2.cloned.1.call-update) | async-done | bytes 1048592 | tf_op jit(solution)/shard_map/psum | solution.py:55
  371.5 2.3 copy.27
  (2 shorter events, 0.0 us)
Async XLA Ops:
  7.2 1.9 copy-start
  7.2 84.6 %all-gather.2.cloned.1.call-start = ((), (), s32[]{:S(2)}) async-start(), calls=%async_computation.2 | async-start | bytes 8519680 | tf_op jit(solution)/shard_map/all_gather | solution.py:16
  14.7 3.7 copy-start.5
  91.8 9.1 %copy-start.1 = (bf16[512,512]{1,0:T(8,128)(2,1)S(1)}, bf16[512,512]{1,0:T(8,128)(2,1)}, u32[]{:S(2)}) copy-start(bf16[512,512]{1,0:T(8,128)(2,1)} %param.7) | copy-start | bytes 1572868
  91.8 9.1 %copy-start.4 = (f32[256,512]{1,0:T(8,128)S(1)}, f32[256,512]{1,0:T(8,128)}, u32[]{:S(2)}) copy-start(f32[256,512]{1,0:T(8,128)} %bitcast_multiply_fusion) | copy-start | bytes 1572868
  91.8 16.6 %copy-start.7 = (bf16[128,512]{1,0:T(8,128)(2,1)S(1)}, bf16[128,512]{1,0:T(8,128)(2,1)}, u32[]{:S(2)}) copy-start(bf16[128,512]{1,0:T(8,128)(2,1)} %param.11) | copy-start | bytes 393220
  100.9 0.8 copy-start.3
  112.4 15.0 %copy-start.6 = (bf16[256,512]{1,0:T(8,128)(2,1)}, bf16[256,512]{1,0:T(8,128)(2,1)S(1)}, u32[]{:S(2)}) copy-start(bf16[256,512]{1,0:T(8,128)(2,1)S(1)} %all_gather.7) | copy-start | bytes 786436
  127.4 122.8 %all-to-all-start.1 = ((bf16[64,128,512]{2,1,0:T(8,128)(2,1)}), bf16[64,128,512]{2,1,0:T(8,128)(2,1)}, u32[]{:S(2)}, u32[]{:S(2)}) async-start(bf16[64,128,512]{2,1,0:T(8,128)(2,1)} %bitcast.43), calls=%async_computation.1 | async-start | bytes 16777216 | tf_op jit(solution)/shard_map/all_to_all | solution.py:56
  136.2 235.2 %all-reduce.2.cloned.1.call-start = ((), (), s32[]{:S(2)}) async-start(), calls=%async_computation.3 | async-start | bytes 2097152 | tf_op jit(solution)/shard_map/psum | solution.py:55
  250.2 4.9 %copy-start.2 = (bf16[512,512]{1,0:T(8,128)(2,1)S(1)}, bf16[512,512]{1,0:T(8,128)(2,1)}, u32[]{:S(2)}) copy-start(bf16[512,512]{1,0:T(8,128)(2,1)} %param.7) | copy-start | bytes 1572868
Sparse Core Ops, SparseCore 0:
  10.9 80.8 all-gather.1
  142.4 228.9 all-reduce.1

commit v6 on v4

--- a/solution.py
+++ b/solution.py
@@ -24,6 +24,9 @@
     degree = 1.0 + lax.psum(jnp.sum(dense, axis=1), "narrow")
     scale = lax.rsqrt(degree)
     panel = dense.astype(jnp.bfloat16)
+    panel_t = jnp.einsum(
+        "skj,sktc->jcst", onehot, tiles, preferred_element_type=jnp.float32
+    ).reshape(owners * tile, copies * tile).astype(jnp.bfloat16)
     projected = jnp.dot(features, weight, preferred_element_type=jnp.float32).astype(jnp.bfloat16)
     own = lax.axis_index("narrow")
     aggregated = jnp.dot(panel, gathered_features, preferred_element_type=jnp.float32)
@@ -43,9 +46,7 @@
         cotangent.astype(jnp.float32) * sig * (1.0 + preact * (1.0 - sig)) * own_scale
     ).astype(jnp.bfloat16)
     all_grad = lax.all_gather(own_grad, "narrow", axis=0, tiled=True)
-    terms = lax.dot_general(
-        panel, all_grad, (((0,), (0,)), ((), ())), preferred_element_type=jnp.float32
-    ).astype(jnp.bfloat16)
+    terms = jnp.dot(panel_t, all_grad, preferred_element_type=jnp.float32).astype(jnp.bfloat16)
     weight_terms = lax.dot_general(
         aggregated, all_grad.astype(jnp.float32), (((0,), (0,)), ((), ())),
         precision=lax.Precision.HIGHEST, preferred_element_type=jnp.float32,

time: 290 us -> 291 us (level)
  transfers between devices with their start and end apart: 2 -> 2, of which waited for: 2 -> 2; matrix products, arithmetic and copies ran while one was open for 5% -> 6% of each run, Pallas kernels for 0% -> 0%
where the time goes in v6:
time: 291 us; the launch traced here: 290 us
  blocking collectives  131 us (45%)
  waiting for transfers between devices  82.9 us (28%)
  matrix products  33.3 us (11%)
  between operations  14.1 us (5%)
  other arithmetic  12.3 us (4%)
  starting transfers between devices  8.84 us (3%)
  local copies, waits for them, and re-layouts  7.58 us (3%)
    all_to_all x1, blocking collectives, per_device(): received = lax.all_to_all(payload, 'wide', 0, 0, tiled=True)  118 us
    all_gather x1, waiting for transfers between devices, per_device(): gathered_features = lax.all_gather(features, 'wide', axis=0, tiled=True)  69.2 us
    all_to_all x1, waiting for transfers between devices, per_device(): lax.all_to_all(jnp.broadcast_to(band[None], (owners, rows, width)), 'wide...  13.1 us
    dot_general x1, matrix products, per_device(): jnp.dot(panel_t, all_grad, preferred_element_type=jnp.float32)  11.7 us
    dot_general x1, matrix products, per_device(): jnp.dot(panel, gathered_features, preferred_element_type=jnp.float32)  9.13 us
    all_to_all x1, starting transfers between devices, per_device(): lax.all_to_all(jnp.broadcast_to(band[None], (owners, rows, width)), 'wide...  8.8 us
    dot_general x1, matrix products, per_device(): jnp.einsum('skj,sktc->stjc', onehot, tiles, preferred_element_type=jnp.fl...  7.68 us
    unnamed x17, local copies, waits for them, and re-layouts  6.33 us
  transfers between devices with their start and end apart: 2, of which 2 were waited for; matrix products, arithmetic and copies ran while one was open for 6% of the time, Pallas kernels for 0%

profile of v6, /device:TPU:0, one launch (start us, length us, event | category | flops | bytes accessed | tf_op | source)
XLA Modules:
  0.0 289.9 jit_solution(16275249894346230457)
XLA Ops:
  7.2 0.0 copy-start
  7.2 0.0 all-gather.2.cloned.1.call-start
  7.2 0.7 all-gather.2.cloned.1.call-update
  7.9 0.9 compare_convert_fusion.1
  8.8 0.2 copy-done
  9.1 7.7 %fusion.17 = (bf16[2,64,128,128]{3,1,2,0:T(8,128)(2,1)}, bf16[2,128,64,128]{3,2,1,0:T(8,128)(2,1)}, f32[2,64,128,128]{3,1,2,0:T(8,128)S(1)}) fusion(bf16[2,48,128,128]{3,2,1,0:T(8,128)(2,1)S(1)} %bitcast.55, s32[2,48]{1,0:T(2,128)} %bitcast.61, bf16[2,48]{1,0:T(2,128)(2,1)S(1)} %compare_convert_fusion.1), kind=kOutput, calls=%fused_computation.38 | convolution fusion | flops 205533184 | bytes 19923520 | tf_op jit(solution)/shard_map/skj,sktc->stjc/dot_general | solution.py:21
  16.7 0.0 copy-start.6
  16.7 1.1 bitcast_reduce_fusion
  17.8 2.5 psum.14
  20.3 0.1 dynamic_slice.3
  20.4 0.1 broadcast_bitcast_fusion
  20.5 0.0 copy-done.6
  20.5 1.3 fusion.8
  21.7 0.9 bitcast_multiply_fusion
  22.6 69.2 %all-gather.2.cloned.1.call-done = bf16[8192,512]{1,0:T(8,128)(2,1)} async-done(((bf16[128,512]{1,0:T(8,128)(2,1)}), bf16[8192,512]{1,0:T(8,128)(2,1)}) %all-gather.2.cloned.1.call-update) | async-done | bytes 8388624 | tf_op jit(solution)/shard_map/all_gather | solution.py:16
  91.8 0.0 copy-start.2
  91.8 0.0 copy-start.5
  91.8 0.0 copy-start.7
  91.8 9.1 %fusion.2 = f32[256,512]{1,0:T(8,128)S(1)} fusion(bf16[8192,512]{1,0:T(8,128)(2,1)} %all-gather.2.cloned.1.call-done, bf16[32,8,64,128]{3,2,1,0:T(8,128)(2,1)} %bitcast.58), kind=kOutput, calls=%fused_computation.7 | convolution fusion | flops 2147483648 | bytes 13107200 | tf_op jit(solution)/shard_map/dot_general | solution.py:32
  100.9 0.0 copy-done.2
  100.9 0.0 copy-done.5
  101.0 0.0 copy-start.4
  101.0 0.6 convolution_add_fusion
  101.6 0.2 copy-done.4
  101.7 4.9 %all_to_all.15 = f32[2,128,512]{2,1,0:T(8,128)} all-to-all(f32[2,128,512]{2,1,0:T(8,128)S(1)} %bitcast.59), channel_id=1, replica_groups=mesh['wide'=64,'narrow'=2] {'narrow'}, dimensions={0} | all-to-all | bytes 1048576 | tf_op jit(solution)/shard_map/all_to_all | solution.py:41
  106.6 1.8 reduce_sum.38
  108.4 0.0 copy-done.7
  108.4 1.8 multiply_convert_fusion
  110.2 2.2 all_gather.7
  112.4 1.7 fusion.18
  114.1 0.3 convert_bitcast_fusion
  114.4 11.7 %convolution_convert_fusion = bf16[8192,512]{1,0:T(8,128)(2,1)S(1)} fusion(bf16[256,512]{1,0:T(8,128)(2,1)S(1)} %all_gather.7, bf16[32,8,64,128]{3,2,1,0:T(8,128)(2,1)} %bitcast.57), kind=kOutput, calls=%fused_computation.1 | convolution fusion | flops 2151677952 | bytes 12845056 | tf_op jit(solution)/shard_map/dot_general | solution.py:49
  126.1 0.7 pad_maximum_fusion
  126.9 118.0 %all_to_all.16 = bf16[64,144,512]{2,1,0:T(8,128)(2,1)S(1)} all-to-all(bf16[64,144,512]{2,1,0:T(8,128)(2,1)S(1)} %pad_maximum_fusion), channel_id=1, replica_groups=mesh['wide'=64,'narrow'=2] {'wide'}, dimensions={0} | all-to-all | bytes 18874368 | tf_op jit(solution)/shard_map/all_to_all | solution.py:67
  244.9 0.0 copy-start.1
  244.9 3.6 %copy-done.1 = bf16[64,144,512]{2,1,0:T(8,128)(2,1)} copy-done((bf16[64,144,512]{2,1,0:T(8,128)(2,1)}, bf16[64,144,512]{2,1,0:T(8,128)(2,1)S(1)}, u32[]{:S(2)}) %copy-start.1) | copy-done | bytes 9437208
  248.5 0.2 add_reduce_fusion
  248.7 3.4 %psum.15 = f32[8,512]{1,0:T(8,128)S(1)} all-reduce(f32[8,512]{1,0:T(8,128)S(1)} %add_reduce_fusion), channel_id=1, replica_groups=mesh['wide'=64,'narrow'=2] {'narrow'}, use_global_device_ids=true, to_apply=%region_5.6 | all-reduce | flops 4096 | bytes 32768 | tf_op jit(solution)/shard_map/psum | solution.py:73
  252.0 1.1 broadcast_in_dim.2
  253.1 8.8 %all-to-all-start.2 = ((f32[64,8,512]{2,1,0:T(8,128)}), f32[64,8,512]{2,1,0:T(8,128)}, u32[]{:S(2)}, u32[]{:S(2)}) async-start(f32[64,8,512]{2,1,0:T(8,128)} %broadcast_in_dim.2), calls=%async_computation.2 | async-start | bytes 2097152 | tf_op jit(solution)/shard_map/all_to_all | solution.py:74
  261.9 0.0 copy-start.3
  261.9 4.8 %convert_reduce_fusion = f32[128,512]{1,0:T(8,128)S(1)} fusion(bf16[64,144,512]{2,1,0:T(8,128)(2,1)} %copy-done.1), kind=kLoop, calls=%fused_computation | loop fusion | flops 8323072 | bytes 8650752 | tf_op jit(solution)/shard_map/reduce_sum | solution.py:77
  266.8 0.0 copy-done.3
  266.8 1.0 convolution_convert_fusion.1
  267.8 13.1 %all-to-all-done.2 = f32[64,8,512]{2,1,0:T(8,128)} async-done(((f32[64,8,512]{2,1,0:T(8,128)}), f32[64,8,512]{2,1,0:T(8,128)}, u32[]{:S(2)}, u32[]{:S(2)}) %all-to-all-start.2) | async-done | bytes 1048608 | tf_op jit(solution)/shard_map/all_to_all | solution.py:74
  280.8 2.3 copy.26
  (2 shorter events, 0.0 us)
Async XLA Ops:
  7.2 1.9 copy-start
  7.2 84.6 %all-gather.2.cloned.1.call-start = ((), (), s32[]{:S(2)}) async-start(), calls=%async_computation.3 | async-start | bytes 8519680 | tf_op jit(solution)/shard_map/all_gather | solution.py:16
  16.7 3.7 %copy-start.6 = (bf16[128,512]{1,0:T(8,128)(2,1)S(1)}, bf16[128,512]{1,0:T(8,128)(2,1)}, u32[]{:S(2)}) copy-start(bf16[128,512]{1,0:T(8,128)(2,1)} %param.6) | copy-start | bytes 393220
  91.8 9.1 %copy-start.2 = (bf16[512,512]{1,0:T(8,128)(2,1)S(1)}, bf16[512,512]{1,0:T(8,128)(2,1)}, u32[]{:S(2)}) copy-start(bf16[512,512]{1,0:T(8,128)(2,1)} %param.7) | copy-start | bytes 1572868
  91.8 9.1 %copy-start.5 = (f32[256,512]{1,0:T(8,128)S(1)}, f32[256,512]{1,0:T(8,128)}, u32[]{:S(2)}) copy-start(f32[256,512]{1,0:T(8,128)} %bitcast_multiply_fusion) | copy-start | bytes 1572868
  91.8 16.6 %copy-start.7 = (bf16[128,512]{1,0:T(8,128)(2,1)S(1)}, bf16[128,512]{1,0:T(8,128)(2,1)}, u32[]{:S(2)}) copy-start(bf16[128,512]{1,0:T(8,128)(2,1)} %param.11) | copy-start | bytes 393220
  101.0 0.8 copy-start.4
  244.9 3.6 %copy-start.1 = (bf16[64,144,512]{2,1,0:T(8,128)(2,1)}, bf16[64,144,512]{2,1,0:T(8,128)(2,1)S(1)}, u32[]{:S(2)}) copy-start(bf16[64,144,512]{2,1,0:T(8,128)(2,1)S(1)} %all_to_all.16) | copy-start | bytes 28311556
  253.1 27.7 %all-to-all-start.2 = ((f32[64,8,512]{2,1,0:T(8,128)}), f32[64,8,512]{2,1,0:T(8,128)}, u32[]{:S(2)}, u32[]{:S(2)}) async-start(f32[64,8,512]{2,1,0:T(8,128)} %broadcast_in_dim.2), calls=%async_computation.2 | async-start | bytes 2097152 | tf_op jit(solution)/shard_map/all_to_all | solution.py:74
  261.9 4.9 %copy-start.3 = (bf16[512,512]{1,0:T(8,128)(2,1)S(1)}, bf16[512,512]{1,0:T(8,128)(2,1)}, u32[]{:S(2)}) copy-start(bf16[512,512]{1,0:T(8,128)(2,1)} %param.7) | copy-start | bytes 1572868
Sparse Core Ops, SparseCore 0:
  10.9 80.8 all-gather.1

commit v7 on v6

--- a/solution.py
+++ b/solution.py
@@ -56,25 +56,19 @@
     rows = width // owners
     high = weight_terms.astype(jnp.bfloat16)
     low = (weight_terms - high.astype(jnp.float32)).astype(jnp.bfloat16)
-    payload = jnp.concatenate(
-        [
-            terms.reshape(owners, tile, width),
-            high.reshape(owners, rows, width),
-            low.reshape(owners, rows, width),
-        ],
-        axis=1,
+    shares = jnp.concatenate(
+        [high.reshape(owners, rows, width), low.reshape(owners, rows, width)], axis=1
     )
-    received = lax.all_to_all(payload, "wide", 0, 0, tiled=True)
+    shares = lax.all_to_all(shares, "wide", 0, 0, tiled=True)
     band = jnp.sum(
-        received[:, tile:tile + rows].astype(jnp.float32)
-        + received[:, tile + rows:].astype(jnp.float32),
-        axis=0,
+        shares[:, :rows].astype(jnp.float32) + shares[:, rows:].astype(jnp.float32), axis=0
     )
     band = lax.psum(band, "narrow")
     grad_weight = lax.all_to_all(
         jnp.broadcast_to(band[None], (owners, rows, width)), "wide", 0, 0, tiled=True
     ).reshape(width, width)
-    gathered_sum = jnp.sum(received[:, :tile].astype(jnp.float32), axis=0)
+    received = lax.all_to_all(terms.reshape(owners, tile, width), "wide", 0, 0, tiled=True)
+    gathered_sum = jnp.sum(received.astype(jnp.float32), axis=0)
     message = (gathered_sum + own_grad.astype(jnp.float32)).astype(jnp.bfloat16)
     grad_features = lax.dot_general(
         message, weight, (((1,), (1,)), ((), ())), preferred_element_type=jnp.float32

time: 291 us -> 319 us (1.096)
  the two profiles are of different devices: /device:TPU:0 before, /device:TPU:18 now
where the time goes in v7:
time: 319 us; the launch traced here: 318 us
  waiting for transfers between devices  196 us (61%)
  blocking collectives  38.1 us (12%)
  matrix products  36.6 us (11%)
  starting transfers between devices  16.5 us (5%)
  between operations  14.1 us (4%)
  other arithmetic  11.6 us (4%)
  local copies, waits for them, and re-layouts  5.37 us (2%)
    all_to_all x1, waiting for transfers between devices, per_device(): lax.all_to_all(terms.reshape(owners, tile, width), 'wide', 0, 0, tiled=True)  124 us
    all_gather x1, waiting for transfers between devices, per_device(): gathered_features = lax.all_gather(features, 'wide', axis=0, tiled=True)  68.9 us
    all_to_all x1, blocking collectives, per_device(): shares = lax.all_to_all(shares, 'wide', 0, 0, tiled=True)  24.9 us
    dot_general x1, matrix products, per_device(): jnp.dot(panel_t, all_grad, preferred_element_type=jnp.float32)  14.9 us
    dot_general x1, matrix products, per_device(): jnp.dot(panel, gathered_features, preferred_element_type=jnp.float32)  9.13 us
    all_to_all x1, starting transfers between devices, per_device(): lax.all_to_all(terms.reshape(owners, tile, width), 'wide', 0, 0, tiled=True)  8.63 us
    all_to_all x1, starting transfers between devices, per_device(): lax.all_to_all(jnp.broadcast_to(band[None], (owners, rows, width)), 'wide...  7.86 us
    dot_general x1, matrix products, per_device(): jnp.einsum('skj,sktc->stjc', onehot, tiles, preferred_element_type=jnp.fl...  7.68 us
  transfers between devices with their start and end apart: 3, of which 3 were waited for; matrix products, arithmetic and copies ran while one was open for 8% of the time, Pallas kernels for 0%

profile of v7, /device:TPU:18, one launch (start us, length us, event | category | flops | bytes accessed | tf_op | source)
XLA Modules:
  0.0 318.0 jit_solution(8297396926433678744)
XLA Ops:
  7.2 0.0 copy-start
  7.2 0.0 all-gather.2.cloned.1.call-start
  7.2 0.7 all-gather.2.cloned.1.call-update
  7.9 0.9 compare_convert_fusion.1
  8.8 0.2 copy-done
  9.1 7.7 %fusion.17 = (bf16[2,64,128,128]{3,1,2,0:T(8,128)(2,1)}, bf16[2,128,64,128]{3,2,1,0:T(8,128)(2,1)}, f32[2,64,128,128]{3,1,2,0:T(8,128)S(1)}) fusion(bf16[2,48,128,128]{3,2,1,0:T(8,128)(2,1)S(1)} %bitcast.55, s32[2,48]{1,0:T(2,128)} %bitcast.61, bf16[2,48]{1,0:T(2,128)(2,1)S(1)} %compare_convert_fusion.1), kind=kOutput, calls=%fused_computation.38 | convolution fusion | flops 205533184 | bytes 19923520 | tf_op jit(solution)/shard_map/skj,sktc->stjc/dot_general | solution.py:21
  16.7 0.0 copy-start.5
  16.7 1.1 bitcast_reduce_fusion
  17.8 2.5 psum.14
  20.3 0.1 dynamic_slice.3
  20.4 0.1 broadcast_bitcast_fusion
  20.5 0.0 copy-done.5
  20.5 1.3 fusion.8
  21.7 0.9 bitcast_multiply_fusion
  22.6 68.9 %all-gather.2.cloned.1.call-done = bf16[8192,512]{1,0:T(8,128)(2,1)} async-done(((bf16[128,512]{1,0:T(8,128)(2,1)}), bf16[8192,512]{1,0:T(8,128)(2,1)}) %all-gather.2.cloned.1.call-update) | async-done | bytes 8388624 | tf_op jit(solution)/shard_map/all_gather | solution.py:16
  91.5 0.0 copy-start.1
  91.5 0.0 copy-start.4
  91.5 0.0 copy-start.8
  91.5 9.1 %fusion.2 = f32[256,512]{1,0:T(8,128)S(1)} fusion(bf16[8192,512]{1,0:T(8,128)(2,1)} %all-gather.2.cloned.1.call-done, bf16[32,8,64,128]{3,2,1,0:T(8,128)(2,1)} %bitcast.58), kind=kOutput, calls=%fused_computation.6 | convolution fusion | flops 2147483648 | bytes 13107200 | tf_op jit(solution)/shard_map/dot_general | solution.py:32
  100.6 0.0 copy-done.1
  100.6 0.0 copy-done.4
  100.6 0.0 copy-start.3
  100.7 0.6 convolution_add_fusion
  101.3 0.2 copy-done.3
  101.4 4.9 %all_to_all.20 = f32[2,128,512]{2,1,0:T(8,128)} all-to-all(f32[2,128,512]{2,1,0:T(8,128)S(1)} %bitcast.59), channel_id=1, replica_groups=mesh['wide'=64,'narrow'=2] {'narrow'}, dimensions={0} | all-to-all | bytes 1048576 | tf_op jit(solution)/shard_map/all_to_all | solution.py:41
  106.3 1.8 reduce_sum.38
  108.1 0.0 copy-done.8
  108.1 1.8 multiply_convert_fusion
  109.9 2.0 all_gather.7
  111.9 0.7 copy-done.6
  112.6 1.7 fusion.18
  114.3 0.3 convert_bitcast_fusion
  114.6 0.0 copy-start.7
  114.7 0.1 pad_maximum_fusion
  114.8 24.9 %all_to_all.21 = bf16[64,16,512]{2,1,0:T(8,128)(2,1)S(1)} all-to-all(bf16[64,16,512]{2,1,0:T(8,128)(2,1)S(1)} %pad_maximum_fusion), channel_id=1, replica_groups=mesh['wide'=64,'narrow'=2] {'wide'}, dimensions={0} | all-to-all | bytes 2097152 | tf_op jit(solution)/shard_map/all_to_all | solution.py:62
  139.7 0.2 add_reduce_fusion
  139.8 4.0 %psum.15 = f32[8,512]{1,0:T(8,128)} all-reduce(f32[8,512]{1,0:T(8,128)S(1)} %add_reduce_fusion), channel_id=1, replica_groups=mesh['wide'=64,'narrow'=2] {'narrow'}, use_global_device_ids=true, to_apply=%region_5.6 | all-reduce | flops 4096 | bytes 32768 | tf_op jit(solution)/shard_map/psum | solution.py:66
  143.8 1.8 broadcast_in_dim.2
  145.6 7.9 %all-to-all-start.3 = ((f32[64,8,512]{2,1,0:T(8,128)}), f32[64,8,512]{2,1,0:T(8,128)}, u32[]{:S(2)}, u32[]{:S(2)}) async-start(f32[64,8,512]{2,1,0:T(8,128)} %broadcast_in_dim.2), calls=%async_computation.3 | async-start | bytes 2097152 | tf_op jit(solution)/shard_map/all_to_all | solution.py:67
  153.5 0.0 copy-done.7
  153.5 14.9 %convolution_convert_fusion = bf16[8192,512]{1,0:T(8,128)(2,1)} fusion(bf16[256,512]{1,0:T(8,128)(2,1)S(1)} %copy-done.7, bf16[32,8,64,128]{3,2,1,0:T(8,128)(2,1)} %bitcast.57), kind=kOutput, calls=%fused_computation.1 | convolution fusion | flops 2151677952 | bytes 12845056 | tf_op jit(solution)/shard_map/dot_general | solution.py:49
  168.4 1.9 all-to-all-done.3
  170.3 8.6 %all-to-all-start.1 = ((bf16[64,128,512]{2,1,0:T(8,128)(2,1)}), bf16[64,128,512]{2,1,0:T(8,128)(2,1)}, u32[]{:S(2)}, u32[]{:S(2)}) async-start(bf16[64,128,512]{2,1,0:T(8,128)(2,1)} %bitcast.56), calls=%async_computation.1 | async-start | bytes 16777216 | tf_op jit(solution)/shard_map/all_to_all | solution.py:70
  178.9 124.1 %all-to-all-done.1 = bf16[64,128,512]{2,1,0:T(8,128)(2,1)} async-done(((bf16[64,128,512]{2,1,0:T(8,128)(2,1)}), bf16[64,128,512]{2,1,0:T(8,128)(2,1)}, u32[]{:S(2)}, u32[]{:S(2)}) %all-to-all-start.1) | async-done | bytes 8388640 | tf_op jit(solution)/shard_map/all_to_all | solution.py:70
  303.0 4.8 %convert_reduce_fusion = f32[128,512]{1,0:T(8,128)S(1)} fusion(bf16[64,128,512]{2,1,0:T(8,128)(2,1)} %all-to-all-done.1), kind=kLoop, calls=%fused_computation | loop fusion | flops 8323072 | bytes 8650752 | tf_op jit(solution)/shard_map/reduce_sum | solution.py:71
  307.9 0.0 copy-done.2
  307.9 1.0 convolution_convert_fusion.1
  308.9 2.3 copy.26
  (4 shorter events, 0.0 us)
Async XLA Ops:
  7.2 1.9 copy-start
  7.2 84.3 %all-gather.2.cloned.1.call-start = ((), (), s32[]{:S(2)}) async-start(), calls=%async_computation.4 | async-start | bytes 8519680 | tf_op jit(solution)/shard_map/all_gather | solution.py:16
  16.7 3.7 %copy-start.5 = (bf16[128,512]{1,0:T(8,128)(2,1)S(1)}, bf16[128,512]{1,0:T(8,128)(2,1)}, u32[]{:S(2)}) copy-start(bf16[128,512]{1,0:T(8,128)(2,1)} %param.6) | copy-start | bytes 393220
  91.5 9.1 %copy-start.1 = (bf16[512,512]{1,0:T(8,128)(2,1)S(1)}, bf16[512,512]{1,0:T(8,128)(2,1)}, u32[]{:S(2)}) copy-start(bf16[512,512]{1,0:T(8,128)(2,1)} %param.7) | copy-start | bytes 1572868
  91.5 9.1 %copy-start.4 = (f32[256,512]{1,0:T(8,128)S(1)}, f32[256,512]{1,0:T(8,128)}, u32[]{:S(2)}) copy-start(f32[256,512]{1,0:T(8,128)} %bitcast_multiply_fusion) | copy-start | bytes 1572868
  91.5 16.6 %copy-start.8 = (bf16[128,512]{1,0:T(8,128)(2,1)S(1)}, bf16[128,512]{1,0:T(8,128)(2,1)}, u32[]{:S(2)}) copy-start(bf16[128,512]{1,0:T(8,128)(2,1)} %param.11) | copy-start | bytes 393220
  100.6 0.8 copy-start.3
  111.9 0.7 copy-start.6
  114.6 38.8 %copy-start.7 = (bf16[256,512]{1,0:T(8,128)(2,1)S(1)}, bf16[256,512]{1,0:T(8,128)(2,1)}, u32[]{:S(2)}) copy-start(bf16[256,512]{1,0:T(8,128)(2,1)} %copy-done.6) | copy-start | bytes 786436
  145.6 24.7 %all-to-all-start.3 = ((f32[64,8,512]{2,1,0:T(8,128)}), f32[64,8,512]{2,1,0:T(8,128)}, u32[]{:S(2)}, u32[]{:S(2)}) async-start(f32[64,8,512]{2,1,0:T(8,128)} %broadcast_in_dim.2), calls=%async_computation.3 | async-start | bytes 2097152 | tf_op jit(solution)/shard_map/all_to_all | solution.py:67
  170.3 132.8 %all-to-all-start.1 = ((bf16[64,128,512]{2,1,0:T(8,128)(2,1)}), bf16[64,128,512]{2,1,0:T(8,128)(2,1)}, u32[]{:S(2)}, u32[]{:S(2)}) async-start(bf16[64,128,512]{2,1,0:T(8,128)(2,1)} %bitcast.56), calls=%async_computation.1 | async-start | bytes 16777216 | tf_op jit(solution)/shard_map/all_to_all | solution.py:70
  303.0 4.8 %copy-start.2 = (bf16[512,512]{1,0:T(8,128)(2,1)S(1)}, bf16[512,512]{1,0:T(8,128)(2,1)}, u32[]{:S(2)}) copy-start(bf16[512,512]{1,0:T(8,128)(2,1)} %param.7) | copy-start | bytes 1572868
Sparse Core Ops, SparseCore 0:
  10.9 80.5 all-gather.1

commit v8 on v4

--- a/solution.py
+++ b/solution.py
@@ -34,15 +34,23 @@
     selector = (jnp.arange(copies, dtype=jnp.int32) == own).astype(jnp.float32)
     self_term = selector[:, None, None] * projected.astype(jnp.float32)[None]
     partial_sum = partial_sum + self_term.reshape(copies * tile, width)
-    own_scale = lax.dynamic_slice_in_dim(scale, own * tile, tile, 0)[:, None]
-    halves = lax.all_to_all(partial_sum.reshape(copies, tile, width), "narrow", 0, 0, tiled=True)
-    preact = jnp.sum(halves, axis=0) * own_scale
+    pair = lax.axis_size("narrow")
+    total = jnp.sum(
+        lax.all_to_all(
+            jnp.broadcast_to(partial_sum[None], (pair,) + partial_sum.shape), "narrow", 0, 0,
+            tiled=True,
+        ),
+        axis=0,
+    )
+    preact_both = total * scale[:, None]
+    sig = jax.nn.sigmoid(preact_both)
+    cot_both = lax.all_gather(cotangent, "narrow", axis=0, tiled=True).astype(jnp.float32)
+    all_grad = (
+        cot_both * sig * (1.0 + preact_both * (1.0 - sig)) * scale[:, None]
+    ).astype(jnp.bfloat16)
+    preact = lax.dynamic_slice_in_dim(preact_both, own * tile, tile, 0)
     activated = jax.nn.silu(preact).astype(jnp.bfloat16)
-    sig = jax.nn.sigmoid(preact)
-    own_grad = (
-        cotangent.astype(jnp.float32) * sig * (1.0 + preact * (1.0 - sig)) * own_scale
-    ).astype(jnp.bfloat16)
-    all_grad = lax.all_gather(own_grad, "narrow", axis=0, tiled=True)
+    own_grad = lax.dynamic_slice_in_dim(all_grad, own * tile, tile, 0)
     terms = lax.dot_general(
         panel, all_grad, (((0,), (0,)), ((), ())), preferred_element_type=jnp.float32
     ).astype(jnp.bfloat16)

time: 290 us -> 291 us (level)
  transfers between devices with their start and end apart: 2 -> 2, of which waited for: 2 -> 2; matrix products, arithmetic and copies ran while one was open for 5% -> 6% of each run, Pallas kernels for 0% -> 0%
where the time goes in v8:
time: 291 us
  blocking collectives  131 us (45%)
  waiting for transfers between devices  82.2 us (28%)
  matrix products  31.8 us (11%)
  between operations  14.2 us (5%)
  other arithmetic  13.4 us (5%)
  starting transfers between devices  10.5 us (4%)
  local copies, waits for them, and re-layouts  7.42 us (3%)
    all_to_all x1, blocking collectives, per_device(): received = lax.all_to_all(payload, 'wide', 0, 0, tiled=True)  118 us
    all_gather x1, waiting for transfers between devices, per_device(): gathered_features = lax.all_gather(features, 'wide', axis=0, tiled=True)  70.2 us
    dot_general x1, matrix products, per_device(): lax.dot_general(panel, all_grad, (((0,), (0,)), ((), ())), preferred_elem...  11.7 us
    all_to_all x1, waiting for transfers between devices, per_device(): lax.all_to_all(jnp.broadcast_to(band[None], (owners, rows, width)), 'wide...  11.4 us
    all_to_all x1, starting transfers between devices, per_device(): lax.all_to_all(jnp.broadcast_to(band[None], (owners, rows, width)), 'wide...  10.5 us
    dot_general x1, matrix products, per_device(): jnp.dot(panel, gathered_features, preferred_element_type=jnp.float32)  9.12 us
    unnamed x17, local copies, waits for them, and re-layouts  6.12 us
    dot_general x1, matrix products, per_device(): jnp.einsum('skj,sktc->stjc', onehot, tiles, preferred_element_type=jnp.fl...  5.9 us
  transfers between devices with their start and end apart: 2, of which 2 were waited for; matrix products, arithmetic and copies ran while one was open for 6% of the time, Pallas kernels for 0%

profile of v8, /device:TPU:0, one launch (start us, length us, event | category | flops | bytes accessed | tf_op | source)
XLA Modules:
  0.0 290.7 jit_solution(1143067712157480927)
XLA Ops:
  7.2 0.0 copy-start
  7.2 0.0 copy-start.7
  7.2 0.0 all-gather.2.cloned.1.call-start
  7.2 0.7 all-gather.2.cloned.1.call-update
  7.9 0.1 broadcast_bitcast_fusion
  8.0 1.5 fusion.8
  9.5 0.9 bitcast_multiply_fusion
  10.4 0.7 compare_convert_fusion.1
  11.1 0.0 copy-done
  11.1 5.9 %bitcast_reduce_fusion = (f32[2,128]{1,0:T(2,128)S(1)}, bf16[2,64,128,128]{3,1,2,0:T(8,128)(2,1)}) fusion(bf16[2,48,128,128]{3,2,1,0:T(8,128)(2,1)S(1)} %bitcast.48, s32[2,48]{1,0:T(2,128)} %bitcast.52, bf16[2,48]{1,0:T(2,128)(2,1)S(1)} %compare_convert_fusion.1), kind=kOutput, calls=%fused_computation.3 | convolution fusion | flops 205532928 | bytes 7341632 | tf_op jit(solution)/shard_map/skj,sktc->stjc/dot_general | solution.py:21
  17.0 2.4 psum.14
  19.5 0.0 copy-done.7
  19.5 2.1 all_gather.7
  21.6 70.2 %all-gather.2.cloned.1.call-done = bf16[8192,512]{1,0:T(8,128)(2,1)} async-done(((bf16[128,512]{1,0:T(8,128)(2,1)}), bf16[8192,512]{1,0:T(8,128)(2,1)}) %all-gather.2.cloned.1.call-update) | async-done | bytes 8388624 | tf_op jit(solution)/shard_map/all_gather | solution.py:16
  91.8 0.0 copy-start.2
  91.8 0.0 copy-start.5
  91.8 9.1 %fusion.1 = f32[256,512]{1,0:T(8,128)S(1)} fusion(bf16[8192,512]{1,0:T(8,128)(2,1)} %all-gather.2.cloned.1.call-done, bf16[32,8,64,128]{3,2,1,0:T(8,128)(2,1)} %bitcast.50), kind=kOutput, calls=%fused_computation.6 | convolution fusion | flops 2147483648 | bytes 13107200 | tf_op jit(solution)/shard_map/dot_general | solution.py:29
  100.9 0.0 copy-done.2
  100.9 0.0 copy-done.5
  100.9 0.0 copy-start.4
  100.9 0.6 convolution_add_fusion
  101.5 0.2 copy-done.4
  101.7 0.1 broadcast_in_dim.4
  101.9 5.4 %all_to_all.15 = f32[2,256,512]{2,1,0:T(8,128)} all-to-all(f32[2,256,512]{2,1,0:T(8,128)S(1)} %broadcast_in_dim.4), channel_id=1, replica_groups=mesh['wide'=64,'narrow'=2] {'narrow'}, dimensions={0} | all-to-all | bytes 2097152 | tf_op jit(solution)/shard_map/all_to_all | solution.py:39
  107.2 2.1 reduce_sum.38
  109.4 2.2 multiply_convert_fusion
  111.6 1.7 fusion.23
  113.3 0.0 copy-start.6
  113.3 11.7 %convolution_convert_fusion = bf16[8192,512]{1,0:T(8,128)(2,1)S(1)} fusion(bf16[256,512]{1,0:T(8,128)(2,1)S(1)} %get-tuple-element.5, bf16[32,8,64,128]{3,2,1,0:T(8,128)(2,1)} %bitcast.51), kind=kOutput, calls=%fused_computation.1 | convolution fusion | flops 2151677952 | bytes 12845056 | tf_op jit(solution)/shard_map/dot_general | solution.py:54
  125.0 0.0 copy-done.6
  125.0 0.3 convert_bitcast_fusion
  125.4 0.7 pad_maximum_fusion
  126.1 117.9 %all_to_all.16 = bf16[64,144,512]{2,1,0:T(8,128)(2,1)S(1)} all-to-all(bf16[64,144,512]{2,1,0:T(8,128)(2,1)S(1)} %pad_maximum_fusion), channel_id=1, replica_groups=mesh['wide'=64,'narrow'=2] {'wide'}, dimensions={0} | all-to-all | bytes 18874368 | tf_op jit(solution)/shard_map/all_to_all | solution.py:74
  244.0 0.0 copy-start.1
  244.0 3.6 %copy-done.1 = bf16[64,144,512]{2,1,0:T(8,128)(2,1)} copy-done((bf16[64,144,512]{2,1,0:T(8,128)(2,1)}, bf16[64,144,512]{2,1,0:T(8,128)(2,1)S(1)}, u32[]{:S(2)}) %copy-start.1) | copy-done | bytes 9437208
  247.6 0.2 add_reduce_fusion
  247.8 3.4 %psum.15 = f32[8,512]{1,0:T(8,128)S(1)} all-reduce(f32[8,512]{1,0:T(8,128)S(1)} %add_reduce_fusion), channel_id=1, replica_groups=mesh['wide'=64,'narrow'=2] {'narrow'}, use_global_device_ids=true, to_apply=%region_5.6 | all-reduce | flops 4096 | bytes 32768 | tf_op jit(solution)/shard_map/psum | solution.py:80
  251.2 1.1 broadcast_in_dim.5
  252.3 10.5 %all-to-all-start.2 = ((f32[64,8,512]{2,1,0:T(8,128)}), f32[64,8,512]{2,1,0:T(8,128)}, u32[]{:S(2)}, u32[]{:S(2)}) async-start(f32[64,8,512]{2,1,0:T(8,128)} %broadcast_in_dim.5), calls=%async_computation.2 | async-start | bytes 2097152 | tf_op jit(solution)/shard_map/all_to_all | solution.py:81
  262.8 0.0 copy-start.3
  262.8 1.7 multiply_convert_fusion.1
  264.5 4.8 %convert_reduce_fusion = f32[128,512]{1,0:T(8,128)S(1)} fusion(bf16[64,144,512]{2,1,0:T(8,128)(2,1)} %copy-done.1), kind=kLoop, calls=%fused_computation | loop fusion | flops 8323072 | bytes 8650752 | tf_op jit(solution)/shard_map/reduce_sum | solution.py:84
  269.3 0.0 copy-done.3
  269.3 1.0 convolution_convert_fusion.1
  270.3 11.4 %all-to-all-done.2 = f32[64,8,512]{2,1,0:T(8,128)} async-done(((f32[64,8,512]{2,1,0:T(8,128)}), f32[64,8,512]{2,1,0:T(8,128)}, u32[]{:S(2)}, u32[]{:S(2)}) %all-to-all-start.2) | async-done | bytes 1048608 | tf_op jit(solution)/shard_map/all_to_all | solution.py:81
  281.6 2.3 copy.26
  (2 shorter events, 0.0 us)
Async XLA Ops:
  7.2 4.0 %copy-start = (bf16[2,1,48,128,128]{4,3,2,1,0:T(8,128)(2,1)S(1)}, bf16[2,1,48,128,128]{4,3,2,1,0:T(8,128)(2,1)}, u32[]{:S(2)}) copy-start(bf16[2,1,48,128,128]{4,3,2,1,0:T(8,128)(2,1)} %param.10) | copy-start | bytes 9437188
  7.2 12.3 %copy-start.7 = (bf16[128,512]{1,0:T(8,128)(2,1)S(1)}, bf16[128,512]{1,0:T(8,128)(2,1)}, u32[]{:S(2)}) copy-start(bf16[128,512]{1,0:T(8,128)(2,1)} %param.11) | copy-start | bytes 393220
  7.2 84.6 %all-gather.2.cloned.1.call-start = ((), (), s32[]{:S(2)}) async-start(), calls=%async_computation.3 | async-start | bytes 8519680 | tf_op jit(solution)/shard_map/all_gather | solution.py:16
  91.8 9.1 %copy-start.2 = (bf16[512,512]{1,0:T(8,128)(2,1)S(1)}, bf16[512,512]{1,0:T(8,128)(2,1)}, u32[]{:S(2)}) copy-start(bf16[512,512]{1,0:T(8,128)(2,1)} %param.7) | copy-start | bytes 1572868
  91.8 9.1 %copy-start.5 = (f32[256,512]{1,0:T(8,128)S(1)}, f32[256,512]{1,0:T(8,128)}, u32[]{:S(2)}) copy-start(f32[256,512]{1,0:T(8,128)} %bitcast_multiply_fusion) | copy-start | bytes 1572868
  100.9 0.8 copy-start.4
  113.3 11.7 %copy-start.6 = (bf16[128,512]{1,0:T(8,128)(2,1)S(1)}, bf16[128,512]{1,0:T(8,128)(2,1)}, u32[]{:S(2)}) copy-start(bf16[128,512]{1,0:T(8,128)(2,1)} %param.6) | copy-start | bytes 393220
  244.0 3.6 %copy-start.1 = (bf16[64,144,512]{2,1,0:T(8,128)(2,1)}, bf16[64,144,512]{2,1,0:T(8,128)(2,1)S(1)}, u32[]{:S(2)}) copy-start(bf16[64,144,512]{2,1,0:T(8,128)(2,1)S(1)} %all_to_all.16) | copy-start | bytes 28311556
  252.3 29.4 %all-to-all-start.2 = ((f32[64,8,512]{2,1,0:T(8,128)}), f32[64,8,512]{2,1,0:T(8,128)}, u32[]{:S(2)}, u32[]{:S(2)}) async-start(f32[64,8,512]{2,1,0:T(8,128)} %broadcast_in_dim.5), calls=%async_computation.2 | async-start | bytes 2097152 | tf_op jit(solution)/shard_map/all_to_all | solution.py:81
  262.8 6.5 %copy-start.3 = (bf16[512,512]{1,0:T(8,128)(2,1)S(1)}, bf16[512,512]{1,0:T(8,128)(2,1)}, u32[]{:S(2)}) copy-start(bf16[512,512]{1,0:T(8,128)(2,1)} %param.7) | copy-start | bytes 1572868
Sparse Core Ops, SparseCore 0:
  10.9 80.8 all-gather.1

commit v9 on v8

--- a/solution.py
+++ b/solution.py
@@ -26,6 +26,7 @@
     panel = dense.astype(jnp.bfloat16)
     projected = jnp.dot(features, weight, preferred_element_type=jnp.float32).astype(jnp.bfloat16)
     own = lax.axis_index("narrow")
+    pair = lax.axis_size("narrow")
     aggregated = jnp.dot(panel, gathered_features, preferred_element_type=jnp.float32)
     partial_sum = jnp.dot(
         aggregated, weight.astype(jnp.float32), precision=lax.Precision.HIGHEST,
@@ -34,7 +35,6 @@
     selector = (jnp.arange(copies, dtype=jnp.int32) == own).astype(jnp.float32)
     self_term = selector[:, None, None] * projected.astype(jnp.float32)[None]
     partial_sum = partial_sum + self_term.reshape(copies * tile, width)
-    pair = lax.axis_size("narrow")
     total = jnp.sum(
         lax.all_to_all(
             jnp.broadcast_to(partial_sum[None], (pair,) + partial_sum.shape), "narrow", 0, 0,
@@ -60,26 +60,24 @@
     ) + lax.dot_general(
         features, own_grad, (((0,), (0,)), ((), ())), preferred_element_type=jnp.float32
     )
-    rows = width // owners
-    high = weight_terms.astype(jnp.bfloat16)
-    low = (weight_terms - high.astype(jnp.float32)).astype(jnp.bfloat16)
-    payload = jnp.concatenate(
-        [
-            terms.reshape(owners, tile, width),
-            high.reshape(owners, rows, width),
-            low.reshape(owners, rows, width),
-        ],
-        axis=1,
+    pair = lax.axis_size("narrow")
+    rows = width // (owners * pair)
+    shares = lax.all_to_all(
+        weight_terms.reshape(owners, pair, rows, width), "narrow", 1, 1, tiled=True
     )
+    shares = jnp.sum(shares, axis=1)
+    high = shares.astype(jnp.bfloat16)
+    low = (shares - high.astype(jnp.float32)).astype(jnp.bfloat16)
+    payload = jnp.concatenate([terms.reshape(owners, tile, width), high, low], axis=1)
     received = lax.all_to_all(payload, "wide", 0, 0, tiled=True)
     band = jnp.sum(
         received[:, tile:tile + rows].astype(jnp.float32)
         + received[:, tile + rows:].astype(jnp.float32),
         axis=0,
     )
-    band = lax.psum(band, "narrow")
     grad_weight = lax.all_to_all(
-        jnp.broadcast_to(band[None], (owners, rows, width)), "wide", 0, 0, tiled=True
+        jnp.broadcast_to(band[None], (owners * pair, rows, width)), ("wide", "narrow"), 0, 0,
+        tiled=True,
     ).reshape(width, width)
     gathered_sum = jnp.sum(received[:, :tile].astype(jnp.float32), axis=0)
     message = (gathered_sum + own_grad.astype(jnp.float32)).astype(jnp.bfloat16)

time: 291 us -> 302 us (1.038)
  other arithmetic: 13.4 us -> 21.5 us
  matrix products: 31.8 us -> 36 us
  local copies, waits for them, and re-layouts: 7.42 us -> 11.4 us
    reshape x0 -> x3, local copies, waits for them, and re-layouts: none -> 6.45 us  [the longest x2 3.89 us: per_device(): weight_terms.reshape(owners, pair, rows, width)]
    all_to_all x1, blocking collectives: 118 us -> 112 us  [per_device(): received = lax.all_to_all(payload, 'wide', 0, 0, tiled=True)]
    all_to_all x0 -> x1, blocking collectives: none -> 5.42 us  [per_device(): lax.all_to_all(weight_terms.reshape(owners, pair, rows, width), 'narrow',...]
    concatenate x1, other arithmetic: 0.75 us -> 4.98 us  [per_device(): jnp.concatenate([terms.reshape(owners, tile, width), high, low], axis=1)]
    psum x1 -> x0, blocking collectives: 3.36 us -> none  [per_device(): band = lax.psum(band, 'narrow')]
    dot_general x1, matrix products: 11.7 us -> 14.9 us  [per_device(): lax.dot_general(panel, all_grad, (((0,), (0,)), ((), ())), preferred_elem...]
    unnamed x17 -> x16, local copies, waits for them, and re-layouts: 6.12 us -> 3.66 us
  transfers between devices with their start and end apart: 2 -> 2, of which waited for: 2 -> 2; matrix products, arithmetic and copies ran while one was open for 6% -> 5% of each run, Pallas kernels for 0% -> 0%
where the time goes in v9:
time: 302 us; the launch traced here: 301 us
  blocking collectives  128 us (42%)
  waiting for transfers between devices  82.1 us (27%)
  matrix products  36 us (12%)
  other arithmetic  21.5 us (7%)
  between operations  14.2 us (5%)
  local copies, waits for them, and re-layouts  11.4 us (4%)
  starting transfers between devices  8.58 us (3%)
    all_to_all x1, blocking collectives, per_device(): received = lax.all_to_all(payload, 'wide', 0, 0, tiled=True)  112 us
    all_gather x1, waiting for transfers between devices, per_device(): gathered_features = lax.all_gather(features, 'wide', axis=0, tiled=True)  70.2 us
    dot_general x1, matrix products, per_device(): lax.dot_general(panel, all_grad, (((0,), (0,)), ((), ())), preferred_elem...  14.9 us
    all_to_all x1, waiting for transfers between devices, per_device(): lax.all_to_all(jnp.broadcast_to(band[None], (owners * pair, rows, width))...  11.2 us
    dot_general x1, matrix products, per_device(): jnp.dot(panel, gathered_features, preferred_element_type=jnp.float32)  9.12 us
    all_to_all x1, starting transfers between devices, per_device(): lax.all_to_all(jnp.broadcast_to(band[None], (owners * pair, rows, width))...  8.54 us
  transfers between devices with their start and end apart: 2, of which 2 were waited for; matrix products, arithmetic and copies ran while one was open for 5% of the time, Pallas kernels for 0%

profile of v9, /device:TPU:0, one launch (start us, length us, event | category | flops | bytes accessed | tf_op | source)
XLA Modules:
  0.0 301.5 jit_solution(14686213122805009287)
XLA Ops:
  7.2 0.0 copy-start
  7.2 0.0 copy-start.7
  7.2 0.0 all-gather.2.cloned.1.call-start
  7.2 0.7 all-gather.2.cloned.1.call-update
  7.9 0.1 broadcast_bitcast_fusion
  8.0 1.5 fusion.8
  9.5 0.9 bitcast_multiply_fusion
  10.4 0.7 compare_convert_fusion.1
  11.1 0.0 copy-done
  11.1 5.9 %bitcast_reduce_fusion = (f32[2,128]{1,0:T(2,128)S(1)}, bf16[2,64,128,128]{3,1,2,0:T(8,128)(2,1)}) fusion(bf16[2,48,128,128]{3,2,1,0:T(8,128)(2,1)S(1)} %bitcast.41, s32[2,48]{1,0:T(2,128)} %bitcast.45, bf16[2,48]{1,0:T(2,128)(2,1)S(1)} %compare_convert_fusion.1), kind=kOutput, calls=%fused_computation.3 | convolution fusion | flops 205532928 | bytes 7341632 | tf_op jit(solution)/shard_map/skj,sktc->stjc/dot_general | solution.py:21
  17.0 2.4 psum.7
  19.5 0.0 copy-done.7
  19.5 2.1 all_gather.7
  21.6 70.2 %all-gather.2.cloned.1.call-done = bf16[8192,512]{1,0:T(8,128)(2,1)} async-done(((bf16[128,512]{1,0:T(8,128)(2,1)}), bf16[8192,512]{1,0:T(8,128)(2,1)}) %all-gather.2.cloned.1.call-update) | async-done | bytes 8388624 | tf_op jit(solution)/shard_map/all_gather | solution.py:16
  91.8 0.0 copy-start.5
  91.8 9.1 %fusion.1 = f32[256,512]{1,0:T(8,128)S(1)} fusion(bf16[8192,512]{1,0:T(8,128)(2,1)} %all-gather.2.cloned.1.call-done, bf16[32,8,64,128]{3,2,1,0:T(8,128)(2,1)} %bitcast.43), kind=kOutput, calls=%fused_computation.6 | convolution fusion | flops 2147483648 | bytes 13107200 | tf_op jit(solution)/shard_map/dot_general | solution.py:30
  100.9 0.0 copy-done.2
  100.9 0.0 copy-done.5
  100.9 0.0 copy-start.4
  100.9 0.6 convolution_add_fusion
  101.5 0.2 copy-done.4
  101.7 0.1 broadcast_in_dim.4
  101.9 5.4 %all_to_all.20 = f32[2,256,512]{2,1,0:T(8,128)} all-to-all(f32[2,256,512]{2,1,0:T(8,128)S(1)} %broadcast_in_dim.4), channel_id=1, replica_groups=mesh['wide'=64,'narrow'=2] {'narrow'}, dimensions={0} | all-to-all | bytes 2097152 | tf_op jit(solution)/shard_map/all_to_all | solution.py:39
  107.2 2.1 reduce_sum.47
  109.4 2.2 multiply_convert_fusion
  111.6 1.7 fusion.20
  113.3 0.0 copy-start.6
  113.3 14.9 %convolution_convert_fusion = bf16[8192,512]{1,0:T(8,128)(2,1)} fusion(bf16[256,512]{1,0:T(8,128)(2,1)S(1)} %get-tuple-element.5, bf16[32,8,64,128]{3,2,1,0:T(8,128)(2,1)} %bitcast.44), kind=kOutput, calls=%fused_computation.1 | convolution fusion | flops 2151677952 | bytes 12845056 | tf_op jit(solution)/shard_map/dot_general | solution.py:54
  128.2 0.0 copy-done.6
  128.2 1.3 fusion.7
  129.5 2.6 reshape.55
  132.1 1.3 copy.13
  133.4 5.4 %all_to_all.21 = f32[64,2,4,512]{3,2,0,1:T(4,128)} all-to-all(f32[64,2,4,512]{3,2,0,1:T(4,128)S(1)} %copy.13), channel_id=1, replica_groups=mesh['wide'=64,'narrow'=2] {'narrow'}, dimensions={1} | all-to-all | bytes 2097152 | tf_op jit(solution)/shard_map/all_to_all | solution.py:65
  138.8 2.4 reduce_sum.50
  141.2 1.4 subtract_convert_fusion
  142.6 5.0 %pad_maximum_fusion = bf16[64,136,512]{2,1,0:T(8,128)(2,1)S(1)} fusion(bf16[64,4,512]{2,1,0:T(4,128)(2,1)S(1)} %get-tuple-element.3, bf16[64,4,512]{2,1,0:T(4,128)(2,1)S(1)} %get-tuple-element.4, bf16[64,128,512]{2,1,0:T(8,128)(2,1)} %bitcast.42), kind=kLoop, calls=%fused_computation.2 | loop fusion | flops 26738688 | bytes 17825792 | tf_op jit(solution)/shard_map/concatenate | solution.py:71
  147.6 112.4 %all_to_all.22 = bf16[64,136,512]{2,1,0:T(8,128)(2,1)S(1)} all-to-all(bf16[64,136,512]{2,1,0:T(8,128)(2,1)S(1)} %pad_maximum_fusion), channel_id=1, replica_groups=mesh['wide'=64,'narrow'=2] {'wide'}, dimensions={0} | all-to-all | bytes 17825792 | tf_op jit(solution)/shard_map/all_to_all | solution.py:72
  260.1 3.4 %copy-done.1 = bf16[64,136,512]{2,1,0:T(8,128)(2,1)} copy-done((bf16[64,136,512]{2,1,0:T(8,128)(2,1)}, bf16[64,136,512]{2,1,0:T(8,128)(2,1)S(1)}, u32[]{:S(2)}) %copy-start.1) | copy-done | bytes 8912920
  263.5 0.2 add_reduce_fusion
  263.7 1.1 broadcast_in_dim.5
  264.8 8.5 %all-to-all-start.3 = ((f32[128,4,512]{2,1,0:T(4,128)}), f32[128,4,512]{2,1,0:T(4,128)}, u32[]{:S(2)}, u32[]{:S(2)}) async-start(f32[128,4,512]{2,1,0:T(4,128)} %broadcast_in_dim.5), calls=%async_computation.3 | async-start | bytes 2097152 | tf_op jit(solution)/shard_map/all_to_all | solution.py:78
  273.4 0.0 copy-start.3
  273.4 1.7 multiply_convert_fusion.1
  275.1 4.8 %convert_reduce_fusion = f32[128,512]{1,0:T(8,128)S(1)} fusion(bf16[64,136,512]{2,1,0:T(8,128)(2,1)} %copy-done.1), kind=kLoop, calls=%fused_computation | loop fusion | flops 8323072 | bytes 8650752 | tf_op jit(solution)/shard_map/reduce_sum | solution.py:82
  279.9 0.0 copy-done.3
  279.9 1.0 convolution_convert_fusion.1
  280.9 11.2 %all-to-all-done.3 = f32[128,4,512]{2,1,0:T(4,128)} async-done(((f32[128,4,512]{2,1,0:T(4,128)}), f32[128,4,512]{2,1,0:T(4,128)}, u32[]{:S(2)}, u32[]{:S(2)}) %all-to-all-start.3) | async-done | bytes 1048608 | tf_op jit(solution)/shard_map/all_to_all | solution.py:78
  292.1 2.6 reshape.56
  (4 shorter events, 0.0 us)
Async XLA Ops:
  7.2 4.0 %copy-start = (bf16[2,1,48,128,128]{4,3,2,1,0:T(8,128)(2,1)S(1)}, bf16[2,1,48,128,128]{4,3,2,1,0:T(8,128)(2,1)}, u32[]{:S(2)}) copy-start(bf16[2,1,48,128,128]{4,3,2,1,0:T(8,128)(2,1)} %param.10) | copy-start | bytes 9437188
  7.2 12.3 %copy-start.7 = (bf16[128,512]{1,0:T(8,128)(2,1)S(1)}, bf16[128,512]{1,0:T(8,128)(2,1)}, u32[]{:S(2)}) copy-start(bf16[128,512]{1,0:T(8,128)(2,1)} %param.11) | copy-start | bytes 393220
  7.2 84.6 %all-gather.2.cloned.1.call-start = ((), (), s32[]{:S(2)}) async-start(), calls=%async_computation.4 | async-start | bytes 8519680 | tf_op jit(solution)/shard_map/all_gather | solution.py:16
  91.8 9.1 %copy-start.2 = (bf16[512,512]{1,0:T(8,128)(2,1)S(1)}, bf16[512,512]{1,0:T(8,128)(2,1)}, u32[]{:S(2)}) copy-start(bf16[512,512]{1,0:T(8,128)(2,1)} %param.7) | copy-start | bytes 1572868
  91.8 9.1 %copy-start.5 = (f32[256,512]{1,0:T(8,128)S(1)}, f32[256,512]{1,0:T(8,128)}, u32[]{:S(2)}) copy-start(f32[256,512]{1,0:T(8,128)} %bitcast_multiply_fusion) | copy-start | bytes 1572868
  100.9 0.8 copy-start.4
  113.3 15.0 %copy-start.6 = (bf16[128,512]{1,0:T(8,128)(2,1)S(1)}, bf16[128,512]{1,0:T(8,128)(2,1)}, u32[]{:S(2)}) copy-start(bf16[128,512]{1,0:T(8,128)(2,1)} %param.6) | copy-start | bytes 393220
  260.1 3.4 %copy-start.1 = (bf16[64,136,512]{2,1,0:T(8,128)(2,1)}, bf16[64,136,512]{2,1,0:T(8,128)(2,1)S(1)}, u32[]{:S(2)}) copy-start(bf16[64,136,512]{2,1,0:T(8,128)(2,1)S(1)} %all_to_all.22) | copy-start | bytes 26738692
  264.8 27.3 %all-to-all-start.3 = ((f32[128,4,512]{2,1,0:T(4,128)}), f32[128,4,512]{2,1,0:T(4,128)}, u32[]{:S(2)}, u32[]{:S(2)}) async-start(f32[128,4,512]{2,1,0:T(4,128)} %broadcast_in_dim.5), calls=%async_computation.3 | async-start | bytes 2097152 | tf_op jit(solution)/shard_map/all_to_all | solution.py:78
  273.4 6.5 %copy-start.3 = (bf16[512,512]{1,0:T(8,128)(2,1)S(1)}, bf16[512,512]{1,0:T(8,128)(2,1)}, u32[]{:S(2)}) copy-start(bf16[512,512]{1,0:T(8,128)(2,1)} %param.7) | copy-start | bytes 1572868
Sparse Core Ops, SparseCore 0:
  10.9 80.8 all-gather.1

commit v10 on v4

--- a/solution.py
+++ b/solution.py
@@ -35,8 +35,11 @@
     self_term = selector[:, None, None] * projected.astype(jnp.float32)[None]
     partial_sum = partial_sum + self_term.reshape(copies * tile, width)
     own_scale = lax.dynamic_slice_in_dim(scale, own * tile, tile, 0)[:, None]
-    halves = lax.all_to_all(partial_sum.reshape(copies, tile, width), "narrow", 0, 0, tiled=True)
-    preact = jnp.sum(halves, axis=0) * own_scale
+    pair = lax.axis_size("narrow")
+    mine = lax.dynamic_slice_in_dim(partial_sum, own * tile, tile, 0)
+    theirs = lax.dynamic_slice_in_dim(partial_sum, (pair - 1 - own) * tile, tile, 0)
+    theirs = lax.ppermute(theirs, "narrow", [(i, pair - 1 - i) for i in range(pair)])
+    preact = (mine + theirs) * own_scale
     activated = jax.nn.silu(preact).astype(jnp.bfloat16)
     sig = jax.nn.sigmoid(preact)
     own_grad = (

time: 290 us -> 291 us (level)
  blocking collectives: 131 us -> 126 us
  starting transfers between devices: 8.84 us -> 13.4 us
  waiting for transfers between devices: 84.8 us -> 88.6 us
  other arithmetic: 12.3 us -> 9.28 us
    all_to_all x1 -> x0, blocking collectives: 4.88 us -> none  [per_device(): lax.all_to_all(partial_sum.reshape(copies, tile, width), 'narrow', 0, 0,...]
    all_to_all x1, starting transfers between devices: 8.8 us -> 13.3 us  [per_device(): lax.all_to_all(jnp.broadcast_to(band[None], (owners, rows, width)), 'wide...]
    all_gather x1, waiting for transfers between devices: 71.1 us -> 74.8 us  [per_device(): gathered_features = lax.all_gather(features, 'wide', axis=0, tiled=True)]
    unnamed x17 -> x19, local copies, waits for them, and re-layouts: 6.33 us -> 6.88 us
  transfers between devices with their start and end apart: 2 -> 3, of which waited for: 2 -> 2; matrix products, arithmetic and copies ran while one was open for 5% -> 5% of each run, Pallas kernels for 0% -> 0%
where the time goes in v10:
time: 291 us
  blocking collectives  126 us (43%)
  waiting for transfers between devices  88.6 us (30%)
  matrix products  31.7 us (11%)
  between operations  14.2 us (5%)
  starting transfers between devices  13.4 us (5%)
  other arithmetic  9.28 us (3%)
  local copies, waits for them, and re-layouts  8.14 us (3%)
    all_to_all x1, blocking collectives, per_device(): received = lax.all_to_all(payload, 'wide', 0, 0, tiled=True)  118 us
    all_gather x1, waiting for transfers between devices, per_device(): gathered_features = lax.all_gather(features, 'wide', axis=0, tiled=True)  74.8 us
    all_to_all x1, starting transfers between devices, per_device(): lax.all_to_all(jnp.broadcast_to(band[None], (owners, rows, width)), 'wide...  13.3 us
    all_to_all x1, waiting for transfers between devices, per_device(): lax.all_to_all(jnp.broadcast_to(band[None], (owners, rows, width)), 'wide...  13.1 us
    dot_general x1, matrix products, per_device(): lax.dot_general(panel, all_grad, (((0,), (0,)), ((), ())), preferred_elem...  11.7 us
    dot_general x1, matrix products, per_device(): jnp.dot(panel, gathered_features, preferred_element_type=jnp.float32)  9.13 us
    unnamed x19, local copies, waits for them, and re-layouts  6.88 us
    dot_general x1, matrix products, per_device(): jnp.einsum('skj,sktc->stjc', onehot, tiles, preferred_element_type=jnp.fl...  5.87 us
  transfers between devices with their start and end apart: 3, of which 2 were waited for; matrix products, arithmetic and copies ran while one was open for 5% of the time, Pallas kernels for 0%

profile of v10, /device:TPU:0, one launch (start us, length us, event | category | flops | bytes accessed | tf_op | source)
XLA Modules:
  0.0 290.9 jit_solution(3622110942539299920)
XLA Ops:
  7.2 0.0 copy-start
  7.2 0.0 all-gather.2.cloned.1.call-start
  7.2 0.7 all-gather.2.cloned.1.call-update
  7.9 0.1 broadcast_bitcast_fusion
  8.0 1.4 fusion.8
  9.4 0.9 bitcast_multiply_fusion
  10.4 0.7 compare_convert_fusion.1
  11.1 0.0 copy-done
  11.1 5.9 %bitcast_reduce_fusion = (f32[2,128]{1,0:T(2,128)S(1)}, bf16[2,64,128,128]{3,1,2,0:T(8,128)(2,1)}) fusion(bf16[2,48,128,128]{3,2,1,0:T(8,128)(2,1)S(1)} %bitcast.49, s32[2,48]{1,0:T(2,128)} %bitcast.53, bf16[2,48]{1,0:T(2,128)(2,1)S(1)} %compare_convert_fusion.1), kind=kOutput, calls=%fused_computation.3 | convolution fusion | flops 205532928 | bytes 7341632 | tf_op jit(solution)/shard_map/skj,sktc->stjc/dot_general | solution.py:21
  16.9 74.8 %all-gather.2.cloned.1.call-done = bf16[8192,512]{1,0:T(8,128)(2,1)} async-done(((bf16[128,512]{1,0:T(8,128)(2,1)}), bf16[8192,512]{1,0:T(8,128)(2,1)}) %all-gather.2.cloned.1.call-update) | async-done | bytes 8388624 | tf_op jit(solution)/shard_map/all_gather | solution.py:16
  91.8 0.0 copy-start.2
  91.8 0.0 copy-start.6
  91.8 0.0 copy-start.8
  91.8 9.1 %fusion.1 = f32[256,512]{1,0:T(8,128)S(1)} fusion(bf16[8192,512]{1,0:T(8,128)(2,1)} %all-gather.2.cloned.1.call-done, bf16[32,8,64,128]{3,2,1,0:T(8,128)(2,1)} %bitcast.51), kind=kOutput, calls=%fused_computation.6 | convolution fusion | flops 2147483648 | bytes 13107200 | tf_op jit(solution)/shard_map/dot_general | solution.py:29
  100.9 0.0 copy-done.2
  100.9 0.0 copy-done.6
  100.9 0.0 copy-start.4
  100.9 0.6 convolution_add_fusion
  101.5 0.2 copy-done.4
  101.7 0.0 copy-start.5
  101.7 0.8 copy-done.5
  102.5 0.0 collective-permute-start
  102.5 2.6 psum.14
  105.1 0.1 dynamic_slice.11
  105.2 0.0 collective-permute-done
  105.2 0.0 copy-done.8
  105.2 1.9 multiply_convert_fusion
  107.1 2.2 all_gather.7
  109.3 1.7 fusion.17
  110.9 0.0 copy-start.7
  111.0 11.7 %convolution_convert_fusion = bf16[8192,512]{1,0:T(8,128)(2,1)S(1)} fusion(bf16[256,512]{1,0:T(8,128)(2,1)S(1)} %all_gather.7, bf16[32,8,64,128]{3,2,1,0:T(8,128)(2,1)} %bitcast.52), kind=kOutput, calls=%fused_computation.1 | convolution fusion | flops 2151677952 | bytes 12845056 | tf_op jit(solution)/shard_map/dot_general | solution.py:49
  122.7 0.0 copy-done.7
  122.7 0.3 convert_bitcast_fusion
  123.0 0.7 pad_maximum_fusion
  123.8 117.5 %all_to_all.10 = bf16[64,144,512]{2,1,0:T(8,128)(2,1)S(1)} all-to-all(bf16[64,144,512]{2,1,0:T(8,128)(2,1)S(1)} %pad_maximum_fusion), channel_id=1, replica_groups=mesh['wide'=64,'narrow'=2] {'wide'}, dimensions={0} | all-to-all | bytes 18874368 | tf_op jit(solution)/shard_map/all_to_all | solution.py:69
  241.3 0.0 copy-start.1
  241.3 3.6 %copy-done.1 = bf16[64,144,512]{2,1,0:T(8,128)(2,1)} copy-done((bf16[64,144,512]{2,1,0:T(8,128)(2,1)}, bf16[64,144,512]{2,1,0:T(8,128)(2,1)S(1)}, u32[]{:S(2)}) %copy-start.1) | copy-done | bytes 9437208
  244.9 0.2 add_reduce_fusion
  245.1 3.4 %psum.15 = f32[8,512]{1,0:T(8,128)S(1)} all-reduce(f32[8,512]{1,0:T(8,128)S(1)} %add_reduce_fusion), channel_id=1, replica_groups=mesh['wide'=64,'narrow'=2] {'narrow'}, use_global_device_ids=true, to_apply=%region_4.5 | all-reduce | flops 4096 | bytes 32768 | tf_op jit(solution)/shard_map/psum | solution.py:75
  248.5 1.1 broadcast_in_dim.2
  249.6 13.3 %all-to-all-start.1 = ((f32[64,8,512]{2,1,0:T(8,128)}), f32[64,8,512]{2,1,0:T(8,128)}, u32[]{:S(2)}, u32[]{:S(2)}) async-start(f32[64,8,512]{2,1,0:T(8,128)} %broadcast_in_dim.2), calls=%async_computation.1 | async-start | bytes 2097152 | tf_op jit(solution)/shard_map/all_to_all | solution.py:76
  262.9 0.0 copy-start.3
  262.9 4.8 %convert_reduce_fusion = f32[128,512]{1,0:T(8,128)S(1)} fusion(bf16[64,144,512]{2,1,0:T(8,128)(2,1)} %copy-done.1), kind=kLoop, calls=%fused_computation | loop fusion | flops 8323072 | bytes 8650752 | tf_op jit(solution)/shard_map/reduce_sum | solution.py:79
  267.8 0.0 copy-done.3
  267.8 1.0 convolution_convert_fusion.1
  268.7 13.1 %all-to-all-done.1 = f32[64,8,512]{2,1,0:T(8,128)} async-done(((f32[64,8,512]{2,1,0:T(8,128)}), f32[64,8,512]{2,1,0:T(8,128)}, u32[]{:S(2)}, u32[]{:S(2)}) %all-to-all-start.1) | async-done | bytes 1048608 | tf_op jit(solution)/shard_map/all_to_all | solution.py:76
  281.8 2.3 copy.25
  (3 shorter events, 0.0 us)
Async XLA Ops:
  7.2 3.9 %copy-start = (bf16[2,1,48,128,128]{4,3,2,1,0:T(8,128)(2,1)S(1)}, bf16[2,1,48,128,128]{4,3,2,1,0:T(8,128)(2,1)}, u32[]{:S(2)}) copy-start(bf16[2,1,48,128,128]{4,3,2,1,0:T(8,128)(2,1)} %param.10) | copy-start | bytes 9437188
  7.2 84.6 %all-gather.2.cloned.1.call-start = ((), (), s32[]{:S(2)}) async-start(), calls=%async_computation.2 | async-start | bytes 8519680 | tf_op jit(solution)/shard_map/all_gather | solution.py:16
  91.8 9.1 %copy-start.2 = (bf16[512,512]{1,0:T(8,128)(2,1)S(1)}, bf16[512,512]{1,0:T(8,128)(2,1)}, u32[]{:S(2)}) copy-start(bf16[512,512]{1,0:T(8,128)(2,1)} %param.7) | copy-start | bytes 1572868
  91.8 9.1 %copy-start.6 = (f32[256,512]{1,0:T(8,128)S(1)}, f32[256,512]{1,0:T(8,128)}, u32[]{:S(2)}) copy-start(f32[256,512]{1,0:T(8,128)} %bitcast_multiply_fusion) | copy-start | bytes 1572868
  91.8 13.4 %copy-start.8 = (bf16[128,512]{1,0:T(8,128)(2,1)S(1)}, bf16[128,512]{1,0:T(8,128)(2,1)}, u32[]{:S(2)}) copy-start(bf16[128,512]{1,0:T(8,128)(2,1)} %param.11) | copy-start | bytes 393220
  100.9 0.8 copy-start.4
  101.7 0.8 copy-start.5
  102.5 2.7 collective-permute-start
  110.9 11.7 %copy-start.7 = (bf16[128,512]{1,0:T(8,128)(2,1)S(1)}, bf16[128,512]{1,0:T(8,128)(2,1)}, u32[]{:S(2)}) copy-start(bf16[128,512]{1,0:T(8,128)(2,1)} %param.6) | copy-start | bytes 393220
  241.3 3.6 %copy-start.1 = (bf16[64,144,512]{2,1,0:T(8,128)(2,1)}, bf16[64,144,512]{2,1,0:T(8,128)(2,1)S(1)}, u32[]{:S(2)}) copy-start(bf16[64,144,512]{2,1,0:T(8,128)(2,1)S(1)} %all_to_all.10) | copy-start | bytes 28311556
  249.6 32.2 %all-to-all-start.1 = ((f32[64,8,512]{2,1,0:T(8,128)}), f32[64,8,512]{2,1,0:T(8,128)}, u32[]{:S(2)}, u32[]{:S(2)}) async-start(f32[64,8,512]{2,1,0:T(8,128)} %broadcast_in_dim.2), calls=%async_computation.1 | async-start | bytes 2097152 | tf_op jit(solution)/shard_map/all_to_all | solution.py:76
  262.9 4.9 %copy-start.3 = (bf16[512,512]{1,0:T(8,128)(2,1)S(1)}, bf16[512,512]{1,0:T(8,128)(2,1)}, u32[]{:S(2)}) copy-start(bf16[512,512]{1,0:T(8,128)(2,1)} %param.7) | copy-start | bytes 1572868
Sparse Core Ops, SparseCore 0:
  10.9 80.8 all-gather.1

commit v11 on v5

--- a/solution.py
+++ b/solution.py
@@ -52,9 +52,18 @@
     ) + lax.dot_general(
         features, own_grad, (((0,), (0,)), ((), ())), preferred_element_type=jnp.float32
     )
-    grad_weight = lax.psum(weight_terms, ("wide", "narrow"))
-    received = lax.all_to_all(terms.reshape(owners, tile, width), "wide", 0, 0, tiled=True)
-    gathered_sum = jnp.sum(received.astype(jnp.float32), axis=0)
+    rows = width // owners
+    payload = jnp.concatenate(
+        [terms.reshape(owners, tile, width), weight_terms.astype(jnp.bfloat16).reshape(owners, rows, width)],
+        axis=1,
+    )
+    received = lax.all_to_all(payload, "wide", 0, 0, tiled=True)
+    band = jnp.sum(received[:, tile:].astype(jnp.float32), axis=0)
+    band = lax.psum(band, "narrow").astype(jnp.bfloat16)
+    grad_weight = lax.all_to_all(
+        jnp.broadcast_to(band[None], (owners, rows, width)), "wide", 0, 0, tiled=True
+    ).reshape(width, width).astype(jnp.float32)
+    gathered_sum = jnp.sum(received[:, :tile].astype(jnp.float32), axis=0)
     message = (gathered_sum + own_grad.astype(jnp.float32)).astype(jnp.bfloat16)
     grad_features = lax.dot_general(
         message, weight, (((1,), (1,)), ((), ())), preferred_element_type=jnp.float32

time: 383 us -> 290 us (0.76)
  waiting for transfers between devices: 298 us -> 79.4 us
  blocking collectives: 9.5 us -> 125 us
  other arithmetic: 11.4 us -> 21.5 us
    psum x1 -> x0, waiting for transfers between devices: 115 us -> none  [per_device(): grad_weight = lax.psum(weight_terms, ('wide', 'narrow'))]
    all_to_all x0 -> x1, blocking collectives: none -> 112 us  [per_device(): received = lax.all_to_all(payload, 'wide', 0, 0, tiled=True)]
    all_to_all x1, waiting for transfers between devices: 111 us -> 7.62 us  [per_device(): lax.all_to_all(jnp.broadcast_to(band[None], (owners, rows, width)), 'wide...]
    concatenate x0 -> x1, other arithmetic: none -> 7.86 us  [per_device(): jnp.concatenate([terms.reshape(owners, tile, width), weight_terms.astype(...]
  transfers between devices with their start and end apart: 3 -> 2, of which waited for: 3 -> 2; matrix products, arithmetic and copies ran while one was open for 5% -> 5% of each run, Pallas kernels for 0% -> 0%
where the time goes in v11:
time: 290 us; the launch traced here: 289 us
  blocking collectives  125 us (43%)
  waiting for transfers between devices  79.4 us (27%)
  matrix products  35.4 us (12%)
  other arithmetic  21.5 us (7%)
  between operations  14.1 us (5%)
  starting transfers between devices  8.92 us (3%)
  local copies, waits for them, and re-layouts  4.85 us (2%)
    all_to_all x1, blocking collectives, per_device(): received = lax.all_to_all(payload, 'wide', 0, 0, tiled=True)  112 us
    all_gather x1, waiting for transfers between devices, per_device(): gathered_features = lax.all_gather(features, 'wide', axis=0, tiled=True)  71.1 us
    dot_general x1, matrix products, per_device(): lax.dot_general(panel, all_grad, (((0,), (0,)), ((), ())), preferred_elem...  14.9 us
    dot_general x1, matrix products, per_device(): jnp.dot(panel, gathered_features, preferred_element_type=jnp.float32)  9.13 us
    all_to_all x1, starting transfers between devices, per_device(): lax.all_to_all(jnp.broadcast_to(band[None], (owners, rows, width)), 'wide...  8.88 us
    concatenate x1, other arithmetic, per_device(): jnp.concatenate([terms.reshape(owners, tile, width), weight_terms.astype(...  7.86 us
    all_to_all x1, waiting for transfers between devices, per_device(): lax.all_to_all(jnp.broadcast_to(band[None], (owners, rows, width)), 'wide...  7.62 us
  transfers between devices with their start and end apart: 2, of which 2 were waited for; matrix products, arithmetic and copies ran while one was open for 5% of the time, Pallas kernels for 0%

profile of v11, /device:TPU:0, one launch (start us, length us, event | category | flops | bytes accessed | tf_op | source)
XLA Modules:
  0.0 289.5 jit_solution(305979991061520943)
XLA Ops:
  7.2 0.0 copy-start
  7.2 0.0 all-gather.2.cloned.1.call-start
  7.2 0.7 all-gather.2.cloned.1.call-update
  7.9 0.9 compare_convert_fusion.1
  8.8 0.2 copy-done
  9.1 0.0 copy-start.6
  9.1 5.7 %bitcast_convert_fusion = (bf16[2,128,64,128]{3,2,1,0:T(8,128)(2,1)}, f32[2,64,128,128]{3,1,2,0:T(8,128)S(1)}) fusion(bf16[2,48,128,128]{3,2,1,0:T(8,128)(2,1)S(1)} %bitcast.51, s32[2,48]{1,0:T(2,128)} %bitcast.56, bf16[2,48]{1,0:T(2,128)(2,1)S(1)} %compare_convert_fusion.1), kind=kOutput, calls=%fused_computation.4 | convolution fusion | flops 203436032 | bytes 15729216 | tf_op jit(solution)/shard_map/skj,sktc->stjc/dot_general | solution.py:21
  14.8 1.1 bitcast_reduce_fusion
  15.9 2.5 psum.14
  18.3 0.1 dynamic_slice.3
  18.4 0.1 broadcast_bitcast_fusion
  18.5 0.0 copy-done.6
  18.5 1.3 fusion.10
  19.8 0.9 bitcast_multiply_fusion
  20.7 71.1 %all-gather.2.cloned.1.call-done = bf16[8192,512]{1,0:T(8,128)(2,1)} async-done(((bf16[128,512]{1,0:T(8,128)(2,1)}), bf16[8192,512]{1,0:T(8,128)(2,1)}) %all-gather.2.cloned.1.call-update) | async-done | bytes 8388624 | tf_op jit(solution)/shard_map/all_gather | solution.py:16
  91.8 0.0 copy-start.2
  91.8 0.0 copy-start.5
  91.8 0.0 copy-start.7
  91.8 9.1 %fusion.1 = f32[256,512]{1,0:T(8,128)S(1)} fusion(bf16[8192,512]{1,0:T(8,128)(2,1)} %all-gather.2.cloned.1.call-done, bf16[32,8,64,128]{3,2,1,0:T(8,128)(2,1)} %bitcast.53), kind=kOutput, calls=%fused_computation.6 | convolution fusion | flops 2147483648 | bytes 13107200 | tf_op jit(solution)/shard_map/dot_general | solution.py:29
  100.9 0.0 copy-done.2
  100.9 0.0 copy-done.5
  100.9 0.0 copy-start.4
  100.9 0.6 convolution_add_fusion
  101.5 0.2 copy-done.4
  101.7 4.9 %all_to_all.15 = f32[2,128,512]{2,1,0:T(8,128)} all-to-all(f32[2,128,512]{2,1,0:T(8,128)S(1)} %bitcast.55), channel_id=1, replica_groups=mesh['wide'=64,'narrow'=2] {'narrow'}, dimensions={0} | all-to-all | bytes 1048576 | tf_op jit(solution)/shard_map/all_to_all | solution.py:38
  106.6 1.8 reduce_sum.38
  108.4 0.0 copy-done.7
  108.4 1.8 multiply_convert_fusion
  110.2 2.2 all_gather.7
  112.4 1.7 fusion.18
  114.0 14.9 %convolution_convert_fusion = bf16[8192,512]{1,0:T(8,128)(2,1)} fusion(bf16[256,512]{1,0:T(8,128)(2,1)S(1)} %all_gather.7, bf16[32,8,64,128]{3,2,1,0:T(8,128)(2,1)} %bitcast.54), kind=kOutput, calls=%fused_computation.1 | convolution fusion | flops 2151677952 | bytes 12845056 | tf_op jit(solution)/shard_map/dot_general | solution.py:46
  129.0 1.1 fusion.9
  130.1 7.9 %pad_maximum_fusion = bf16[64,136,512]{2,1,0:T(8,128)(2,1)} fusion(bf16[64,8,512]{2,1,0:T(8,128)(2,1)} %fusion.9, bf16[64,128,512]{2,1,0:T(8,128)(2,1)} %bitcast.52), kind=kLoop, calls=%fused_computation.2 | loop fusion | flops 17825792 | bytes 17825792 | tf_op jit(solution)/shard_map/concatenate | solution.py:56
  138.0 112.5 %all_to_all.16 = bf16[64,136,512]{2,1,0:T(8,128)(2,1)S(1)} all-to-all(bf16[64,136,512]{2,1,0:T(8,128)(2,1)} %pad_maximum_fusion), channel_id=1, replica_groups=mesh['wide'=64,'narrow'=2] {'wide'}, dimensions={0} | all-to-all | bytes 17825792 | tf_op jit(solution)/shard_map/all_to_all | solution.py:60
  250.4 0.0 copy-start.1
  250.4 3.4 %copy-done.1 = bf16[64,136,512]{2,1,0:T(8,128)(2,1)} copy-done((bf16[64,136,512]{2,1,0:T(8,128)(2,1)}, bf16[64,136,512]{2,1,0:T(8,128)(2,1)S(1)}, u32[]{:S(2)}) %copy-start.1) | copy-done | bytes 8912920
  253.8 0.1 convert_reduce_fusion.1
  253.9 3.4 %psum.15 = bf16[8,512]{1,0:T(8,128)(2,1)S(1)} all-reduce(f32[8,512]{1,0:T(8,128)S(1)} %convert_reduce_fusion.1), channel_id=1, replica_groups=mesh['wide'=64,'narrow'=2] {'narrow'}, use_global_device_ids=true, to_apply=%region_5.6 | all-reduce | flops 4096 | bytes 24576 | tf_op jit(solution)/shard_map/psum | solution.py:62
  257.3 0.8 broadcast_in_dim.2
  258.1 8.9 %all-to-all-start.2 = ((bf16[64,8,512]{2,1,0:T(8,128)(2,1)}), bf16[64,8,512]{2,1,0:T(8,128)(2,1)}, u32[]{:S(2)}, u32[]{:S(2)}) async-start(bf16[64,8,512]{2,1,0:T(8,128)(2,1)} %broadcast_in_dim.2), calls=%async_computation.2 | async-start | bytes 1048576 | tf_op jit(solution)/shard_map/all_to_all | solution.py:63
  267.0 0.0 copy-start.3
  267.0 4.8 %convert_reduce_fusion = f32[128,512]{1,0:T(8,128)S(1)} fusion(bf16[64,136,512]{2,1,0:T(8,128)(2,1)} %copy-done.1), kind=kLoop, calls=%fused_computation | loop fusion | flops 8323072 | bytes 8650752 | tf_op jit(solution)/shard_map/reduce_sum | solution.py:66
  271.9 0.0 copy-done.3
  271.9 1.0 convolution_convert_fusion.1
  272.9 7.6 %all-to-all-done.2 = bf16[64,8,512]{2,1,0:T(8,128)(2,1)} async-done(((bf16[64,8,512]{2,1,0:T(8,128)(2,1)}), bf16[64,8,512]{2,1,0:T(8,128)(2,1)}, u32[]{:S(2)}, u32[]{:S(2)}) %all-to-all-start.2) | async-done | bytes 524320 | tf_op jit(solution)/shard_map/all_to_all | solution.py:63
  280.5 2.1 bitcast_convert_fusion.1
  (2 shorter events, 0.0 us)
Async XLA Ops:
  7.2 1.9 copy-start
  7.2 84.6 %all-gather.2.cloned.1.call-start = ((), (), s32[]{:S(2)}) async-start(), calls=%async_computation.3 | async-start | bytes 8519680 | tf_op jit(solution)/shard_map/all_gather | solution.py:16
  9.1 9.4 %copy-start.6 = (bf16[128,512]{1,0:T(8,128)(2,1)S(1)}, bf16[128,512]{1,0:T(8,128)(2,1)}, u32[]{:S(2)}) copy-start(bf16[128,512]{1,0:T(8,128)(2,1)} %param.6) | copy-start | bytes 393220
  91.8 9.1 %copy-start.2 = (bf16[512,512]{1,0:T(8,128)(2,1)S(1)}, bf16[512,512]{1,0:T(8,128)(2,1)}, u32[]{:S(2)}) copy-start(bf16[512,512]{1,0:T(8,128)(2,1)} %param.7) | copy-start | bytes 1572868
  91.8 9.1 %copy-start.5 = (f32[256,512]{1,0:T(8,128)S(1)}, f32[256,512]{1,0:T(8,128)}, u32[]{:S(2)}) copy-start(f32[256,512]{1,0:T(8,128)} %bitcast_multiply_fusion) | copy-start | bytes 1572868
  91.8 16.6 %copy-start.7 = (bf16[128,512]{1,0:T(8,128)(2,1)S(1)}, bf16[128,512]{1,0:T(8,128)(2,1)}, u32[]{:S(2)}) copy-start(bf16[128,512]{1,0:T(8,128)(2,1)} %param.11) | copy-start | bytes 393220
  100.9 0.8 copy-start.4
  250.4 3.4 %copy-start.1 = (bf16[64,136,512]{2,1,0:T(8,128)(2,1)}, bf16[64,136,512]{2,1,0:T(8,128)(2,1)S(1)}, u32[]{:S(2)}) copy-start(bf16[64,136,512]{2,1,0:T(8,128)(2,1)S(1)} %all_to_all.16) | copy-start | bytes 26738692
  258.1 22.3 %all-to-all-start.2 = ((bf16[64,8,512]{2,1,0:T(8,128)(2,1)}), bf16[64,8,512]{2,1,0:T(8,128)(2,1)}, u32[]{:S(2)}, u32[]{:S(2)}) async-start(bf16[64,8,512]{2,1,0:T(8,128)(2,1)} %broadcast_in_dim.2), calls=%async_computation.2 | async-start | bytes 1048576 | tf_op jit(solution)/shard_map/all_to_all | solution.py:63
  267.0 4.9 %copy-start.3 = (bf16[512,512]{1,0:T(8,128)(2,1)S(1)}, bf16[512,512]{1,0:T(8,128)(2,1)}, u32[]{:S(2)}) copy-start(bf16[512,512]{1,0:T(8,128)(2,1)} %param.7) | copy-start | bytes 1572868
Sparse Core Ops, SparseCore 0:
  10.9 80.8 all-gather.1

commit v12 on v4

--- a/solution.py
+++ b/solution.py
@@ -69,10 +69,10 @@
         + received[:, tile + rows:].astype(jnp.float32),
         axis=0,
     )
-    band = lax.psum(band, "narrow")
+    band = lax.psum(band, "narrow").astype(jnp.bfloat16)
     grad_weight = lax.all_to_all(
         jnp.broadcast_to(band[None], (owners, rows, width)), "wide", 0, 0, tiled=True
-    ).reshape(width, width)
+    ).reshape(width, width).astype(jnp.float32)
     gathered_sum = jnp.sum(received[:, :tile].astype(jnp.float32), axis=0)
     message = (gathered_sum + own_grad.astype(jnp.float32)).astype(jnp.bfloat16)
     grad_features = lax.dot_general(

time: 290 us -> 285 us (0.983)
  waiting for transfers between devices: 84.8 us -> 79.4 us
    all_to_all x1, waiting for transfers between devices: 13.1 us -> 7.62 us  [per_device(): lax.all_to_all(jnp.broadcast_to(band[None], (owners, rows, width)), 'wide...]
    unnamed x17 -> x16, local copies, waits for them, and re-layouts: 6.33 us -> 4.06 us
  transfers between devices with their start and end apart: 2 -> 2, of which waited for: 2 -> 2; matrix products, arithmetic and copies ran while one was open for 5% -> 6% of each run, Pallas kernels for 0% -> 0%
where the time goes in v12:
time: 285 us; the launch traced here: 284 us
  blocking collectives  131 us (46%)
  waiting for transfers between devices  79.4 us (28%)
  matrix products  31.4 us (11%)
  other arithmetic  14.4 us (5%)
  between operations  14.1 us (5%)
  starting transfers between devices  8.84 us (3%)
  local copies, waits for them, and re-layouts  5.04 us (2%)
    all_to_all x1, blocking collectives, per_device(): received = lax.all_to_all(payload, 'wide', 0, 0, tiled=True)  118 us
    all_gather x1, waiting for transfers between devices, per_device(): gathered_features = lax.all_gather(features, 'wide', axis=0, tiled=True)  71.1 us
    dot_general x1, matrix products, per_device(): lax.dot_general(panel, all_grad, (((0,), (0,)), ((), ())), preferred_elem...  11.7 us
    dot_general x1, matrix products, per_device(): jnp.dot(panel, gathered_features, preferred_element_type=jnp.float32)  9.13 us
    all_to_all x1, starting transfers between devices, per_device(): lax.all_to_all(jnp.broadcast_to(band[None], (owners, rows, width)), 'wide...  8.8 us
    all_to_all x1, waiting for transfers between devices, per_device(): lax.all_to_all(jnp.broadcast_to(band[None], (owners, rows, width)), 'wide...  7.62 us
    dot_general x1, matrix products, per_device(): jnp.einsum('skj,sktc->stjc', onehot, tiles, preferred_element_type=jnp.fl...  5.73 us
  transfers between devices with their start and end apart: 2, of which 2 were waited for; matrix products, arithmetic and copies ran while one was open for 6% of the time, Pallas kernels for 0%

profile of v12, /device:TPU:0, one launch (start us, length us, event | category | flops | bytes accessed | tf_op | source)
XLA Modules:
  0.0 284.1 jit_solution(4881337958595297857)
XLA Ops:
  7.2 0.0 copy-start
  7.2 0.0 all-gather.2.cloned.1.call-start
  7.2 0.7 all-gather.2.cloned.1.call-update
  7.9 0.9 compare_convert_fusion.1
  8.8 0.2 copy-done
  9.1 0.0 copy-start.6
  9.1 5.7 %bitcast_convert_fusion = (bf16[2,128,64,128]{3,2,1,0:T(8,128)(2,1)}, f32[2,64,128,128]{3,1,2,0:T(8,128)S(1)}) fusion(bf16[2,48,128,128]{3,2,1,0:T(8,128)(2,1)S(1)} %bitcast.51, s32[2,48]{1,0:T(2,128)} %bitcast.56, bf16[2,48]{1,0:T(2,128)(2,1)S(1)} %compare_convert_fusion.1), kind=kOutput, calls=%fused_computation.4 | convolution fusion | flops 203436032 | bytes 15729216 | tf_op jit(solution)/shard_map/skj,sktc->stjc/dot_general | solution.py:21
  14.8 1.1 bitcast_reduce_fusion
  15.9 2.5 psum.14
  18.4 0.1 dynamic_slice.3
  18.4 0.1 broadcast_bitcast_fusion
  18.5 0.0 copy-done.6
  18.5 1.3 fusion.8
  19.8 0.9 bitcast_multiply_fusion
  20.7 71.1 %all-gather.2.cloned.1.call-done = bf16[8192,512]{1,0:T(8,128)(2,1)} async-done(((bf16[128,512]{1,0:T(8,128)(2,1)}), bf16[8192,512]{1,0:T(8,128)(2,1)}) %all-gather.2.cloned.1.call-update) | async-done | bytes 8388624 | tf_op jit(solution)/shard_map/all_gather | solution.py:16
  91.8 0.0 copy-start.2
  91.8 0.0 copy-start.5
  91.8 0.0 copy-start.7
  91.8 9.1 %fusion.1 = f32[256,512]{1,0:T(8,128)S(1)} fusion(bf16[8192,512]{1,0:T(8,128)(2,1)} %all-gather.2.cloned.1.call-done, bf16[32,8,64,128]{3,2,1,0:T(8,128)(2,1)} %bitcast.53), kind=kOutput, calls=%fused_computation.6 | convolution fusion | flops 2147483648 | bytes 13107200 | tf_op jit(solution)/shard_map/dot_general | solution.py:29
  100.9 0.0 copy-done.2
  100.9 0.0 copy-done.5
  100.9 0.0 copy-start.4
  100.9 0.6 convolution_add_fusion
  101.5 0.2 copy-done.4
  101.7 4.9 %all_to_all.15 = f32[2,128,512]{2,1,0:T(8,128)} all-to-all(f32[2,128,512]{2,1,0:T(8,128)S(1)} %bitcast.55), channel_id=1, replica_groups=mesh['wide'=64,'narrow'=2] {'narrow'}, dimensions={0} | all-to-all | bytes 1048576 | tf_op jit(solution)/shard_map/all_to_all | solution.py:38
  106.6 1.8 reduce_sum.38
  108.4 0.0 copy-done.7
  108.4 1.8 multiply_convert_fusion
  110.2 2.2 all_gather.7
  112.4 1.7 fusion.17
  114.0 11.7 %convolution_convert_fusion = bf16[8192,512]{1,0:T(8,128)(2,1)S(1)} fusion(bf16[256,512]{1,0:T(8,128)(2,1)S(1)} %all_gather.7, bf16[32,8,64,128]{3,2,1,0:T(8,128)(2,1)} %bitcast.54), kind=kOutput, calls=%fused_computation.1 | convolution fusion | flops 2151677952 | bytes 12845056 | tf_op jit(solution)/shard_map/dot_general | solution.py:46
  125.7 0.3 convert_bitcast_fusion
  126.1 0.7 pad_maximum_fusion
  126.8 118.0 %all_to_all.16 = bf16[64,144,512]{2,1,0:T(8,128)(2,1)S(1)} all-to-all(bf16[64,144,512]{2,1,0:T(8,128)(2,1)S(1)} %pad_maximum_fusion), channel_id=1, replica_groups=mesh['wide'=64,'narrow'=2] {'wide'}, dimensions={0} | all-to-all | bytes 18874368 | tf_op jit(solution)/shard_map/all_to_all | solution.py:66
  244.8 0.0 copy-start.1
  244.8 3.6 %copy-done.1 = bf16[64,144,512]{2,1,0:T(8,128)(2,1)} copy-done((bf16[64,144,512]{2,1,0:T(8,128)(2,1)}, bf16[64,144,512]{2,1,0:T(8,128)(2,1)S(1)}, u32[]{:S(2)}) %copy-start.1) | copy-done | bytes 9437208
  248.5 0.2 add_reduce_fusion
  248.6 3.4 %psum.15 = bf16[8,512]{1,0:T(8,128)(2,1)S(1)} all-reduce(f32[8,512]{1,0:T(8,128)S(1)} %add_reduce_fusion), channel_id=1, replica_groups=mesh['wide'=64,'narrow'=2] {'narrow'}, use_global_device_ids=true, to_apply=%region_5.6 | all-reduce | flops 4096 | bytes 24576 | tf_op jit(solution)/shard_map/psum | solution.py:72
  252.0 0.8 broadcast_in_dim.2
  252.8 8.8 %all-to-all-start.2 = ((bf16[64,8,512]{2,1,0:T(8,128)(2,1)}), bf16[64,8,512]{2,1,0:T(8,128)(2,1)}, u32[]{:S(2)}, u32[]{:S(2)}) async-start(bf16[64,8,512]{2,1,0:T(8,128)(2,1)} %broadcast_in_dim.2), calls=%async_computation.2 | async-start | bytes 1048576 | tf_op jit(solution)/shard_map/all_to_all | solution.py:73
  261.6 0.0 copy-start.3
  261.6 4.8 %convert_reduce_fusion = f32[128,512]{1,0:T(8,128)S(1)} fusion(bf16[64,144,512]{2,1,0:T(8,128)(2,1)} %copy-done.1), kind=kLoop, calls=%fused_computation | loop fusion | flops 8323072 | bytes 8650752 | tf_op jit(solution)/shard_map/reduce_sum | solution.py:76
  266.5 0.0 copy-done.3
  266.5 1.0 convolution_convert_fusion.1
  267.5 7.6 %all-to-all-done.2 = bf16[64,8,512]{2,1,0:T(8,128)(2,1)} async-done(((bf16[64,8,512]{2,1,0:T(8,128)(2,1)}), bf16[64,8,512]{2,1,0:T(8,128)(2,1)}, u32[]{:S(2)}, u32[]{:S(2)}) %all-to-all-start.2) | async-done | bytes 524320 | tf_op jit(solution)/shard_map/all_to_all | solution.py:73
  275.1 2.1 bitcast_convert_fusion.1
  (2 shorter events, 0.0 us)
Async XLA Ops:
  7.2 1.9 copy-start
  7.2 84.6 %all-gather.2.cloned.1.call-start = ((), (), s32[]{:S(2)}) async-start(), calls=%async_computation.3 | async-start | bytes 8519680 | tf_op jit(solution)/shard_map/all_gather | solution.py:16
  9.1 9.4 %copy-start.6 = (bf16[128,512]{1,0:T(8,128)(2,1)S(1)}, bf16[128,512]{1,0:T(8,128)(2,1)}, u32[]{:S(2)}) copy-start(bf16[128,512]{1,0:T(8,128)(2,1)} %param.6) | copy-start | bytes 393220
  91.8 9.1 %copy-start.2 = (bf16[512,512]{1,0:T(8,128)(2,1)S(1)}, bf16[512,512]{1,0:T(8,128)(2,1)}, u32[]{:S(2)}) copy-start(bf16[512,512]{1,0:T(8,128)(2,1)} %param.7) | copy-start | bytes 1572868
  91.8 9.1 %copy-start.5 = (f32[256,512]{1,0:T(8,128)S(1)}, f32[256,512]{1,0:T(8,128)}, u32[]{:S(2)}) copy-start(f32[256,512]{1,0:T(8,128)} %bitcast_multiply_fusion) | copy-start | bytes 1572868
  91.8 16.6 %copy-start.7 = (bf16[128,512]{1,0:T(8,128)(2,1)S(1)}, bf16[128,512]{1,0:T(8,128)(2,1)}, u32[]{:S(2)}) copy-start(bf16[128,512]{1,0:T(8,128)(2,1)} %param.11) | copy-start | bytes 393220
  100.9 0.8 copy-start.4
  244.8 3.6 %copy-start.1 = (bf16[64,144,512]{2,1,0:T(8,128)(2,1)}, bf16[64,144,512]{2,1,0:T(8,128)(2,1)S(1)}, u32[]{:S(2)}) copy-start(bf16[64,144,512]{2,1,0:T(8,128)(2,1)S(1)} %all_to_all.16) | copy-start | bytes 28311556
  252.8 22.3 %all-to-all-start.2 = ((bf16[64,8,512]{2,1,0:T(8,128)(2,1)}), bf16[64,8,512]{2,1,0:T(8,128)(2,1)}, u32[]{:S(2)}, u32[]{:S(2)}) async-start(bf16[64,8,512]{2,1,0:T(8,128)(2,1)} %broadcast_in_dim.2), calls=%async_computation.2 | async-start | bytes 1048576 | tf_op jit(solution)/shard_map/all_to_all | solution.py:73
  261.6 4.9 %copy-start.3 = (bf16[512,512]{1,0:T(8,128)(2,1)S(1)}, bf16[512,512]{1,0:T(8,128)(2,1)}, u32[]{:S(2)}) copy-start(bf16[512,512]{1,0:T(8,128)(2,1)} %param.7) | copy-start | bytes 1572868
Sparse Core Ops, SparseCore 0:
  10.9 80.8 all-gather.1

commit v13 on v12

--- a/solution.py
+++ b/solution.py
@@ -69,7 +69,10 @@
         + received[:, tile + rows:].astype(jnp.float32),
         axis=0,
     )
-    band = lax.psum(band, "narrow").astype(jnp.bfloat16)
+    pair = lax.axis_size("narrow")
+    band = (band + lax.ppermute(band, "narrow", [(i, pair - 1 - i) for i in range(pair)])).astype(
+        jnp.bfloat16
+    )
     grad_weight = lax.all_to_all(
         jnp.broadcast_to(band[None], (owners, rows, width)), "wide", 0, 0, tiled=True
     ).reshape(width, width).astype(jnp.float32)

time: 285 us -> 283 us (level)
  blocking collectives: 131 us -> 127 us
    psum x1 -> x0, blocking collectives: 3.37 us -> none  [per_device(): band = lax.psum(band, 'narrow').astype(jnp.bfloat16)]
  transfers between devices with their start and end apart: 2 -> 3, of which waited for: 2 -> 3; matrix products, arithmetic and copies ran while one was open for 6% -> 6% of each run, Pallas kernels for 0% -> 0%
where the time goes in v13:
time: 283 us; the launch traced here: 282 us
  blocking collectives  127 us (45%)
  waiting for transfers between devices  80.4 us (28%)
  matrix products  31.4 us (11%)
  other arithmetic  14.4 us (5%)
  between operations  14.1 us (5%)
  starting transfers between devices  9.38 us (3%)
  local copies, waits for them, and re-layouts  5.04 us (2%)
    all_to_all x1, blocking collectives, per_device(): received = lax.all_to_all(payload, 'wide', 0, 0, tiled=True)  118 us
    all_gather x1, waiting for transfers between devices, per_device(): gathered_features = lax.all_gather(features, 'wide', axis=0, tiled=True)  71.1 us
    dot_general x1, matrix products, per_device(): lax.dot_general(panel, all_grad, (((0,), (0,)), ((), ())), preferred_elem...  11.7 us
    all_to_all x1, starting transfers between devices, per_device(): lax.all_to_all(jnp.broadcast_to(band[None], (owners, rows, width)), 'wide...  9.26 us
    dot_general x1, matrix products, per_device(): jnp.dot(panel, gathered_features, preferred_element_type=jnp.float32)  9.13 us
    all_to_all x1, waiting for transfers between devices, per_device(): lax.all_to_all(jnp.broadcast_to(band[None], (owners, rows, width)), 'wide...  7.44 us
    dot_general x1, matrix products, per_device(): jnp.einsum('skj,sktc->stjc', onehot, tiles, preferred_element_type=jnp.fl...  5.71 us
  transfers between devices with their start and end apart: 3, of which 3 were waited for; matrix products, arithmetic and copies ran while one was open for 6% of the time, Pallas kernels for 0%

profile of v13, /device:TPU:0, one launch (start us, length us, event | category | flops | bytes accessed | tf_op | source)
XLA Modules:
  0.0 282.1 jit_solution(14058284336426943415)
XLA Ops:
  7.2 0.0 copy-start
  7.2 0.0 all-gather.2.cloned.1.call-start
  7.2 0.7 all-gather.2.cloned.1.call-update
  7.9 0.9 compare_convert_fusion.1
  8.8 0.2 copy-done
  9.1 0.0 copy-start.6
  9.1 5.7 %bitcast_convert_fusion = (bf16[2,128,64,128]{3,2,1,0:T(8,128)(2,1)}, f32[2,64,128,128]{3,1,2,0:T(8,128)S(1)}) fusion(bf16[2,48,128,128]{3,2,1,0:T(8,128)(2,1)S(1)} %bitcast.51, s32[2,48]{1,0:T(2,128)} %bitcast.56, bf16[2,48]{1,0:T(2,128)(2,1)S(1)} %compare_convert_fusion.1), kind=kOutput, calls=%fused_computation.4 | convolution fusion | flops 203436032 | bytes 15729216 | tf_op jit(solution)/shard_map/skj,sktc->stjc/dot_general | solution.py:21
  14.8 1.1 bitcast_reduce_fusion
  15.9 2.5 psum.7
  18.3 0.1 dynamic_slice.3
  18.4 0.1 broadcast_bitcast_fusion
  18.5 0.0 copy-done.6
  18.5 1.3 fusion.8
  19.8 0.9 bitcast_multiply_fusion
  20.7 71.1 %all-gather.2.cloned.1.call-done = bf16[8192,512]{1,0:T(8,128)(2,1)} async-done(((bf16[128,512]{1,0:T(8,128)(2,1)}), bf16[8192,512]{1,0:T(8,128)(2,1)}) %all-gather.2.cloned.1.call-update) | async-done | bytes 8388624 | tf_op jit(solution)/shard_map/all_gather | solution.py:16
  91.8 0.0 copy-start.2
  91.8 0.0 copy-start.5
  91.8 0.0 copy-start.7
  91.8 9.1 %fusion.1 = f32[256,512]{1,0:T(8,128)S(1)} fusion(bf16[8192,512]{1,0:T(8,128)(2,1)} %all-gather.2.cloned.1.call-done, bf16[32,8,64,128]{3,2,1,0:T(8,128)(2,1)} %bitcast.53), kind=kOutput, calls=%fused_computation.6 | convolution fusion | flops 2147483648 | bytes 13107200 | tf_op jit(solution)/shard_map/dot_general | solution.py:29
  100.9 0.0 copy-done.2
  100.9 0.0 copy-done.5
  100.9 0.0 copy-start.4
  100.9 0.6 convolution_add_fusion
  101.5 0.2 copy-done.4
  101.7 4.9 %all_to_all.15 = f32[2,128,512]{2,1,0:T(8,128)} all-to-all(f32[2,128,512]{2,1,0:T(8,128)S(1)} %bitcast.55), channel_id=1, replica_groups=mesh['wide'=64,'narrow'=2] {'narrow'}, dimensions={0} | all-to-all | bytes 1048576 | tf_op jit(solution)/shard_map/all_to_all | solution.py:38
  106.6 1.8 reduce_sum.38
  108.4 0.0 copy-done.7
  108.4 1.8 multiply_convert_fusion
  110.2 2.2 all_gather.7
  112.4 1.7 fusion.17
  114.0 11.7 %convolution_convert_fusion = bf16[8192,512]{1,0:T(8,128)(2,1)S(1)} fusion(bf16[256,512]{1,0:T(8,128)(2,1)S(1)} %all_gather.7, bf16[32,8,64,128]{3,2,1,0:T(8,128)(2,1)} %bitcast.54), kind=kOutput, calls=%fused_computation.1 | convolution fusion | flops 2151677952 | bytes 12845056 | tf_op jit(solution)/shard_map/dot_general | solution.py:46
  125.7 0.3 convert_bitcast_fusion
  126.1 0.7 pad_maximum_fusion
  126.8 117.9 %all_to_all.16 = bf16[64,144,512]{2,1,0:T(8,128)(2,1)S(1)} all-to-all(bf16[64,144,512]{2,1,0:T(8,128)(2,1)S(1)} %pad_maximum_fusion), channel_id=1, replica_groups=mesh['wide'=64,'narrow'=2] {'wide'}, dimensions={0} | all-to-all | bytes 18874368 | tf_op jit(solution)/shard_map/all_to_all | solution.py:66
  244.7 0.0 copy-start.1
  244.7 3.6 %copy-done.1 = bf16[64,144,512]{2,1,0:T(8,128)(2,1)} copy-done((bf16[64,144,512]{2,1,0:T(8,128)(2,1)}, bf16[64,144,512]{2,1,0:T(8,128)(2,1)S(1)}, u32[]{:S(2)}) %copy-start.1) | copy-done | bytes 9437208
  248.4 0.2 add_reduce_fusion
  248.5 0.1 collective-permute-start
  248.6 1.2 collective-permute-done
  249.8 0.8 broadcast_in_dim.2
  250.6 9.3 %all-to-all-start.2 = ((bf16[64,8,512]{2,1,0:T(8,128)(2,1)}), bf16[64,8,512]{2,1,0:T(8,128)(2,1)}, u32[]{:S(2)}, u32[]{:S(2)}) async-start(bf16[64,8,512]{2,1,0:T(8,128)(2,1)} %broadcast_in_dim.2), calls=%async_computation.2 | async-start | bytes 1048576 | tf_op jit(solution)/shard_map/all_to_all | solution.py:76
  259.9 0.0 copy-start.3
  259.9 4.8 %convert_reduce_fusion = f32[128,512]{1,0:T(8,128)S(1)} fusion(bf16[64,144,512]{2,1,0:T(8,128)(2,1)} %copy-done.1), kind=kLoop, calls=%fused_computation | loop fusion | flops 8323072 | bytes 8650752 | tf_op jit(solution)/shard_map/reduce_sum | solution.py:79
  264.7 0.0 copy-done.3
  264.7 1.0 convolution_convert_fusion.1
  265.7 7.4 %all-to-all-done.2 = bf16[64,8,512]{2,1,0:T(8,128)(2,1)} async-done(((bf16[64,8,512]{2,1,0:T(8,128)(2,1)}), bf16[64,8,512]{2,1,0:T(8,128)(2,1)}, u32[]{:S(2)}, u32[]{:S(2)}) %all-to-all-start.2) | async-done | bytes 524320 | tf_op jit(solution)/shard_map/all_to_all | solution.py:76
  273.2 2.1 bitcast_convert_fusion.1
  (3 shorter events, 0.0 us)
Async XLA Ops:
  7.2 1.9 copy-start
  7.2 84.6 %all-gather.2.cloned.1.call-start = ((), (), s32[]{:S(2)}) async-start(), calls=%async_computation.3 | async-start | bytes 8519680 | tf_op jit(solution)/shard_map/all_gather | solution.py:16
  9.1 9.4 %copy-start.6 = (bf16[128,512]{1,0:T(8,128)(2,1)S(1)}, bf16[128,512]{1,0:T(8,128)(2,1)}, u32[]{:S(2)}) copy-start(bf16[128,512]{1,0:T(8,128)(2,1)} %param.6) | copy-start | bytes 393220
  91.8 9.1 %copy-start.2 = (bf16[512,512]{1,0:T(8,128)(2,1)S(1)}, bf16[512,512]{1,0:T(8,128)(2,1)}, u32[]{:S(2)}) copy-start(bf16[512,512]{1,0:T(8,128)(2,1)} %param.7) | copy-start | bytes 1572868
  91.8 9.1 %copy-start.5 = (f32[256,512]{1,0:T(8,128)S(1)}, f32[256,512]{1,0:T(8,128)}, u32[]{:S(2)}) copy-start(f32[256,512]{1,0:T(8,128)} %bitcast_multiply_fusion) | copy-start | bytes 1572868
  91.8 16.6 %copy-start.7 = (bf16[128,512]{1,0:T(8,128)(2,1)S(1)}, bf16[128,512]{1,0:T(8,128)(2,1)}, u32[]{:S(2)}) copy-start(bf16[128,512]{1,0:T(8,128)(2,1)} %param.11) | copy-start | bytes 393220
  100.9 0.8 copy-start.4
  244.7 3.6 %copy-start.1 = (bf16[64,144,512]{2,1,0:T(8,128)(2,1)}, bf16[64,144,512]{2,1,0:T(8,128)(2,1)S(1)}, u32[]{:S(2)}) copy-start(bf16[64,144,512]{2,1,0:T(8,128)(2,1)S(1)} %all_to_all.16) | copy-start | bytes 28311556
  248.5 1.3 collective-permute-start
  250.6 22.5 %all-to-all-start.2 = ((bf16[64,8,512]{2,1,0:T(8,128)(2,1)}), bf16[64,8,512]{2,1,0:T(8,128)(2,1)}, u32[]{:S(2)}, u32[]{:S(2)}) async-start(bf16[64,8,512]{2,1,0:T(8,128)(2,1)} %broadcast_in_dim.2), calls=%async_computation.2 | async-start | bytes 1048576 | tf_op jit(solution)/shard_map/all_to_all | solution.py:76
  259.9 4.9 %copy-start.3 = (bf16[512,512]{1,0:T(8,128)(2,1)S(1)}, bf16[512,512]{1,0:T(8,128)(2,1)}, u32[]{:S(2)}) copy-start(bf16[512,512]{1,0:T(8,128)(2,1)} %param.7) | copy-start | bytes 1572868
Sparse Core Ops, SparseCore 0:
  10.9 80.8 all-gather.1

commit v14 on v10

--- a/solution.py
+++ b/solution.py
@@ -24,6 +24,7 @@
     degree = 1.0 + lax.psum(jnp.sum(dense, axis=1), "narrow")
     scale = lax.rsqrt(degree)
     panel = dense.astype(jnp.bfloat16)
+    panel, scale = lax.optimization_barrier((panel, scale))
     projected = jnp.dot(features, weight, preferred_element_type=jnp.float32).astype(jnp.bfloat16)
     own = lax.axis_index("narrow")
     aggregated = jnp.dot(panel, gathered_features, preferred_element_type=jnp.float32)
@@ -72,10 +73,12 @@
         + received[:, tile + rows:].astype(jnp.float32),
         axis=0,
     )
-    band = lax.psum(band, "narrow")
+    band = (band + lax.ppermute(band, "narrow", [(i, pair - 1 - i) for i in range(pair)])).astype(
+        jnp.bfloat16
+    )
     grad_weight = lax.all_to_all(
         jnp.broadcast_to(band[None], (owners, rows, width)), "wide", 0, 0, tiled=True
-    ).reshape(width, width)
+    ).reshape(width, width).astype(jnp.float32)
     gathered_sum = jnp.sum(received[:, :tile].astype(jnp.float32), axis=0)
     message = (gathered_sum + own_grad.astype(jnp.float32)).astype(jnp.bfloat16)
     grad_features = lax.dot_general(

time: 291 us -> 270 us (0.928)
  waiting for transfers between devices: 88.6 us -> 74 us
  matrix products: 31.7 us -> 20.1 us
  local copies, waits for them, and re-layouts: 8.14 us -> 16 us
  starting transfers between devices: 13.4 us -> 9.38 us
  other arithmetic: 9.28 us -> 12.9 us
  blocking collectives: 126 us -> 123 us
    all_gather x1, waiting for transfers between devices: 74.8 us -> 62.9 us  [per_device(): gathered_features = lax.all_gather(features, 'wide', axis=0, tiled=True)]
    unnamed x19, local copies, waits for them, and re-layouts: 6.88 us -> 14.3 us
    dot_general x1, matrix products: 11.7 us -> 4.57 us  [per_device(): lax.dot_general(panel, all_grad, (((0,), (0,)), ((), ())), preferred_elem...]
    all_to_all x1, waiting for transfers between devices: 13.1 us -> 7.44 us  [per_device(): lax.all_to_all(jnp.broadcast_to(band[None], (owners, rows, width)), 'wide...]
    all_to_all x1, starting transfers between devices: 13.3 us -> 9.26 us  [per_device(): lax.all_to_all(jnp.broadcast_to(band[None], (owners, rows, width)), 'wide...]
    psum x1 -> x0, blocking collectives: 3.36 us -> none  [per_device(): band = lax.psum(band, 'narrow')]
  transfers between devices with their start and end apart: 3 -> 4, of which waited for: 2 -> 4; matrix products, arithmetic and copies ran while one was open for 5% -> 9% of each run, Pallas kernels for 0% -> 0%
where the time goes in v14:
time: 270 us; the launch traced here: 269 us
  blocking collectives  123 us (46%)
  waiting for transfers between devices  74 us (27%)
  matrix products  20.1 us (7%)
  local copies, waits for them, and re-layouts  16 us (6%)
  between operations  14.2 us (5%)
  other arithmetic  12.9 us (5%)
  starting transfers between devices  9.38 us (3%)
    all_to_all x1, blocking collectives, per_device(): received = lax.all_to_all(payload, 'wide', 0, 0, tiled=True)  118 us
    all_gather x1, waiting for transfers between devices, per_device(): gathered_features = lax.all_gather(features, 'wide', axis=0, tiled=True)  62.9 us
    unnamed x19, local copies, waits for them, and re-layouts  14.3 us
    all_to_all x1, starting transfers between devices, per_device(): lax.all_to_all(jnp.broadcast_to(band[None], (owners, rows, width)), 'wide...  9.26 us
    all_to_all x1, waiting for transfers between devices, per_device(): lax.all_to_all(jnp.broadcast_to(band[None], (owners, rows, width)), 'wide...  7.44 us
    dot_general x1, matrix products, per_device(): jnp.dot(panel, gathered_features, preferred_element_type=jnp.float32)  7.05 us
  transfers between devices with their start and end apart: 4, of which 4 were waited for; matrix products, arithmetic and copies ran while one was open for 9% of the time, Pallas kernels for 0%

profile of v14, /device:TPU:0, one launch (start us, length us, event | category | flops | bytes accessed | tf_op | source)
XLA Modules:
  0.0 269.1 jit_solution(8017786079868260769)
XLA Ops:
  7.2 0.0 copy-start
  7.2 0.0 all-gather.2.cloned.1.call-start
  7.2 0.7 all-gather.2.cloned.1.call-update
  7.9 0.9 compare_convert_fusion.1
  8.8 0.2 copy-done
  9.1 3.7 %bitcast_convert_fusion = (bf16[2,128,64,128]{3,2,1,0:T(8,128)(2,1)S(1)}, f32[2,64,128,128]{3,1,2,0:T(8,128)S(1)}) fusion(bf16[2,48,128,128]{3,2,1,0:T(8,128)(2,1)S(1)} %bitcast.50, s32[2,48]{1,0:T(2,128)} %bitcast.55, bf16[2,48]{1,0:T(2,128)(2,1)S(1)} %compare_convert_fusion.1), kind=kOutput, calls=%fused_computation.4 | convolution fusion | flops 203436032 | bytes 15729216 | tf_op jit(solution)/shard_map/skj,sktc->stjc/dot_general | solution.py:21
  12.8 0.0 copy-start.7
  12.8 10.1 %copy.17 = bf16[32,8,64,128]{3,1,2,0:T(8,128)(2,1)} copy(bf16[32,8,64,128]{3,2,1,0:T(8,128)(2,1)S(1)} %bitcast.54) | data formatting | bytes 8388608
  22.9 1.1 bitcast_reduce_fusion
  24.0 2.6 psum.7
  26.6 0.1 broadcast_bitcast_fusion
  26.7 0.0 copy-done.7
  26.7 1.3 fusion.3
  28.0 0.9 bitcast_multiply_fusion
  28.9 0.0 copy-start.8
  28.9 62.9 %all-gather.2.cloned.1.call-done = bf16[8192,512]{1,0:T(8,128)(2,1)} async-done(((bf16[128,512]{1,0:T(8,128)(2,1)}), bf16[8192,512]{1,0:T(8,128)(2,1)}) %all-gather.2.cloned.1.call-update) | async-done | bytes 8388624 | tf_op jit(solution)/shard_map/all_gather | solution.py:16
  91.8 0.0 copy-start.2
  91.8 7.0 %fusion.12 = f32[256,512]{1,0:T(8,128)S(1)} fusion(bf16[256,8192]{1,0:T(8,128)(2,1)} %bitcast.52, bf16[8192,512]{1,0:T(8,128)(2,1)} %all-gather.2.cloned.1.call-done), kind=kOutput, calls=%fused_computation.38 | convolution fusion | flops 2147483648 | bytes 13107200 | tf_op jit(solution)/shard_map/dot_general | solution.py:30
  98.8 0.0 copy-done.2
  98.8 0.0 copy-done.6
  98.8 0.0 copy-start.4
  98.9 0.6 convolution_add_fusion
  99.5 0.2 copy-done.4
  99.6 0.8 constant_dynamic-slice_fusion
  100.4 0.1 copy-done.5
  100.5 0.0 collective-permute-start
  100.5 0.1 dynamic_slice.11
  100.6 1.8 collective-permute-done
  102.4 0.0 copy-done.8
  102.4 1.9 multiply_convert_fusion
  104.3 2.0 all_gather.7
  106.3 1.7 fusion.13
  107.9 4.6 %convolution_convert_fusion = bf16[8192,512]{1,0:T(8,128)(2,1)S(1)} fusion(bf16[256,8192]{1,0:T(8,128)(2,1)} %bitcast.53, bf16[256,512]{1,0:T(8,128)(2,1)S(1)} %all_gather.7), kind=kOutput, calls=%fused_computation.1 | convolution fusion | flops 2151677952 | bytes 12845056 | tf_op jit(solution)/shard_map/dot_general | solution.py:50
  112.5 0.3 convert_bitcast_fusion
  112.9 0.9 pad_maximum_fusion
  113.8 117.9 %all_to_all.10 = bf16[64,144,512]{2,1,0:T(8,128)(2,1)S(1)} all-to-all(bf16[64,144,512]{2,1,0:T(8,128)(2,1)S(1)} %pad_maximum_fusion), channel_id=1, replica_groups=mesh['wide'=64,'narrow'=2] {'wide'}, dimensions={0} | all-to-all | bytes 18874368 | tf_op jit(solution)/shard_map/all_to_all | solution.py:70
  231.7 3.6 %copy-done.1 = bf16[64,144,512]{2,1,0:T(8,128)(2,1)} copy-done((bf16[64,144,512]{2,1,0:T(8,128)(2,1)}, bf16[64,144,512]{2,1,0:T(8,128)(2,1)S(1)}, u32[]{:S(2)}) %copy-start.1) | copy-done | bytes 9437208
  235.3 0.2 add_reduce_fusion
  235.5 0.1 collective-permute-start.1
  235.6 1.2 collective-permute-done.1
  236.7 0.8 broadcast_in_dim.2
  237.6 9.3 %all-to-all-start.1 = ((bf16[64,8,512]{2,1,0:T(8,128)(2,1)}), bf16[64,8,512]{2,1,0:T(8,128)(2,1)}, u32[]{:S(2)}, u32[]{:S(2)}) async-start(bf16[64,8,512]{2,1,0:T(8,128)(2,1)} %broadcast_in_dim.2), calls=%async_computation.1 | async-start | bytes 1048576 | tf_op jit(solution)/shard_map/all_to_all | solution.py:79
  246.8 0.0 copy-start.3
  246.8 4.8 %convert_reduce_fusion = f32[128,512]{1,0:T(8,128)S(1)} fusion(bf16[64,144,512]{2,1,0:T(8,128)(2,1)} %copy-done.1), kind=kLoop, calls=%fused_computation | loop fusion | flops 8323072 | bytes 8650752 | tf_op jit(solution)/shard_map/reduce_sum | solution.py:82
  251.7 0.0 copy-done.3
  251.7 1.0 convolution_convert_fusion.1
  252.7 7.4 %all-to-all-done.1 = bf16[64,8,512]{2,1,0:T(8,128)(2,1)} async-done(((bf16[64,8,512]{2,1,0:T(8,128)(2,1)}), bf16[64,8,512]{2,1,0:T(8,128)(2,1)}, u32[]{:S(2)}, u32[]{:S(2)}) %all-to-all-start.1) | async-done | bytes 524320 | tf_op jit(solution)/shard_map/all_to_all | solution.py:79
  260.1 2.1 bitcast_convert_fusion.1
  (6 shorter events, 0.0 us)
Async XLA Ops:
  7.2 1.9 copy-start
  7.2 84.6 %all-gather.2.cloned.1.call-start = ((), (), s32[]{:S(2)}) async-start(), calls=%async_computation.2 | async-start | bytes 8519680 | tf_op jit(solution)/shard_map/all_gather | solution.py:16
  12.8 14.0 %copy-start.7 = (bf16[128,512]{1,0:T(8,128)(2,1)S(1)}, bf16[128,512]{1,0:T(8,128)(2,1)}, u32[]{:S(2)}) copy-start(bf16[128,512]{1,0:T(8,128)(2,1)} %param.6) | copy-start | bytes 393220
  28.9 73.5 %copy-start.8 = (bf16[128,512]{1,0:T(8,128)(2,1)S(1)}, bf16[128,512]{1,0:T(8,128)(2,1)}, u32[]{:S(2)}) copy-start(bf16[128,512]{1,0:T(8,128)(2,1)} %param.11) | copy-start | bytes 393220
  91.8 7.1 %copy-start.2 = (bf16[512,512]{1,0:T(8,128)(2,1)S(1)}, bf16[512,512]{1,0:T(8,128)(2,1)}, u32[]{:S(2)}) copy-start(bf16[512,512]{1,0:T(8,128)(2,1)} %param.7) | copy-start | bytes 1572868
  91.8 7.1 %copy-start.6 = (f32[256,512]{1,0:T(8,128)S(1)}, f32[256,512]{1,0:T(8,128)}, u32[]{:S(2)}) copy-start(f32[256,512]{1,0:T(8,128)} %bitcast_multiply_fusion) | copy-start | bytes 1572868
  98.8 0.8 copy-start.4
  99.6 0.9 copy-start.5
  100.5 1.9 collective-permute-start
  231.7 3.6 %copy-start.1 = (bf16[64,144,512]{2,1,0:T(8,128)(2,1)}, bf16[64,144,512]{2,1,0:T(8,128)(2,1)S(1)}, u32[]{:S(2)}) copy-start(bf16[64,144,512]{2,1,0:T(8,128)(2,1)S(1)} %all_to_all.10) | copy-start | bytes 28311556
  235.5 1.3 collective-permute-start.1
  237.6 22.5 %all-to-all-start.1 = ((bf16[64,8,512]{2,1,0:T(8,128)(2,1)}), bf16[64,8,512]{2,1,0:T(8,128)(2,1)}, u32[]{:S(2)}, u32[]{:S(2)}) async-start(bf16[64,8,512]{2,1,0:T(8,128)(2,1)} %broadcast_in_dim.2), calls=%async_computation.1 | async-start | bytes 1048576 | tf_op jit(solution)/shard_map/all_to_all | solution.py:79
  246.8 4.9 %copy-start.3 = (bf16[512,512]{1,0:T(8,128)(2,1)S(1)}, bf16[512,512]{1,0:T(8,128)(2,1)}, u32[]{:S(2)}) copy-start(bf16[512,512]{1,0:T(8,128)(2,1)} %param.7) | copy-start | bytes 1572868
Sparse Core Ops, SparseCore 0:
  10.9 80.8 all-gather.1

commit v15 on v8

--- a/solution.py
+++ b/solution.py
@@ -24,6 +24,7 @@
     degree = 1.0 + lax.psum(jnp.sum(dense, axis=1), "narrow")
     scale = lax.rsqrt(degree)
     panel = dense.astype(jnp.bfloat16)
+    panel, scale = lax.optimization_barrier((panel, scale))
     projected = jnp.dot(features, weight, preferred_element_type=jnp.float32).astype(jnp.bfloat16)
     own = lax.axis_index("narrow")
     aggregated = jnp.dot(panel, gathered_features, preferred_element_type=jnp.float32)
@@ -35,14 +36,8 @@
     self_term = selector[:, None, None] * projected.astype(jnp.float32)[None]
     partial_sum = partial_sum + self_term.reshape(copies * tile, width)
     pair = lax.axis_size("narrow")
-    total = jnp.sum(
-        lax.all_to_all(
-            jnp.broadcast_to(partial_sum[None], (pair,) + partial_sum.shape), "narrow", 0, 0,
-            tiled=True,
-        ),
-        axis=0,
-    )
-    preact_both = total * scale[:, None]
+    theirs = lax.ppermute(partial_sum, "narrow", [(i, pair - 1 - i) for i in range(pair)])
+    preact_both = (partial_sum + theirs) * scale[:, None]
     sig = jax.nn.sigmoid(preact_both)
     cot_both = lax.all_gather(cotangent, "narrow", axis=0, tiled=True).astype(jnp.float32)
     all_grad = (
@@ -77,10 +72,12 @@
         + received[:, tile + rows:].astype(jnp.float32),
         axis=0,
     )
-    band = lax.psum(band, "narrow")
+    band = (band + lax.ppermute(band, "narrow", [(i, pair - 1 - i) for i in range(pair)])).astype(
+        jnp.bfloat16
+    )
     grad_weight = lax.all_to_all(
         jnp.broadcast_to(band[None], (owners, rows, width)), "wide", 0, 0, tiled=True
-    ).reshape(width, width)
+    ).reshape(width, width).astype(jnp.float32)
     gathered_sum = jnp.sum(received[:, :tile].astype(jnp.float32), axis=0)
     message = (gathered_sum + own_grad.astype(jnp.float32)).astype(jnp.bfloat16)
     grad_features = lax.dot_general(

time: 291 us -> 268 us (0.921)
  matrix products: 31.8 us -> 20.9 us
  waiting for transfers between devices: 82.2 us -> 71.4 us
  blocking collectives: 131 us -> 123 us
  local copies, waits for them, and re-layouts: 7.42 us -> 14.9 us
    unnamed x17, local copies, waits for them, and re-layouts: 6.12 us -> 14 us
    all_gather x1, waiting for transfers between devices: 70.2 us -> 62.9 us  [per_device(): gathered_features = lax.all_gather(features, 'wide', axis=0, tiled=True)]
    dot_general x1, matrix products: 11.7 us -> 4.57 us  [per_device(): lax.dot_general(panel, all_grad, (((0,), (0,)), ((), ())), preferred_elem...]
    all_to_all x1 -> x0, blocking collectives: 5.36 us -> none  [per_device(): lax.all_to_all(jnp.broadcast_to(partial_sum[None], (pair,) + partial_sum....]
    all_to_all x1, waiting for transfers between devices: 11.4 us -> 7.43 us  [per_device(): lax.all_to_all(jnp.broadcast_to(band[None], (owners, rows, width)), 'wide...]
    psum x1 -> x0, blocking collectives: 3.36 us -> none  [per_device(): band = lax.psum(band, 'narrow')]
  transfers between devices with their start and end apart: 2 -> 4, of which waited for: 2 -> 3; matrix products, arithmetic and copies ran while one was open for 6% -> 9% of each run, Pallas kernels for 0% -> 0%
where the time goes in v15:
time: 268 us
  blocking collectives  123 us (46%)
  waiting for transfers between devices  71.4 us (27%)
  matrix products  20.9 us (8%)
  local copies, waits for them, and re-layouts  14.9 us (6%)
  between operations  14.2 us (5%)
  other arithmetic  13.3 us (5%)
  starting transfers between devices  10.4 us (4%)
    all_to_all x1, blocking collectives, per_device(): received = lax.all_to_all(payload, 'wide', 0, 0, tiled=True)  118 us
    all_gather x1, waiting for transfers between devices, per_device(): gathered_features = lax.all_gather(features, 'wide', axis=0, tiled=True)  62.9 us
    unnamed x17, local copies, waits for them, and re-layouts  14 us
    all_to_all x1, starting transfers between devices, per_device(): lax.all_to_all(jnp.broadcast_to(band[None], (owners, rows, width)), 'wide...  10.3 us
    all_to_all x1, waiting for transfers between devices, per_device(): lax.all_to_all(jnp.broadcast_to(band[None], (owners, rows, width)), 'wide...  7.43 us
    dot_general x1, matrix products, per_device(): jnp.dot(panel, gathered_features, preferred_element_type=jnp.float32)  7.05 us
  transfers between devices with their start and end apart: 4, of which 3 were waited for; matrix products, arithmetic and copies ran while one was open for 9% of the time, Pallas kernels for 0%

profile of v15, /device:TPU:0, one launch (start us, length us, event | category | flops | bytes accessed | tf_op | source)
XLA Modules:
  0.0 268.0 jit_solution(5812290850096293579)
XLA Ops:
  7.2 0.0 copy-start
  7.2 0.0 all-gather.2.cloned.1.call-start
  7.2 0.7 all-gather.2.cloned.1.call-update
  7.9 0.9 compare_convert_fusion.1
  8.8 0.2 copy-done
  9.1 3.7 %bitcast_convert_fusion = (bf16[2,128,64,128]{3,2,1,0:T(8,128)(2,1)S(1)}, f32[2,64,128,128]{3,1,2,0:T(8,128)S(1)}) fusion(bf16[2,48,128,128]{3,2,1,0:T(8,128)(2,1)S(1)} %bitcast.49, s32[2,48]{1,0:T(2,128)} %bitcast.54, bf16[2,48]{1,0:T(2,128)(2,1)S(1)} %compare_convert_fusion.1), kind=kOutput, calls=%fused_computation.4 | convolution fusion | flops 203436032 | bytes 15729216 | tf_op jit(solution)/shard_map/skj,sktc->stjc/dot_general | solution.py:21
  12.8 0.0 copy-start.6
  12.8 10.1 %copy.17 = bf16[32,8,64,128]{3,1,2,0:T(8,128)(2,1)} copy(bf16[32,8,64,128]{3,2,1,0:T(8,128)(2,1)S(1)} %bitcast.53) | data formatting | bytes 8388608
  22.9 1.1 bitcast_reduce_fusion
  24.0 2.6 psum.7
  26.7 0.1 broadcast_bitcast_fusion
  26.7 0.0 copy-done.6
  26.7 1.3 fusion.3
  28.0 0.9 bitcast_multiply_fusion
  28.9 0.0 copy-start.7
  28.9 62.9 %all-gather.2.cloned.1.call-done = bf16[8192,512]{1,0:T(8,128)(2,1)} async-done(((bf16[128,512]{1,0:T(8,128)(2,1)}), bf16[8192,512]{1,0:T(8,128)(2,1)}) %all-gather.2.cloned.1.call-update) | async-done | bytes 8388624 | tf_op jit(solution)/shard_map/all_gather | solution.py:16
  91.8 0.0 copy-start.2
  91.8 0.0 copy-start.5
  91.8 7.0 %fusion.18 = f32[256,512]{1,0:T(8,128)S(1)} fusion(bf16[256,8192]{1,0:T(8,128)(2,1)} %bitcast.51, bf16[8192,512]{1,0:T(8,128)(2,1)} %all-gather.2.cloned.1.call-done), kind=kOutput, calls=%fused_computation.40 | convolution fusion | flops 2147483648 | bytes 13107200 | tf_op jit(solution)/shard_map/dot_general | solution.py:30
  98.8 0.0 copy-done.2
  98.8 0.0 copy-done.5
  98.8 0.0 copy-start.4
  98.9 1.4 convolution_add_fusion
  100.2 0.0 copy-done.4
  100.2 0.0 collective-permute-start
  100.2 0.0 copy-done.7
  100.3 2.3 all_gather.7
  102.6 0.0 collective-permute-done
  102.6 1.5 multiply_convert_fusion
  104.1 1.7 fusion.19
  105.7 4.6 %convolution_convert_fusion = bf16[8192,512]{1,0:T(8,128)(2,1)S(1)} fusion(bf16[256,8192]{1,0:T(8,128)(2,1)} %bitcast.52, bf16[256,512]{1,0:T(8,128)(2,1)S(1)} %get-tuple-element.7), kind=kOutput, calls=%fused_computation.1 | convolution fusion | flops 2151677952 | bytes 12845056 | tf_op jit(solution)/shard_map/dot_general | solution.py:49
  110.3 0.3 convert_bitcast_fusion
  110.7 1.0 pad_maximum_fusion
  111.7 117.9 %all_to_all.10 = bf16[64,144,512]{2,1,0:T(8,128)(2,1)S(1)} all-to-all(bf16[64,144,512]{2,1,0:T(8,128)(2,1)S(1)} %pad_maximum_fusion), channel_id=1, replica_groups=mesh['wide'=64,'narrow'=2] {'wide'}, dimensions={0} | all-to-all | bytes 18874368 | tf_op jit(solution)/shard_map/all_to_all | solution.py:69
  229.6 0.0 copy-start.1
  229.6 3.6 %copy-done.1 = bf16[64,144,512]{2,1,0:T(8,128)(2,1)} copy-done((bf16[64,144,512]{2,1,0:T(8,128)(2,1)}, bf16[64,144,512]{2,1,0:T(8,128)(2,1)S(1)}, u32[]{:S(2)}) %copy-start.1) | copy-done | bytes 9437208
  233.2 0.2 add_reduce_fusion
  233.4 0.1 collective-permute-start.1
  233.5 0.7 multiply_convert_fusion.1
  234.2 0.4 collective-permute-done.1
  234.6 0.8 broadcast_in_dim.2
  235.5 10.3 %all-to-all-start.1 = ((bf16[64,8,512]{2,1,0:T(8,128)(2,1)}), bf16[64,8,512]{2,1,0:T(8,128)(2,1)}, u32[]{:S(2)}, u32[]{:S(2)}) async-start(bf16[64,8,512]{2,1,0:T(8,128)(2,1)} %broadcast_in_dim.2), calls=%async_computation.1 | async-start | bytes 1048576 | tf_op jit(solution)/shard_map/all_to_all | solution.py:78
  245.7 0.0 copy-start.3
  245.7 4.8 %convert_reduce_fusion = f32[128,512]{1,0:T(8,128)S(1)} fusion(bf16[64,144,512]{2,1,0:T(8,128)(2,1)} %copy-done.1), kind=kLoop, calls=%fused_computation | loop fusion | flops 8323072 | bytes 8650752 | tf_op jit(solution)/shard_map/reduce_sum | solution.py:81
  250.6 0.0 copy-done.3
  250.6 1.0 convolution_convert_fusion.1
  251.6 7.4 %all-to-all-done.1 = bf16[64,8,512]{2,1,0:T(8,128)(2,1)} async-done(((bf16[64,8,512]{2,1,0:T(8,128)(2,1)}), bf16[64,8,512]{2,1,0:T(8,128)(2,1)}, u32[]{:S(2)}, u32[]{:S(2)}) %all-to-all-start.1) | async-done | bytes 524320 | tf_op jit(solution)/shard_map/all_to_all | solution.py:78
  259.0 2.1 bitcast_convert_fusion.1
  (3 shorter events, 0.0 us)
Async XLA Ops:
  7.2 1.9 copy-start
  7.2 84.6 %all-gather.2.cloned.1.call-start = ((), (), s32[]{:S(2)}) async-start(), calls=%async_computation.2 | async-start | bytes 8519680 | tf_op jit(solution)/shard_map/all_gather | solution.py:16
  12.8 14.0 %copy-start.6 = (bf16[128,512]{1,0:T(8,128)(2,1)S(1)}, bf16[128,512]{1,0:T(8,128)(2,1)}, u32[]{:S(2)}) copy-start(bf16[128,512]{1,0:T(8,128)(2,1)} %param.6) | copy-start | bytes 393220
  28.9 71.3 %copy-start.7 = (bf16[128,512]{1,0:T(8,128)(2,1)S(1)}, bf16[128,512]{1,0:T(8,128)(2,1)}, u32[]{:S(2)}) copy-start(bf16[128,512]{1,0:T(8,128)(2,1)} %param.11) | copy-start | bytes 393220
  91.8 7.1 %copy-start.2 = (bf16[512,512]{1,0:T(8,128)(2,1)S(1)}, bf16[512,512]{1,0:T(8,128)(2,1)}, u32[]{:S(2)}) copy-start(bf16[512,512]{1,0:T(8,128)(2,1)} %param.7) | copy-start | bytes 1572868
  91.8 7.1 %copy-start.5 = (f32[256,512]{1,0:T(8,128)S(1)}, f32[256,512]{1,0:T(8,128)}, u32[]{:S(2)}) copy-start(f32[256,512]{1,0:T(8,128)} %bitcast_multiply_fusion) | copy-start | bytes 1572868
  98.8 1.4 copy-start.4
  100.2 2.3 collective-permute-start
  229.6 3.6 %copy-start.1 = (bf16[64,144,512]{2,1,0:T(8,128)(2,1)}, bf16[64,144,512]{2,1,0:T(8,128)(2,1)S(1)}, u32[]{:S(2)}) copy-start(bf16[64,144,512]{2,1,0:T(8,128)(2,1)S(1)} %all_to_all.10) | copy-start | bytes 28311556
  233.4 1.3 collective-permute-start.1
  235.5 23.5 %all-to-all-start.1 = ((bf16[64,8,512]{2,1,0:T(8,128)(2,1)}), bf16[64,8,512]{2,1,0:T(8,128)(2,1)}, u32[]{:S(2)}, u32[]{:S(2)}) async-start(bf16[64,8,512]{2,1,0:T(8,128)(2,1)} %broadcast_in_dim.2), calls=%async_computation.1 | async-start | bytes 1048576 | tf_op jit(solution)/shard_map/all_to_all | solution.py:78
  245.7 4.9 %copy-start.3 = (bf16[512,512]{1,0:T(8,128)(2,1)S(1)}, bf16[512,512]{1,0:T(8,128)(2,1)}, u32[]{:S(2)}) copy-start(bf16[512,512]{1,0:T(8,128)(2,1)} %param.7) | copy-start | bytes 1572868
Sparse Core Ops, SparseCore 0:
  10.9 80.8 all-gather.1

commit v16 on v15

--- a/solution.py
+++ b/solution.py
@@ -24,7 +24,10 @@
     degree = 1.0 + lax.psum(jnp.sum(dense, axis=1), "narrow")
     scale = lax.rsqrt(degree)
     panel = dense.astype(jnp.bfloat16)
-    panel, scale = lax.optimization_barrier((panel, scale))
+    panel_t = jnp.einsum(
+        "skj,sktc->jcst", onehot, tiles, preferred_element_type=jnp.float32
+    ).reshape(owners * tile, copies * tile).astype(jnp.bfloat16)
+    panel, panel_t, scale = lax.optimization_barrier((panel, panel_t, scale))
     projected = jnp.dot(features, weight, preferred_element_type=jnp.float32).astype(jnp.bfloat16)
     own = lax.axis_index("narrow")
     aggregated = jnp.dot(panel, gathered_features, preferred_element_type=jnp.float32)
@@ -46,9 +49,7 @@
     preact = lax.dynamic_slice_in_dim(preact_both, own * tile, tile, 0)
     activated = jax.nn.silu(preact).astype(jnp.bfloat16)
     own_grad = lax.dynamic_slice_in_dim(all_grad, own * tile, tile, 0)
-    terms = lax.dot_general(
-        panel, all_grad, (((0,), (0,)), ((), ())), preferred_element_type=jnp.float32
-    ).astype(jnp.bfloat16)
+    terms = jnp.dot(panel_t, all_grad, preferred_element_type=jnp.float32).astype(jnp.bfloat16)
     weight_terms = lax.dot_general(
         aggregated, all_grad.astype(jnp.float32), (((0,), (0,)), ((), ())),
         precision=lax.Precision.HIGHEST, preferred_element_type=jnp.float32,

time: 268 us -> 266 us (level)
  waiting for transfers between devices: 71.4 us -> 57.6 us
  local copies, waits for them, and re-layouts: 14.9 us -> 26.5 us
    convert_element_type x0 -> x1, local copies, waits for them, and re-layouts: none -> 21.7 us  [per_device(): panel_t = jnp.einsum('skj,sktc->jcst', onehot, tiles, preferred_element_t...]
    all_gather x1, waiting for transfers between devices: 62.9 us -> 49.1 us  [per_device(): gathered_features = lax.all_gather(features, 'wide', axis=0, tiled=True)]
    unnamed x17 -> x14, local copies, waits for them, and re-layouts: 14 us -> 3.88 us
    dot_general x1, matrix products: 3.7 us -> 7.69 us  [per_device(): jnp.einsum('skj,sktc->stjc', onehot, tiles, preferred_element_type=jnp.fl...]
  transfers between devices with their start and end apart: 4 -> 4, of which waited for: 3 -> 3; matrix products, arithmetic and copies ran while one was open for 9% -> 14% of each run, Pallas kernels for 0% -> 0%
where the time goes in v16:
time: 266 us
  blocking collectives  123 us (46%)
  waiting for transfers between devices  57.6 us (22%)
  local copies, waits for them, and re-layouts  26.5 us (10%)
  matrix products  22 us (8%)
  between operations  14.2 us (5%)
  starting transfers between devices  11.3 us (4%)
  other arithmetic  11.3 us (4%)
    all_to_all x1, blocking collectives, per_device(): received = lax.all_to_all(payload, 'wide', 0, 0, tiled=True)  118 us
    all_gather x1, waiting for transfers between devices, per_device(): gathered_features = lax.all_gather(features, 'wide', axis=0, tiled=True)  49.1 us
    convert_element_type x1, local copies, waits for them, and re-layouts, per_device(): panel_t = jnp.einsum('skj,sktc->jcst', onehot, tiles, preferred_element_t...  21.7 us
    all_to_all x1, starting transfers between devices, per_device(): lax.all_to_all(jnp.broadcast_to(band[None], (owners, rows, width)), 'wide...  11.1 us
    dot_general x1, matrix products, per_device(): jnp.einsum('skj,sktc->stjc', onehot, tiles, preferred_element_type=jnp.fl...  7.69 us
    all_to_all x1, waiting for transfers between devices, per_device(): lax.all_to_all(jnp.broadcast_to(band[None], (owners, rows, width)), 'wide...  7.43 us
    dot_general x1, matrix products, per_device(): jnp.dot(panel, gathered_features, preferred_element_type=jnp.float32)  6.97 us
  transfers between devices with their start and end apart: 4, of which 3 were waited for; matrix products, arithmetic and copies ran while one was open for 14% of the time, Pallas kernels for 0%

profile of v16, /device:TPU:0, one launch (start us, length us, event | category | flops | bytes accessed | tf_op | source)
XLA Modules:
  0.0 265.8 jit_solution(16875776601040912449)
XLA Ops:
  7.2 0.0 copy-start
  7.2 0.0 all-gather.2.cloned.1.call-start
  7.2 0.7 all-gather.2.cloned.1.call-update
  7.9 0.9 compare_convert_fusion.1
  8.8 0.2 copy-done
  9.1 7.7 %fusion.16 = (bf16[2,64,128,128]{3,1,2,0:T(8,128)(2,1)}, bf16[2,128,64,128]{3,2,1,0:T(8,128)(2,1)}, f32[2,64,128,128]{3,1,2,0:T(8,128)S(1)}) fusion(bf16[2,48,128,128]{3,2,1,0:T(8,128)(2,1)S(1)} %bitcast.55, s32[2,48]{1,0:T(2,128)} %bitcast.60, bf16[2,48]{1,0:T(2,128)(2,1)S(1)} %compare_convert_fusion.1), kind=kOutput, calls=%fused_computation.41 | convolution fusion | flops 205533184 | bytes 19923520 | tf_op jit(solution)/shard_map/skj,sktc->stjc/dot_general | solution.py:21
  16.7 1.1 bitcast_reduce_fusion
  17.8 2.6 psum.7
  20.5 0.0 copy-start.3
  20.5 0.0 copy-start.5
  20.5 21.7 %copy_bitcast_fusion = (bf16[8192,256]{0,1:T(8,128)(2,1)}, bf16[256,8192]{1,0:T(8,128)(2,1)}) fusion(bf16[32,8,64,128]{3,2,1,0:T(8,128)(2,1)} %bitcast.57, bf16[32,8,64,128]{3,2,1,0:T(8,128)(2,1)} %bitcast.58), kind=kLoop, calls=%fused_computation.5 | loop fusion | bytes 16777216 | tf_op jit(solution)/shard_map/convert_element_type | solution.py:29
  42.2 0.1 broadcast_bitcast_fusion
  42.3 0.0 copy-done.3
  42.3 0.0 copy-done.5
  42.3 0.2 fusion.3
  42.6 0.1 bitcast_multiply_fusion
  42.7 0.0 copy-start.6
  42.7 49.1 %all-gather.2.cloned.1.call-done = bf16[8192,512]{1,0:T(8,128)(2,1)} async-done(((bf16[128,512]{1,0:T(8,128)(2,1)}), bf16[8192,512]{1,0:T(8,128)(2,1)}) %all-gather.2.cloned.1.call-update) | async-done | bytes 8388624 | tf_op jit(solution)/shard_map/all_gather | solution.py:16
  91.8 7.0 %fusion.19 = f32[256,512]{1,0:T(8,128)S(1)} fusion(bf16[256,8192]{1,0:T(8,128)(2,1)} %get-tuple-element.6, bf16[8192,512]{1,0:T(8,128)(2,1)} %all-gather.2.cloned.1.call-done), kind=kOutput, calls=%fused_computation.42 | convolution fusion | flops 2147483648 | bytes 13107200 | tf_op jit(solution)/shard_map/dot_general | solution.py:33
  98.8 0.6 convolution_add_fusion
  99.3 0.1 collective-permute-start
  99.4 0.0 copy-done.6
  99.5 2.3 all_gather.7
  101.8 0.0 collective-permute-done
  101.8 0.3 multiply_convert_fusion
  102.1 0.6 fusion.20
  102.7 4.6 %convolution_convert_fusion = bf16[8192,512]{1,0:T(8,128)(2,1)S(1)} fusion(bf16[8192,256]{0,1:T(8,128)(2,1)} %get-tuple-element.8, bf16[256,512]{1,0:T(8,128)(2,1)S(1)} %get-tuple-element.9), kind=kOutput, calls=%fused_computation.1 | convolution fusion | flops 2151677952 | bytes 12845056 | tf_op jit(solution)/shard_map/dot_general | solution.py:52
  107.3 0.3 convert_bitcast_fusion
  107.7 0.9 pad_maximum_fusion
  108.6 0.0 copy-start.1
  108.6 118.0 %all_to_all.10 = bf16[64,144,512]{2,1,0:T(8,128)(2,1)S(1)} all-to-all(bf16[64,144,512]{2,1,0:T(8,128)(2,1)S(1)} %pad_maximum_fusion), channel_id=1, replica_groups=mesh['wide'=64,'narrow'=2] {'wide'}, dimensions={0} | all-to-all | bytes 18874368 | tf_op jit(solution)/shard_map/all_to_all | solution.py:70
  226.6 0.0 copy-start.2
  226.6 3.6 %copy-done.2 = bf16[64,144,512]{2,1,0:T(8,128)(2,1)} copy-done((bf16[64,144,512]{2,1,0:T(8,128)(2,1)}, bf16[64,144,512]{2,1,0:T(8,128)(2,1)S(1)}, u32[]{:S(2)}) %copy-start.2) | copy-done | bytes 9437208
  230.2 0.2 add_reduce_fusion
  230.4 0.1 collective-permute-start.1
  230.5 0.7 multiply_convert_fusion.1
  231.2 0.4 collective-permute-done.1
  231.6 0.8 broadcast_in_dim.2
  232.5 11.1 %all-to-all-start.1 = ((bf16[64,8,512]{2,1,0:T(8,128)(2,1)}), bf16[64,8,512]{2,1,0:T(8,128)(2,1)}, u32[]{:S(2)}, u32[]{:S(2)}) async-start(bf16[64,8,512]{2,1,0:T(8,128)(2,1)} %broadcast_in_dim.2), calls=%async_computation.1 | async-start | bytes 1048576 | tf_op jit(solution)/shard_map/all_to_all | solution.py:79
  243.6 0.0 copy-start.4
  243.6 4.8 %convert_reduce_fusion = f32[128,512]{1,0:T(8,128)S(1)} fusion(bf16[64,144,512]{2,1,0:T(8,128)(2,1)} %copy-done.2), kind=kLoop, calls=%fused_computation | loop fusion | flops 8323072 | bytes 8650752 | tf_op jit(solution)/shard_map/reduce_sum | solution.py:82
  248.4 0.0 copy-done.4
  248.4 1.0 convolution_convert_fusion.1
  249.4 7.4 %all-to-all-done.1 = bf16[64,8,512]{2,1,0:T(8,128)(2,1)} async-done(((bf16[64,8,512]{2,1,0:T(8,128)(2,1)}), bf16[64,8,512]{2,1,0:T(8,128)(2,1)}, u32[]{:S(2)}, u32[]{:S(2)}) %all-to-all-start.1) | async-done | bytes 524320 | tf_op jit(solution)/shard_map/all_to_all | solution.py:79
  256.8 2.1 bitcast_convert_fusion.1
  259.0 0.0 copy-done.1
  (3 shorter events, 0.0 us)
Async XLA Ops:
  7.2 1.9 copy-start
  7.2 84.6 %all-gather.2.cloned.1.call-start = ((), (), s32[]{:S(2)}) async-start(), calls=%async_computation.2 | async-start | bytes 8519680 | tf_op jit(solution)/shard_map/all_gather | solution.py:16
  20.5 21.8 %copy-start.3 = (bf16[512,512]{1,0:T(8,128)(2,1)S(1)}, bf16[512,512]{1,0:T(8,128)(2,1)}, u32[]{:S(2)}) copy-start(bf16[512,512]{1,0:T(8,128)(2,1)} %param.7) | copy-start | bytes 1572868
  20.5 21.8 %copy-start.5 = (bf16[128,512]{1,0:T(8,128)(2,1)S(1)}, bf16[128,512]{1,0:T(8,128)(2,1)}, u32[]{:S(2)}) copy-start(bf16[128,512]{1,0:T(8,128)(2,1)} %param.6) | copy-start | bytes 393220
  42.7 56.8 %copy-start.6 = (bf16[128,512]{1,0:T(8,128)(2,1)S(1)}, bf16[128,512]{1,0:T(8,128)(2,1)}, u32[]{:S(2)}) copy-start(bf16[128,512]{1,0:T(8,128)(2,1)} %param.11) | copy-start | bytes 393220
  99.3 2.4 collective-permute-start
  108.6 150.4 %copy-start.1 = (bf16[2,1,48,128,128]{4,3,2,1,0:T(8,128)(2,1)S(1)}, bf16[2,1,48,128,128]{4,3,2,1,0:T(8,128)(2,1)}, u32[]{:S(2)}) copy-start(bf16[2,1,48,128,128]{4,3,2,1,0:T(8,128)(2,1)} %param.10) | copy-start | bytes 9437188
  226.6 3.6 %copy-start.2 = (bf16[64,144,512]{2,1,0:T(8,128)(2,1)}, bf16[64,144,512]{2,1,0:T(8,128)(2,1)S(1)}, u32[]{:S(2)}) copy-start(bf16[64,144,512]{2,1,0:T(8,128)(2,1)S(1)} %all_to_all.10) | copy-start | bytes 28311556
  230.4 1.3 collective-permute-start.1
  232.5 24.4 %all-to-all-start.1 = ((bf16[64,8,512]{2,1,0:T(8,128)(2,1)}), bf16[64,8,512]{2,1,0:T(8,128)(2,1)}, u32[]{:S(2)}, u32[]{:S(2)}) async-start(bf16[64,8,512]{2,1,0:T(8,128)(2,1)} %broadcast_in_dim.2), calls=%async_computation.1 | async-start | bytes 1048576 | tf_op jit(solution)/shard_map/all_to_all | solution.py:79
  243.6 4.9 %copy-start.4 = (bf16[512,512]{1,0:T(8,128)(2,1)S(1)}, bf16[512,512]{1,0:T(8,128)(2,1)}, u32[]{:S(2)}) copy-start(bf16[512,512]{1,0:T(8,128)(2,1)} %param.7) | copy-start | bytes 1572868
Sparse Core Ops, SparseCore 0:
  10.9 80.8 all-gather.1

commit v17 on v16

--- a/solution.py
+++ b/solution.py
@@ -27,7 +27,8 @@
     panel_t = jnp.einsum(
         "skj,sktc->jcst", onehot, tiles, preferred_element_type=jnp.float32
     ).reshape(owners * tile, copies * tile).astype(jnp.bfloat16)
-    panel, panel_t, scale = lax.optimization_barrier((panel, panel_t, scale))
+    cot_both = lax.all_gather(cotangent, "narrow", axis=0, tiled=True)
+    panel, panel_t, scale, cot_both = lax.optimization_barrier((panel, panel_t, scale, cot_both))
     projected = jnp.dot(features, weight, preferred_element_type=jnp.float32).astype(jnp.bfloat16)
     own = lax.axis_index("narrow")
     aggregated = jnp.dot(panel, gathered_features, preferred_element_type=jnp.float32)
@@ -42,7 +43,7 @@
     theirs = lax.ppermute(partial_sum, "narrow", [(i, pair - 1 - i) for i in range(pair)])
     preact_both = (partial_sum + theirs) * scale[:, None]
     sig = jax.nn.sigmoid(preact_both)
-    cot_both = lax.all_gather(cotangent, "narrow", axis=0, tiled=True).astype(jnp.float32)
+    cot_both = cot_both.astype(jnp.float32)
     all_grad = (
         cot_both * sig * (1.0 + preact_both * (1.0 - sig)) * scale[:, None]
     ).astype(jnp.bfloat16)

time: 266 us -> 264 us (level)
  transfers between devices with their start and end apart: 4 -> 4, of which waited for: 3 -> 4; matrix products, arithmetic and copies ran while one was open for 14% -> 15% of each run, Pallas kernels for 0% -> 0%
where the time goes in v17:
time: 264 us
  blocking collectives  123 us (47%)
  waiting for transfers between devices  57.4 us (22%)
  local copies, waits for them, and re-layouts  26.7 us (10%)
  matrix products  22 us (8%)
  between operations  14.2 us (5%)
  other arithmetic  11.2 us (4%)
  starting transfers between devices  9.54 us (4%)
    all_to_all x1, blocking collectives, per_device(): received = lax.all_to_all(payload, 'wide', 0, 0, tiled=True)  118 us
    all_gather x1, waiting for transfers between devices, per_device(): gathered_features = lax.all_gather(features, 'wide', axis=0, tiled=True)  47 us
    convert_element_type x1, local copies, waits for them, and re-layouts, per_device(): panel_t = jnp.einsum('skj,sktc->jcst', onehot, tiles, preferred_element_t...  21.9 us
    all_to_all x1, starting transfers between devices, per_device(): lax.all_to_all(jnp.broadcast_to(band[None], (owners, rows, width)), 'wide...  9.11 us
    dot_general x1, matrix products, per_device(): jnp.einsum('skj,sktc->stjc', onehot, tiles, preferred_element_type=jnp.fl...  7.69 us
    all_to_all x1, waiting for transfers between devices, per_device(): lax.all_to_all(jnp.broadcast_to(band[None], (owners, rows, width)), 'wide...  7.43 us
    dot_general x1, matrix products, per_device(): jnp.dot(panel, gathered_features, preferred_element_type=jnp.float32)  6.97 us
  transfers between devices with their start and end apart: 4, of which 4 were waited for; matrix products, arithmetic and copies ran while one was open for 15% of the time, Pallas kernels for 0%

profile of v17, /device:TPU:0, one launch (start us, length us, event | category | flops | bytes accessed | tf_op | source)
XLA Modules:
  0.0 263.9 jit_solution(4746101957128973760)
XLA Ops:
  7.2 0.0 copy-start
  7.2 0.0 all-gather.2.cloned.1.call-start
  7.2 0.7 all-gather.2.cloned.1.call-update
  7.9 0.9 compare_convert_fusion.1
  8.8 0.2 copy-done
  9.1 7.7 %fusion.16 = (bf16[2,64,128,128]{3,1,2,0:T(8,128)(2,1)}, bf16[2,128,64,128]{3,2,1,0:T(8,128)(2,1)}, f32[2,64,128,128]{3,1,2,0:T(8,128)S(1)}) fusion(bf16[2,48,128,128]{3,2,1,0:T(8,128)(2,1)S(1)} %bitcast.55, s32[2,48]{1,0:T(2,128)} %bitcast.60, bf16[2,48]{1,0:T(2,128)(2,1)S(1)} %compare_convert_fusion.1), kind=kOutput, calls=%fused_computation.41 | convolution fusion | flops 205533184 | bytes 19923520 | tf_op jit(solution)/shard_map/skj,sktc->stjc/dot_general | solution.py:21
  16.7 0.0 copy-start.6
  16.8 1.1 bitcast_reduce_fusion
  17.8 2.5 psum.7
  20.3 0.0 copy-done.6
  20.3 2.2 all_gather.6
  22.5 0.0 copy-start.3
  22.5 0.0 copy-start.5
  22.5 21.9 %copy_bitcast_fusion = (bf16[8192,256]{0,1:T(8,128)(2,1)}, bf16[256,8192]{1,0:T(8,128)(2,1)}) fusion(bf16[32,8,64,128]{3,2,1,0:T(8,128)(2,1)} %bitcast.57, bf16[32,8,64,128]{3,2,1,0:T(8,128)(2,1)} %bitcast.58), kind=kLoop, calls=%fused_computation.5 | loop fusion | bytes 16777216 | tf_op jit(solution)/shard_map/convert_element_type | solution.py:29
  44.4 0.1 broadcast_bitcast_fusion
  44.4 0.0 copy-done.3
  44.4 0.0 copy-done.5
  44.5 0.2 fusion.3
  44.7 0.1 bitcast_multiply_fusion
  44.8 47.0 %all-gather.2.cloned.1.call-done = bf16[8192,512]{1,0:T(8,128)(2,1)} async-done(((bf16[128,512]{1,0:T(8,128)(2,1)}), bf16[8192,512]{1,0:T(8,128)(2,1)}) %all-gather.2.cloned.1.call-update) | async-done | bytes 8388624 | tf_op jit(solution)/shard_map/all_gather | solution.py:16
  91.8 7.0 %fusion.19 = f32[256,512]{1,0:T(8,128)S(1)} fusion(bf16[256,8192]{1,0:T(8,128)(2,1)} %get-tuple-element.7, bf16[8192,512]{1,0:T(8,128)(2,1)} %all-gather.2.cloned.1.call-done), kind=kOutput, calls=%fused_computation.42 | convolution fusion | flops 2147483648 | bytes 13107200 | tf_op jit(solution)/shard_map/dot_general | solution.py:34
  98.8 0.6 convolution_add_fusion
  99.3 0.3 collective-permute-start
  99.7 1.9 collective-permute-done
  101.6 0.3 multiply_convert_fusion
  101.9 0.6 fusion.20
  102.5 4.6 %convolution_convert_fusion = bf16[8192,512]{1,0:T(8,128)(2,1)S(1)} fusion(bf16[8192,256]{0,1:T(8,128)(2,1)} %get-tuple-element.9, bf16[256,512]{1,0:T(8,128)(2,1)S(1)} %get-tuple-element.11), kind=kOutput, calls=%fused_computation.1 | convolution fusion | flops 2151677952 | bytes 12845056 | tf_op jit(solution)/shard_map/dot_general | solution.py:53
  107.1 0.3 convert_bitcast_fusion
  107.4 0.9 pad_maximum_fusion
  108.4 0.0 copy-start.1
  108.4 118.2 %all_to_all.10 = bf16[64,144,512]{2,1,0:T(8,128)(2,1)S(1)} all-to-all(bf16[64,144,512]{2,1,0:T(8,128)(2,1)S(1)} %pad_maximum_fusion), channel_id=1, replica_groups=mesh['wide'=64,'narrow'=2] {'wide'}, dimensions={0} | all-to-all | bytes 18874368 | tf_op jit(solution)/shard_map/all_to_all | solution.py:71
  226.6 0.0 copy-start.2
  226.6 3.6 %copy-done.2 = bf16[64,144,512]{2,1,0:T(8,128)(2,1)} copy-done((bf16[64,144,512]{2,1,0:T(8,128)(2,1)}, bf16[64,144,512]{2,1,0:T(8,128)(2,1)S(1)}, u32[]{:S(2)}) %copy-start.2) | copy-done | bytes 9437208
  230.2 0.2 add_reduce_fusion
  230.4 0.1 collective-permute-start.1
  230.5 0.7 multiply_convert_fusion.1
  231.2 0.4 collective-permute-done.1
  231.6 0.8 broadcast_in_dim.2
  232.5 9.1 %all-to-all-start.1 = ((bf16[64,8,512]{2,1,0:T(8,128)(2,1)}), bf16[64,8,512]{2,1,0:T(8,128)(2,1)}, u32[]{:S(2)}, u32[]{:S(2)}) async-start(bf16[64,8,512]{2,1,0:T(8,128)(2,1)} %broadcast_in_dim.2), calls=%async_computation.1 | async-start | bytes 1048576 | tf_op jit(solution)/shard_map/all_to_all | solution.py:80
  241.6 0.0 copy-start.4
  241.6 4.8 %convert_reduce_fusion = f32[128,512]{1,0:T(8,128)S(1)} fusion(bf16[64,144,512]{2,1,0:T(8,128)(2,1)} %copy-done.2), kind=kLoop, calls=%fused_computation | loop fusion | flops 8323072 | bytes 8650752 | tf_op jit(solution)/shard_map/reduce_sum | solution.py:83
  246.4 0.0 copy-done.4
  246.5 1.0 convolution_convert_fusion.1
  247.4 7.4 %all-to-all-done.1 = bf16[64,8,512]{2,1,0:T(8,128)(2,1)} async-done(((bf16[64,8,512]{2,1,0:T(8,128)(2,1)}), bf16[64,8,512]{2,1,0:T(8,128)(2,1)}, u32[]{:S(2)}, u32[]{:S(2)}) %all-to-all-start.1) | async-done | bytes 524320 | tf_op jit(solution)/shard_map/all_to_all | solution.py:80
  254.9 2.1 bitcast_convert_fusion.1
  257.0 0.0 copy-done.1
  (3 shorter events, 0.0 us)
Async XLA Ops:
  7.2 1.9 copy-start
  7.2 84.6 %all-gather.2.cloned.1.call-start = ((), (), s32[]{:S(2)}) async-start(), calls=%async_computation.2 | async-start | bytes 8519680 | tf_op jit(solution)/shard_map/all_gather | solution.py:16
  16.7 3.6 %copy-start.6 = (bf16[128,512]{1,0:T(8,128)(2,1)S(1)}, bf16[128,512]{1,0:T(8,128)(2,1)}, u32[]{:S(2)}) copy-start(bf16[128,512]{1,0:T(8,128)(2,1)} %param.11) | copy-start | bytes 393220
  22.5 22.0 %copy-start.3 = (bf16[512,512]{1,0:T(8,128)(2,1)S(1)}, bf16[512,512]{1,0:T(8,128)(2,1)}, u32[]{:S(2)}) copy-start(bf16[512,512]{1,0:T(8,128)(2,1)} %param.7) | copy-start | bytes 1572868
  22.5 22.0 %copy-start.5 = (bf16[128,512]{1,0:T(8,128)(2,1)S(1)}, bf16[128,512]{1,0:T(8,128)(2,1)}, u32[]{:S(2)}) copy-start(bf16[128,512]{1,0:T(8,128)(2,1)} %param.6) | copy-start | bytes 393220
  99.3 2.2 collective-permute-start
  108.4 148.7 %copy-start.1 = (bf16[2,1,48,128,128]{4,3,2,1,0:T(8,128)(2,1)S(1)}, bf16[2,1,48,128,128]{4,3,2,1,0:T(8,128)(2,1)}, u32[]{:S(2)}) copy-start(bf16[2,1,48,128,128]{4,3,2,1,0:T(8,128)(2,1)} %param.10) | copy-start | bytes 9437188
  226.6 3.6 %copy-start.2 = (bf16[64,144,512]{2,1,0:T(8,128)(2,1)}, bf16[64,144,512]{2,1,0:T(8,128)(2,1)S(1)}, u32[]{:S(2)}) copy-start(bf16[64,144,512]{2,1,0:T(8,128)(2,1)S(1)} %all_to_all.10) | copy-start | bytes 28311556
  230.4 1.3 collective-permute-start.1
  232.5 22.4 %all-to-all-start.1 = ((bf16[64,8,512]{2,1,0:T(8,128)(2,1)}), bf16[64,8,512]{2,1,0:T(8,128)(2,1)}, u32[]{:S(2)}, u32[]{:S(2)}) async-start(bf16[64,8,512]{2,1,0:T(8,128)(2,1)} %broadcast_in_dim.2), calls=%async_computation.1 | async-start | bytes 1048576 | tf_op jit(solution)/shard_map/all_to_all | solution.py:80
  241.6 4.9 %copy-start.4 = (bf16[512,512]{1,0:T(8,128)(2,1)S(1)}, bf16[512,512]{1,0:T(8,128)(2,1)}, u32[]{:S(2)}) copy-start(bf16[512,512]{1,0:T(8,128)(2,1)} %param.7) | copy-start | bytes 1572868
Sparse Core Ops, SparseCore 0:
  10.9 80.8 all-gather.1
